TPU v7x, 512 devices: a whole 4x4x16 slice. The times are simulated.
512 devices in a mesh: tm: 32 (over z, x_lo), recv: 16 (over x_hi, y, core).
Axes of the slice: x: 4 (x_hi: 2, x_lo: 2; x = x_hi * 2 + x_lo), y: 4, z: 16, core: 2. Of those that a mesh axis runs over, the one named last changes fastest.
Arguments:
- traces: bfloat16 [128, 4096, 2048], P('tm', 'recv'), may hold values from -6 to 6
- valid: int32 [128, 4096], P('tm', 'recv'), may hold values 0 or 1
- src_idx: int32 [32], replicated, may hold values from 0 to 4095
Outputs:
- stacks: float32 [32, 2, 61, 4096], P('tm', None, None, 'recv')
All inputs are finite; a program needn't handle non-finite values. No bound on the sum of `valid` on one device may be relied on, other than what follows from the above.
Results may differ from a plain program's by a relative error of at most 0.0035.
Values sent between devices are 32-bit elements; how exact they have to be, the bound alone decides.
No kernel may reach another device: no remote copies, remote signals or barrier semaphores. Data moves between devices by JAX's collectives and lax.ppermute only.
A program may use at most 64 MiB of HBM per device.

v0:
```python
import math

import jax
import jax.numpy as jnp
from jax import lax
from jax.sharding import PartitionSpec as P

NS = 2048
NB = 61
BIN0 = 40


def basis_table():
    sample_ids = jnp.arange(NS, dtype=jnp.int32)
    bin_ids = BIN0 + jnp.arange(NB, dtype=jnp.int32)
    phase_ids = bin_ids[:, None] * sample_ids[None, :] % NS
    angle = 2.0 * math.pi / NS * phase_ids.astype(jnp.float32)
    return jnp.concatenate([jnp.cos(angle), -jnp.sin(angle)], axis=0).astype(jnp.bfloat16)


def whiten_block(spec, valid_float):
    real_part = spec[:NB]
    imag_part = spec[NB:]
    power = real_part * real_part + imag_part * imag_part
    level = jnp.sum(power, axis=0) / (2.0 * NB)
    scale = lax.rsqrt(power + level[None] + 1e-06) * valid_float[None]
    return jnp.concatenate([real_part * scale, imag_part * scale], axis=0)


def share_panel(partial_value):
    return lax.psum(partial_value, "recv")


def cross_terms(panel, white, factor):
    high = lax.Precision.HIGHEST
    src_real = panel[:NB]
    src_imag = panel[NB:]
    own_real = white[:NB]
    own_imag = white[NB:]
    real_sum = jnp.einsum("fts,ftc->sfc", src_real, own_real, precision=high) + jnp.einsum(
        "fts,ftc->sfc", src_imag, own_imag, precision=high
    )
    imag_sum = jnp.einsum("fts,ftc->sfc", src_real, own_imag, precision=high) - jnp.einsum(
        "fts,ftc->sfc", src_imag, own_real, precision=high
    )
    return jnp.stack([real_sum, imag_sum], axis=1) * factor


def on_device(traces, valid, src_idx):
    seg_count = traces.shape[0]
    chan_count = traces.shape[1]
    basis = basis_table()
    valid_float = valid.astype(jnp.float32)
    offset = lax.axis_index("recv") * chan_count
    onehot = (src_idx[:, None] == offset + jnp.arange(chan_count, dtype=jnp.int32)[None, :]).astype(
        jnp.float32
    )
    spec = lax.dot_general(
        basis, traces, (((1,), (2,)), ((), ())), preferred_element_type=jnp.float32
    )
    white = whiten_block(spec, valid_float)
    partial_value = jnp.einsum("ktc,sc->kts", white, onehot, precision=lax.Precision.HIGHEST)
    panel = share_panel(partial_value)
    factor = 1.0 / math.sqrt(seg_count * lax.axis_size("tm"))
    totals = cross_terms(panel, white, factor)
    return lax.psum_scatter(totals, "tm", scatter_dimension=0, tiled=True)


def solution(mesh):
    return jax.shard_map(
        on_device,
        mesh=mesh,
        in_specs=(P("tm", "recv", None), P("tm", "recv"), P()),
        out_specs=P("tm", None, None, "recv"),
        check_vma=False,
    )
```

profile of v0, /device:TPU:2, one launch (start us, length us, event | category | flops | bytes accessed | tf_op | source)
XLA Modules:
  0.0 392.3 jit_solution(107525465795028076)
XLA Ops:
  6.5 0.0 all-reduce.3.cloned.1.call-start
  6.5 2.4 cosine_convert_fusion
  9.0 0.0 copy-start
  9.0 0.0 copy-start.1
  9.0 3.7 fusion.3
  12.7 0.1 fusion.25
  12.8 0.0 copy-done
  12.9 0.1 slice_multiply_fusion.1
  13.0 0.0 copy-done.1
  13.0 0.4 fusion.6
  13.4 68.9 %psum.7 = f32[122,4,32]{0,2,1:T(8,128)S(1)} all-reduce(f32[122,4,32]{0,2,1:T(8,128)S(1)} %fusion.6), channel_id=1, replica_groups=mesh['tm'=32,'recv'=16] {'recv'}, use_global_device_ids=true, to_apply=%region_1.2 | all-reduce | flops 15616 | bytes 124928 | tf_op jit(solution)/shard_map/psum | solution.py:31
  82.3 0.1 fusion.26
  82.4 0.1 copy.14
  82.5 3.1 fusion.17
  85.6 1.8 fusion.13
  87.4 0.1 copy.16
  87.5 3.3 add_bitcast_fusion
  90.8 1.8 subtract_bitcast_fusion
  92.6 0.5 maximum_multiply_fusion
  93.1 5.0 %copy.21 = f32[32,2,61,256]{3,1,2,0:T(2,128)} copy(f32[32,2,61,256]{3,0,2,1:T(8,128)S(1)} %maximum_multiply_fusion) | data formatting | bytes 7995392 | tf_op jit(solution)/shard_map/mul | solution.py:46
  98.1 0.0 all-reduce.3.cloned.1.call-update
  98.1 1.2 dynamic-slice
  99.3 284.0 %all-reduce.3.cloned.1.call-done = f32[32,2,61,256]{3,1,2,0:T(2,128)} async-done(((f32[32,2,61,256]{3,1,2,0:T(2,128)}), f32[32,2,61,256]{3,1,2,0:T(2,128)}) %all-reduce.3.cloned.1.call-update) | async-done | bytes 3997712
  383.4 2.1 constant_dynamic-slice_fusion
  (4 shorter events, 0.0 us)
Async XLA Ops:
  6.5 376.8 %all-reduce.3.cloned.1.call-start = ((), (), s32[]{:S(2)}) async-start(), calls=%async_computation | async-start | bytes 7995392
  9.0 3.8 copy-start
  9.0 4.0 %copy-start.1 = (s32[32]{0:T(128)S(1)}, s32[32]{0:T(128)}, u32[]{:S(2)}) copy-start(s32[32]{0:T(128)} %param.5) | copy-start | bytes 388
Sparse Core Ops, SparseCore 0:
  98.2 285.1 all-reduce.2
where the time goes:
time: 393 us; the launch traced here: 392 us
  waiting for transfers between devices  284 us (72%)
  blocking collectives  68.9 us (18%)
  matrix products  14.1 us (4%)
  between operations  13.5 us (3%)
  local copies, waits for them, and re-layouts  8.66 us (2%)
    unnamed x2, waiting for transfers between devices  284 us
    psum x1, blocking collectives, share_panel(): return lax.psum(partial_value, 'recv')  68.9 us
  transfers between devices with their start and end apart: 1, of which 1 were waited for; matrix products, arithmetic and copies ran while one was open for 0% of the time, Pallas kernels for 0%

commit v1 on v0

--- a/solution.py
+++ b/solution.py
@@ -2,12 +2,15 @@
 
 import jax
 import jax.numpy as jnp
+import numpy as np
 from jax import lax
+from jax.sharding import Mesh
 from jax.sharding import PartitionSpec as P
 
 NS = 2048
 NB = 61
 BIN0 = 40
+NB_PAD = 64
 
 
 def basis_table():
@@ -27,16 +30,16 @@
     return jnp.concatenate([real_part * scale, imag_part * scale], axis=0)
 
 
-def share_panel(partial_value):
-    return lax.psum(partial_value, "recv")
+def pad_bins(part):
+    return jnp.pad(part, [(0, NB_PAD - NB)] + [(0, 0)] * (part.ndim - 1))
 
 
 def cross_terms(panel, white, factor):
     high = lax.Precision.HIGHEST
-    src_real = panel[:NB]
-    src_imag = panel[NB:]
-    own_real = white[:NB]
-    own_imag = white[NB:]
+    src_real = pad_bins(panel[:NB])
+    src_imag = pad_bins(panel[NB:])
+    own_real = pad_bins(white[:NB])
+    own_imag = pad_bins(white[NB:])
     real_sum = jnp.einsum("fts,ftc->sfc", src_real, own_real, precision=high) + jnp.einsum(
         "fts,ftc->sfc", src_imag, own_imag, precision=high
     )
@@ -46,9 +49,20 @@
     return jnp.stack([real_sum, imag_sum], axis=1) * factor
 
 
+def psum_recv(value, size):
+    bit = 1
+    while bit < size:
+        pairs = [(i, i ^ bit) for i in range(size)]
+        value = value + lax.ppermute(value, "recv", pairs)
+        bit *= 2
+    return value
+
+
 def on_device(traces, valid, src_idx):
     seg_count = traces.shape[0]
     chan_count = traces.shape[1]
+    pair = lax.axis_size("xlo")
+    total_segs = seg_count * pair * lax.axis_size("z")
     basis = basis_table()
     valid_float = valid.astype(jnp.float32)
     offset = lax.axis_index("recv") * chan_count
@@ -60,17 +74,27 @@
     )
     white = whiten_block(spec, valid_float)
     partial_value = jnp.einsum("ktc,sc->kts", white, onehot, precision=lax.Precision.HIGHEST)
-    panel = share_panel(partial_value)
-    factor = 1.0 / math.sqrt(seg_count * lax.axis_size("tm"))
-    totals = cross_terms(panel, white, factor)
-    return lax.psum_scatter(totals, "tm", scatter_dimension=0, tiled=True)
+    panel = psum_recv(partial_value, lax.axis_size("recv"))
+    white_pair = lax.all_gather(white, "xlo", axis=1, tiled=True)
+    panel_pair = lax.all_gather(panel, "xlo", axis=1, tiled=True)
+    nsrc = panel_pair.shape[2]
+    panel_pair = panel_pair.reshape(panel_pair.shape[0], panel_pair.shape[1], nsrc // pair, pair)
+    panel_own = lax.dynamic_index_in_dim(panel_pair, lax.axis_index("xlo"), axis=3, keepdims=False)
+    factor = 1.0 / math.sqrt(total_segs)
+    totals = cross_terms(panel_own, white_pair, factor)
+    out = lax.psum_scatter(totals, "z", scatter_dimension=0, tiled=True)
+    return out[:, :, :NB, :]
 
 
 def solution(mesh):
+    tm_size = mesh.shape["tm"]
+    recv_size = mesh.shape["recv"]
+    devices = np.asarray(mesh.devices).reshape(tm_size // 2, 2, recv_size)
+    inner = Mesh(devices, ("z", "xlo", "recv"))
     return jax.shard_map(
         on_device,
-        mesh=mesh,
-        in_specs=(P("tm", "recv", None), P("tm", "recv"), P()),
-        out_specs=P("tm", None, None, "recv"),
+        mesh=inner,
+        in_specs=(P(("z", "xlo"), "recv", None), P(("z", "xlo"), "recv"), P()),
+        out_specs=P(("z", "xlo"), None, None, "recv"),
         check_vma=False,
     )

time: 393 us -> 148 us (0.38)
  the two profiles are of different devices: /device:TPU:2 before, /device:TPU:4 now
where the time goes in v1:
time: 148 us
  waiting for transfers between devices  82.4 us (56%)
  blocking collectives  18.2 us (12%)
  starting transfers between devices  15.4 us (10%)
  between operations  13.6 us (9%)
  matrix products  9.34 us (6%)
  local copies, waits for them, and re-layouts  4.88 us (3%)
  other arithmetic  3.74 us (3%)
    reduce_scatter x1, waiting for transfers between devices, on_device(): out = lax.psum_scatter(totals, 'z', scatter_dimension=0, tiled=True)  75.9 us
    ppermute x4, starting transfers between devices, psum_recv(): value = value + lax.ppermute(value, 'recv', pairs)  15.4 us
    all_gather x1, blocking collectives, on_device(): white_pair = lax.all_gather(white, 'xlo', axis=1, tiled=True)  13.2 us
    ppermute x4, waiting for transfers between devices, psum_recv(): value = value + lax.ppermute(value, 'recv', pairs)  6.43 us
    all_gather x1, blocking collectives, on_device(): panel_pair = lax.all_gather(panel, 'xlo', axis=1, tiled=True)  4.94 us
    dot_general x1, matrix products, on_device(): lax.dot_general(basis, traces, (((1,), (2,)), ((), ())), preferred_elemen...  3.72 us
  transfers between devices with their start and end apart: 5, of which 4 were waited for; matrix products, arithmetic and copies ran while one was open for 0% of the time, Pallas kernels for 0%

profile of v1, /device:TPU:4, one launch (start us, length us, event | category | flops | bytes accessed | tf_op | source)
XLA Modules:
  0.0 147.5 jit_solution(16755863571880813395)
XLA Ops:
  6.5 0.0 reduce-scatter.2.cloned.1.call-start
  6.5 0.7 convert_element_type.17
  7.2 2.4 %cosine_convert_fusion = (bf16[61,2048]{1,0:T(8,128)(2,1)S(1)}, bf16[61,2048]{1,0:T(8,128)(2,1)S(1)}) fusion(s32[61]{0:T(128)S(1)} %iota_add_fusion.1), kind=kLoop, calls=%fused_computation.18 | loop fusion | flops 2123776 | bytes 499956 | tf_op jit(solution)/shard_map/convert
  9.7 0.0 copy-start.1
  9.7 3.7 %fusion.5 = f32[122,4,256]{2,0,1:T(8,128)S(1)} fusion(bf16[4,256,2048]{2,1,0:T(8,128)(2,1)} %param.3, bf16[61,2048]{1,0:T(8,128)(2,1)S(1)} %get-tuple-element.10, bf16[61,2048]{1,0:T(8,128)(2,1)S(1)} %get-tuple-element.9), kind=kOutput, calls=%fused_computation.13 | convolution fusion | flops 512704512 | bytes 5193728 | tf_op jit(solution)/shard_map/dot_general | solution.py:72
  13.4 0.1 fusion.31
  13.5 0.1 slice_multiply_fusion.1
  13.6 0.0 copy-start
  13.6 0.0 copy-done.1
  13.6 0.4 fusion.21
  14.0 1.9 %collective-permute-start = (f32[122,4,32]{0,2,1:T(8,128)S(1)}, f32[122,4,32]{0,2,1:T(8,128)S(1)}, u32[]{:S(2)}, u32[]{:S(2)}) collective-permute-start(f32[122,4,32]{0,2,1:T(8,128)S(1)} %fusion.21), channel_id=1, source_target_pairs={{0,1},{1,0},{2,3},{3,2},{4,5},{5,4},{6,7},{7,6},{8,9},{9,8},{10,11... | collective-permute-start | bytes 187400 | tf_op jit(solution)/shard_map/ppermute | solution.py:56
  16.0 1.2 collective-permute-done
  17.2 3.5 %collective-permute-start.1 = (f32[122,4,32]{0,2,1:T(8,128)S(1)}, f32[122,4,32]{0,2,1:T(8,128)S(1)}, u32[]{:S(2)}, u32[]{:S(2)}) collective-permute-start(f32[122,4,32]{0,2,1:T(8,128)S(1)} %add.88), channel_id=1, source_target_pairs={{0,2},{1,3},{2,0},{3,1},{4,6},{5,7},{6,4},{7,5},{8,10},{9,11},{10,... | collective-permute-start | bytes 187400 | tf_op jit(solution)/shard_map/ppermute | solution.py:56
  20.7 2.6 %collective-permute-done.1 = f32[122,4,32]{0,2,1:T(8,128)S(1)} collective-permute-done((f32[122,4,32]{0,2,1:T(8,128)S(1)}, f32[122,4,32]{0,2,1:T(8,128)S(1)}, u32[]{:S(2)}, u32[]{:S(2)}) %collective-permute-start.1) | collective-permute-done | bytes 62496 | tf_op jit(solution)/shard_map/ppermute | solution.py:56
  23.4 5.1 %collective-permute-start.2 = (f32[122,4,32]{0,2,1:T(8,128)S(1)}, f32[122,4,32]{0,2,1:T(8,128)S(1)}, u32[]{:S(2)}, u32[]{:S(2)}) collective-permute-start(f32[122,4,32]{0,2,1:T(8,128)S(1)} %add.89), channel_id=1, source_target_pairs={{0,4},{1,5},{2,6},{3,7},{4,0},{5,1},{6,2},{7,3},{8,12},{9,13},{10,... | collective-permute-start | bytes 187400 | tf_op jit(solution)/shard_map/ppermute | solution.py:56
  28.5 13.2 %all_gather.6 = f32[122,8,256]{2,0,1:T(8,128)S(1)} all-gather(f32[122,4,256]{2,0,1:T(8,128)S(1)} %pad_maximum_fusion), channel_id=1, replica_groups=mesh['z'=16,'xlo'=2,'recv'=16] {'xlo'}, dimensions={1}, use_global_device_ids=true | all-gather | bytes 1499136 | tf_op jit(solution)/shard_map/all_gather | solution.py:78
  41.7 0.0 collective-permute-done.2
  41.7 4.9 %collective-permute-start.3 = (f32[122,4,32]{0,2,1:T(8,128)S(1)}, f32[122,4,32]{0,2,1:T(8,128)S(1)}, u32[]{:S(2)}, u32[]{:S(2)}) collective-permute-start(f32[122,4,32]{0,2,1:T(8,128)S(1)} %add.90), channel_id=1, source_target_pairs={{0,8},{1,9},{2,10},{3,11},{4,12},{5,13},{6,14},{7,15},{8,0},{9,1},... | collective-permute-start | bytes 187400 | tf_op jit(solution)/shard_map/ppermute | solution.py:56
  46.6 0.0 copy-done
  46.6 0.1 slice_select_fusion
  46.8 2.6 %collective-permute-done.3 = f32[122,4,32]{0,2,1:T(8,128)S(1)} collective-permute-done((f32[122,4,32]{0,2,1:T(8,128)S(1)}, f32[122,4,32]{0,2,1:T(8,128)S(1)}, u32[]{:S(2)}, u32[]{:S(2)}) %collective-permute-start.3) | collective-permute-done | bytes 62496 | tf_op jit(solution)/shard_map/ppermute | solution.py:56
  49.4 4.9 %all_gather.7 = f32[122,8,32]{0,2,1:T(8,128)S(1)} all-gather(f32[122,4,32]{0,2,1:T(8,128)S(1)} %add.91), channel_id=1, replica_groups=mesh['z'=16,'xlo'=2,'recv'=16] {'xlo'}, dimensions={1}, use_global_device_ids=true | all-gather | bytes 187392 | tf_op jit(solution)/shard_map/all_gather | solution.py:79
  54.4 0.2 constant_dynamic-slice_fusion.1
  54.6 0.2 copy.27
  54.7 0.2 copy.25
  55.0 1.3 fusion.13
  56.3 1.3 fusion.15
  57.6 1.3 fusion.1
  58.9 1.3 fusion
  60.2 0.2 maximum_multiply_fusion
  60.5 2.6 %copy.20 = f32[16,2,64,256]{3,2,1,0:T(8,128)} copy(f32[16,2,64,256]{3,0,2,1:T(8,128)S(1)} %maximum_multiply_fusion) | data formatting | bytes 4194304 | tf_op jit(solution)/shard_map/mul | solution.py:49
  63.1 0.0 reduce-scatter.2.cloned.1.call-update
  63.1 75.9 %reduce-scatter.2.cloned.1.call-done = f32[1,2,64,256]{3,2,1,0:T(8,128)} async-done(((f32[16,2,64,256]{3,2,1,0:T(8,128)}), f32[1,2,64,256]{3,2,1,0:T(8,128)}) %reduce-scatter.2.cloned.1.call-update) | async-done | bytes 131088 | tf_op jit(solution)/shard_map/reduce_scatter | solution.py:85
  139.0 1.6 %copy.21 = f32[1,2,61,256]{3,1,2,0:T(2,128)} copy(f32[1,2,61,256]{3,2,1,0:T(8,128)} %bitcast.26) | data formatting | bytes 249856 | tf_op jit(solution)/shard_map/slice | solution.py:86
  (11 shorter events, 0.2 us)
Async XLA Ops:
  6.5 132.5 %reduce-scatter.2.cloned.1.call-start = ((), (), s32[]{:S(2)}) async-start(), calls=%async_computation.1 | async-start | bytes 2228224 | tf_op jit(solution)/shard_map/reduce_scatter | solution.py:85
  9.7 3.9 %copy-start.1 = (s32[32]{0:T(128)S(1)}, s32[32]{0:T(128)}, u32[]{:S(2)}) copy-start(s32[32]{0:T(128)} %param.5) | copy-start | bytes 388
  13.6 33.0 %copy-start = (pred[64]{0:T(512)(128)(4,1)S(1)}, pred[64]{0:T(512)(128)(4,1)}, u32[]{:S(2)}) copy-start(pred[64]{0:T(512)(128)(4,1)} %constant.19.clone.1) | copy-start | bytes 196
  14.0 3.1 %collective-permute-start = (f32[122,4,32]{0,2,1:T(8,128)S(1)}, f32[122,4,32]{0,2,1:T(8,128)S(1)}, u32[]{:S(2)}, u32[]{:S(2)}) collective-permute-start(f32[122,4,32]{0,2,1:T(8,128)S(1)} %fusion.21), channel_id=1, source_target_pairs={{0,1},{1,0},{2,3},{3,2},{4,5},{5,4},{6,7},{7,6},{8,9},{9,8},{10,11... | collective-permute-start | bytes 187400 | tf_op jit(solution)/shard_map/ppermute | solution.py:56
  17.2 6.2 %collective-permute-start.1 = (f32[122,4,32]{0,2,1:T(8,128)S(1)}, f32[122,4,32]{0,2,1:T(8,128)S(1)}, u32[]{:S(2)}, u32[]{:S(2)}) collective-permute-start(f32[122,4,32]{0,2,1:T(8,128)S(1)} %add.88), channel_id=1, source_target_pairs={{0,2},{1,3},{2,0},{3,1},{4,6},{5,7},{6,4},{7,5},{8,10},{9,11},{10,... | collective-permute-start | bytes 187400 | tf_op jit(solution)/shard_map/ppermute | solution.py:56
  23.4 18.3 %collective-permute-start.2 = (f32[122,4,32]{0,2,1:T(8,128)S(1)}, f32[122,4,32]{0,2,1:T(8,128)S(1)}, u32[]{:S(2)}, u32[]{:S(2)}) collective-permute-start(f32[122,4,32]{0,2,1:T(8,128)S(1)} %add.89), channel_id=1, source_target_pairs={{0,4},{1,5},{2,6},{3,7},{4,0},{5,1},{6,2},{7,3},{8,12},{9,13},{10,... | collective-permute-start | bytes 187400 | tf_op jit(solution)/shard_map/ppermute | solution.py:56
  41.7 7.7 %collective-permute-start.3 = (f32[122,4,32]{0,2,1:T(8,128)S(1)}, f32[122,4,32]{0,2,1:T(8,128)S(1)}, u32[]{:S(2)}, u32[]{:S(2)}) collective-permute-start(f32[122,4,32]{0,2,1:T(8,128)S(1)} %add.90), channel_id=1, source_target_pairs={{0,8},{1,9},{2,10},{3,11},{4,12},{5,13},{6,14},{7,15},{8,0},{9,1},... | collective-permute-start | bytes 187400 | tf_op jit(solution)/shard_map/ppermute | solution.py:56
Sparse Core Ops, SparseCore 0:
  63.2 75.7 reduce-scatter.1

commit v2 on v1

--- a/solution.py
+++ b/solution.py
@@ -75,11 +75,14 @@
     white = whiten_block(spec, valid_float)
     partial_value = jnp.einsum("ktc,sc->kts", white, onehot, precision=lax.Precision.HIGHEST)
     panel = psum_recv(partial_value, lax.axis_size("recv"))
-    white_pair = lax.all_gather(white, "xlo", axis=1, tiled=True)
-    panel_pair = lax.all_gather(panel, "xlo", axis=1, tiled=True)
-    nsrc = panel_pair.shape[2]
-    panel_pair = panel_pair.reshape(panel_pair.shape[0], panel_pair.shape[1], nsrc // pair, pair)
-    panel_own = lax.dynamic_index_in_dim(panel_pair, lax.axis_index("xlo"), axis=3, keepdims=False)
+    swap = [(0, 1), (1, 0)]
+    mine = lax.axis_index("xlo")
+    white_pair = jnp.concatenate([white, lax.ppermute(white, "xlo", swap)], axis=1)
+    nsrc = panel.shape[2]
+    panel = panel.reshape(panel.shape[0], panel.shape[1], nsrc // pair, pair)
+    panel_mine = lax.dynamic_index_in_dim(panel, mine, axis=3, keepdims=False)
+    panel_theirs = lax.dynamic_index_in_dim(panel, 1 - mine, axis=3, keepdims=False)
+    panel_own = jnp.concatenate([panel_mine, lax.ppermute(panel_theirs, "xlo", swap)], axis=1)
     factor = 1.0 / math.sqrt(total_segs)
     totals = cross_terms(panel_own, white_pair, factor)
     out = lax.psum_scatter(totals, "z", scatter_dimension=0, tiled=True)

time: 148 us -> 144 us (0.973)
  the two profiles are of different devices: /device:TPU:4 before, /device:TPU:2 now
where the time goes in v2:
time: 144 us
  waiting for transfers between devices  85.7 us (60%)
  starting transfers between devices  26.6 us (18%)
  between operations  13.7 us (10%)
  matrix products  9.25 us (6%)
  local copies, waits for them, and re-layouts  4.68 us (3%)
  other arithmetic  3.92 us (3%)
    reduce_scatter x1, waiting for transfers between devices, on_device(): out = lax.psum_scatter(totals, 'z', scatter_dimension=0, tiled=True)  74.3 us
    ppermute x4, starting transfers between devices, psum_recv(): value = value + lax.ppermute(value, 'recv', pairs)  14.5 us
    ppermute x4, waiting for transfers between devices, psum_recv(): value = value + lax.ppermute(value, 'recv', pairs)  6.45 us
    ppermute x1, starting transfers between devices, on_device(): lax.ppermute(panel_theirs, 'xlo', swap)  6.37 us
    ppermute x1, starting transfers between devices, on_device(): lax.ppermute(white, 'xlo', swap)  5.7 us
    ppermute x1, waiting for transfers between devices, on_device(): lax.ppermute(panel_theirs, 'xlo', swap)  4.85 us
    dot_general x1, matrix products, on_device(): lax.dot_general(basis, traces, (((1,), (2,)), ((), ())), preferred_elemen...  3.72 us
  transfers between devices with their start and end apart: 7, of which 5 were waited for; matrix products, arithmetic and copies ran while one was open for 0% of the time, Pallas kernels for 0%

profile of v2, /device:TPU:2, one launch (start us, length us, event | category | flops | bytes accessed | tf_op | source)
XLA Modules:
  0.0 143.8 jit_solution(9585716356831838098)
XLA Ops:
  6.5 0.0 reduce-scatter.2.cloned.1.call-start
  6.5 0.7 convert_element_type.17
  7.2 2.4 %cosine_convert_fusion = (bf16[61,2048]{1,0:T(8,128)(2,1)S(1)}, bf16[61,2048]{1,0:T(8,128)(2,1)S(1)}) fusion(s32[61]{0:T(128)S(1)} %iota_add_fusion.1), kind=kLoop, calls=%fused_computation.19 | loop fusion | flops 2123776 | bytes 499956 | tf_op jit(solution)/shard_map/convert
  9.7 0.0 copy-start.1
  9.7 3.7 %fusion.5 = f32[122,4,256]{2,0,1:T(8,128)S(1)} fusion(bf16[4,256,2048]{2,1,0:T(8,128)(2,1)} %param.3, bf16[61,2048]{1,0:T(8,128)(2,1)S(1)} %get-tuple-element.10, bf16[61,2048]{1,0:T(8,128)(2,1)S(1)} %get-tuple-element.9), kind=kOutput, calls=%fused_computation.14 | convolution fusion | flops 512704512 | bytes 5193728 | tf_op jit(solution)/shard_map/dot_general | solution.py:72
  13.4 0.1 fusion.27
  13.5 0.0 copy-start
  13.5 0.1 slice_multiply_fusion.1
  13.6 0.0 copy-done.1
  13.6 0.4 fusion.19
  14.0 1.9 %collective-permute-start.1 = (f32[122,4,32]{0,2,1:T(8,128)S(1)}, f32[122,4,32]{0,2,1:T(8,128)S(1)}, u32[]{:S(2)}, u32[]{:S(2)}) collective-permute-start(f32[122,4,32]{0,2,1:T(8,128)S(1)} %fusion.19), channel_id=1, source_target_pairs={{0,1},{1,0},{2,3},{3,2},{4,5},{5,4},{6,7},{7,6},{8,9},{9,8},{10,11... | collective-permute-start | bytes 187400 | tf_op jit(solution)/shard_map/ppermute | solution.py:56
  16.0 1.2 collective-permute-done.1
  17.2 3.5 %collective-permute-start.2 = (f32[122,4,32]{0,2,1:T(8,128)S(1)}, f32[122,4,32]{0,2,1:T(8,128)S(1)}, u32[]{:S(2)}, u32[]{:S(2)}) collective-permute-start(f32[122,4,32]{0,2,1:T(8,128)S(1)} %add.90), channel_id=1, source_target_pairs={{0,2},{1,3},{2,0},{3,1},{4,6},{5,7},{6,4},{7,5},{8,10},{9,11},{10,... | collective-permute-start | bytes 187400 | tf_op jit(solution)/shard_map/ppermute | solution.py:56
  20.7 2.7 %collective-permute-done.2 = f32[122,4,32]{0,2,1:T(8,128)S(1)} collective-permute-done((f32[122,4,32]{0,2,1:T(8,128)S(1)}, f32[122,4,32]{0,2,1:T(8,128)S(1)}, u32[]{:S(2)}, u32[]{:S(2)}) %collective-permute-start.2) | collective-permute-done | bytes 62496 | tf_op jit(solution)/shard_map/ppermute | solution.py:56
  23.4 5.1 %collective-permute-start.3 = (f32[122,4,32]{0,2,1:T(8,128)S(1)}, f32[122,4,32]{0,2,1:T(8,128)S(1)}, u32[]{:S(2)}, u32[]{:S(2)}) collective-permute-start(f32[122,4,32]{0,2,1:T(8,128)S(1)} %add.91), channel_id=1, source_target_pairs={{0,4},{1,5},{2,6},{3,7},{4,0},{5,1},{6,2},{7,3},{8,12},{9,13},{10,... | collective-permute-start | bytes 187400 | tf_op jit(solution)/shard_map/ppermute | solution.py:56
  28.5 2.6 %collective-permute-done.3 = f32[122,4,32]{0,2,1:T(8,128)S(1)} collective-permute-done((f32[122,4,32]{0,2,1:T(8,128)S(1)}, f32[122,4,32]{0,2,1:T(8,128)S(1)}, u32[]{:S(2)}, u32[]{:S(2)}) %collective-permute-start.3) | collective-permute-done | bytes 62496 | tf_op jit(solution)/shard_map/ppermute | solution.py:56
  31.1 4.0 %collective-permute-start.4 = (f32[122,4,32]{0,2,1:T(8,128)S(1)}, f32[122,4,32]{0,2,1:T(8,128)S(1)}, u32[]{:S(2)}, u32[]{:S(2)}) collective-permute-start(f32[122,4,32]{0,2,1:T(8,128)S(1)} %add.92), channel_id=1, source_target_pairs={{0,8},{1,9},{2,10},{3,11},{4,12},{5,13},{6,14},{7,15},{8,0},{9,1},... | collective-permute-start | bytes 187400 | tf_op jit(solution)/shard_map/ppermute | solution.py:56
  35.1 5.7 %collective-permute-start = (f32[122,4,256]{2,0,1:T(8,128)S(1)}, f32[122,4,256]{2,0,1:T(8,128)S(1)}, u32[]{:S(2)}, u32[]{:S(2)}) collective-permute-start(f32[122,4,256]{2,0,1:T(8,128)S(1)} %pad_maximum_fusion.1), channel_id=1, source_target_pairs={{0,16},{16,0},{1,17},{17,1},{2,18},{18,2},{3,19},{19,3},{4,20},{20... | collective-permute-start | bytes 1499144 | tf_op jit(solution)/shard_map/ppermute | solution.py:80
  40.9 0.0 collective-permute-done.4
  40.9 0.1 constant_dynamic-slice_fusion.1
  41.0 6.4 %collective-permute-start.5 = (f32[122,4,16]{0,2,1:T(8,128)S(1)}, f32[122,4,16]{0,2,1:T(8,128)S(1)}, u32[]{:S(2)}, u32[]{:S(2)}) collective-permute-start(f32[122,4,16]{0,2,1:T(8,128)S(1)} %bitcast.27), channel_id=1, source_target_pairs={{0,16},{16,0},{1,17},{17,1},{2,18},{18,2},{3,19},{19,3},{4,20},{20... | collective-permute-start | bytes 93704 | tf_op jit(solution)/shard_map/ppermute | solution.py:85
  47.3 4.8 %collective-permute-done.5 = f32[122,4,16]{0,2,1:T(8,128)S(1)} collective-permute-done((f32[122,4,16]{0,2,1:T(8,128)S(1)}, f32[122,4,16]{0,2,1:T(8,128)S(1)}, u32[]{:S(2)}, u32[]{:S(2)}) %collective-permute-start.5) | collective-permute-done | bytes 31264 | tf_op jit(solution)/shard_map/ppermute | solution.py:85
  52.2 0.1 pad_maximum_fusion.2
  52.3 0.2 copy.20
  52.4 0.0 copy-done
  52.5 0.1 copy.12
  52.7 0.0 collective-permute-done
  52.7 0.1 pad_maximum_fusion
  52.8 0.1 slice_select_fusion
  52.9 1.3 fusion.11
  54.2 1.3 fusion.13
  55.5 1.3 fusion
  56.8 1.3 fusion.1
  58.1 0.2 maximum_multiply_fusion
  58.3 2.6 %copy.18 = f32[16,2,64,256]{3,2,1,0:T(8,128)} copy(f32[16,2,64,256]{3,0,2,1:T(8,128)S(1)} %maximum_multiply_fusion) | data formatting | bytes 4194304 | tf_op jit(solution)/shard_map/mul | solution.py:49
  60.9 0.0 reduce-scatter.2.cloned.1.call-update
  60.9 74.3 %reduce-scatter.2.cloned.1.call-done = f32[1,2,64,256]{3,2,1,0:T(8,128)} async-done(((f32[16,2,64,256]{3,2,1,0:T(8,128)}), f32[1,2,64,256]{3,2,1,0:T(8,128)}) %reduce-scatter.2.cloned.1.call-update) | async-done | bytes 131088 | tf_op jit(solution)/shard_map/reduce_scatter | solution.py:88
  135.3 1.6 %copy.19 = f32[1,2,61,256]{3,1,2,0:T(2,128)} copy(f32[1,2,61,256]{3,2,1,0:T(8,128)} %bitcast.26) | data formatting | bytes 249856 | tf_op jit(solution)/shard_map/slice | solution.py:89
  (11 shorter events, 0.2 us)
Async XLA Ops:
  6.5 128.7 %reduce-scatter.2.cloned.1.call-start = ((), (), s32[]{:S(2)}) async-start(), calls=%async_computation.1 | async-start | bytes 2228224 | tf_op jit(solution)/shard_map/reduce_scatter | solution.py:88
  9.7 4.0 %copy-start.1 = (s32[32]{0:T(128)S(1)}, s32[32]{0:T(128)}, u32[]{:S(2)}) copy-start(s32[32]{0:T(128)} %param.5) | copy-start | bytes 388
  13.5 39.0 %copy-start = (pred[64]{0:T(512)(128)(4,1)S(1)}, pred[64]{0:T(512)(128)(4,1)}, u32[]{:S(2)}) copy-start(pred[64]{0:T(512)(128)(4,1)} %constant.38.clone.1) | copy-start | bytes 196
  14.0 3.1 %collective-permute-start.1 = (f32[122,4,32]{0,2,1:T(8,128)S(1)}, f32[122,4,32]{0,2,1:T(8,128)S(1)}, u32[]{:S(2)}, u32[]{:S(2)}) collective-permute-start(f32[122,4,32]{0,2,1:T(8,128)S(1)} %fusion.19), channel_id=1, source_target_pairs={{0,1},{1,0},{2,3},{3,2},{4,5},{5,4},{6,7},{7,6},{8,9},{9,8},{10,11... | collective-permute-start | bytes 187400 | tf_op jit(solution)/shard_map/ppermute | solution.py:56
  17.2 6.2 %collective-permute-start.2 = (f32[122,4,32]{0,2,1:T(8,128)S(1)}, f32[122,4,32]{0,2,1:T(8,128)S(1)}, u32[]{:S(2)}, u32[]{:S(2)}) collective-permute-start(f32[122,4,32]{0,2,1:T(8,128)S(1)} %add.90), channel_id=1, source_target_pairs={{0,2},{1,3},{2,0},{3,1},{4,6},{5,7},{6,4},{7,5},{8,10},{9,11},{10,... | collective-permute-start | bytes 187400 | tf_op jit(solution)/shard_map/ppermute | solution.py:56
  23.4 7.7 %collective-permute-start.3 = (f32[122,4,32]{0,2,1:T(8,128)S(1)}, f32[122,4,32]{0,2,1:T(8,128)S(1)}, u32[]{:S(2)}, u32[]{:S(2)}) collective-permute-start(f32[122,4,32]{0,2,1:T(8,128)S(1)} %add.91), channel_id=1, source_target_pairs={{0,4},{1,5},{2,6},{3,7},{4,0},{5,1},{6,2},{7,3},{8,12},{9,13},{10,... | collective-permute-start | bytes 187400 | tf_op jit(solution)/shard_map/ppermute | solution.py:56
  31.1 9.8 %collective-permute-start.4 = (f32[122,4,32]{0,2,1:T(8,128)S(1)}, f32[122,4,32]{0,2,1:T(8,128)S(1)}, u32[]{:S(2)}, u32[]{:S(2)}) collective-permute-start(f32[122,4,32]{0,2,1:T(8,128)S(1)} %add.92), channel_id=1, source_target_pairs={{0,8},{1,9},{2,10},{3,11},{4,12},{5,13},{6,14},{7,15},{8,0},{9,1},... | collective-permute-start | bytes 187400 | tf_op jit(solution)/shard_map/ppermute | solution.py:56
  35.1 17.5 %collective-permute-start = (f32[122,4,256]{2,0,1:T(8,128)S(1)}, f32[122,4,256]{2,0,1:T(8,128)S(1)}, u32[]{:S(2)}, u32[]{:S(2)}) collective-permute-start(f32[122,4,256]{2,0,1:T(8,128)S(1)} %pad_maximum_fusion.1), channel_id=1, source_target_pairs={{0,16},{16,0},{1,17},{17,1},{2,18},{18,2},{3,19},{19,3},{4,20},{20... | collective-permute-start | bytes 1499144 | tf_op jit(solution)/shard_map/ppermute | solution.py:80
  41.0 11.2 %collective-permute-start.5 = (f32[122,4,16]{0,2,1:T(8,128)S(1)}, f32[122,4,16]{0,2,1:T(8,128)S(1)}, u32[]{:S(2)}, u32[]{:S(2)}) collective-permute-start(f32[122,4,16]{0,2,1:T(8,128)S(1)} %bitcast.27), channel_id=1, source_target_pairs={{0,16},{16,0},{1,17},{17,1},{2,18},{18,2},{3,19},{19,3},{4,20},{20... | collective-permute-start | bytes 93704 | tf_op jit(solution)/shard_map/ppermute | solution.py:85
Sparse Core Ops, SparseCore 0:
  61.1 74.1 reduce-scatter.1

commit v3 on v1

--- a/solution.py
+++ b/solution.py
@@ -61,8 +61,9 @@
 def on_device(traces, valid, src_idx):
     seg_count = traces.shape[0]
     chan_count = traces.shape[1]
-    pair = lax.axis_size("xlo")
-    total_segs = seg_count * pair * lax.axis_size("z")
+    group = ("zlo", "xlo")
+    width = lax.axis_size("zlo") * lax.axis_size("xlo")
+    total_segs = seg_count * width * lax.axis_size("zhi")
     basis = basis_table()
     valid_float = valid.astype(jnp.float32)
     offset = lax.axis_index("recv") * chan_count
@@ -73,28 +74,35 @@
         basis, traces, (((1,), (2,)), ((), ())), preferred_element_type=jnp.float32
     )
     white = whiten_block(spec, valid_float)
+    q = lax.axis_index("zlo") * lax.axis_size("xlo") + lax.axis_index("xlo")
+    moves = [[(r, r ^ b) for r in range(width)] for b in range(1, width)]
+    white_all = jnp.concatenate(
+        [white] + [lax.ppermute(white, group, pairs) for pairs in moves], axis=1
+    )
     partial_value = jnp.einsum("ktc,sc->kts", white, onehot, precision=lax.Precision.HIGHEST)
     panel = psum_recv(partial_value, lax.axis_size("recv"))
-    white_pair = lax.all_gather(white, "xlo", axis=1, tiled=True)
-    panel_pair = lax.all_gather(panel, "xlo", axis=1, tiled=True)
-    nsrc = panel_pair.shape[2]
-    panel_pair = panel_pair.reshape(panel_pair.shape[0], panel_pair.shape[1], nsrc // pair, pair)
-    panel_own = lax.dynamic_index_in_dim(panel_pair, lax.axis_index("xlo"), axis=3, keepdims=False)
+    nsrc = panel.shape[2]
+    panel = panel.reshape(panel.shape[0], panel.shape[1], nsrc // width, width)
+    blocks = [lax.dynamic_index_in_dim(panel, q, axis=3, keepdims=False)]
+    for b, pairs in zip(range(1, width), moves):
+        theirs = lax.dynamic_index_in_dim(panel, q ^ b, axis=3, keepdims=False)
+        blocks.append(lax.ppermute(theirs, group, pairs))
+    panel_own = jnp.concatenate(blocks, axis=1)
     factor = 1.0 / math.sqrt(total_segs)
-    totals = cross_terms(panel_own, white_pair, factor)
-    out = lax.psum_scatter(totals, "z", scatter_dimension=0, tiled=True)
+    totals = cross_terms(panel_own, white_all, factor)
+    out = lax.psum_scatter(totals, "zhi", scatter_dimension=0, tiled=True)
     return out[:, :, :NB, :]
 
 
 def solution(mesh):
     tm_size = mesh.shape["tm"]
     recv_size = mesh.shape["recv"]
-    devices = np.asarray(mesh.devices).reshape(tm_size // 2, 2, recv_size)
-    inner = Mesh(devices, ("z", "xlo", "recv"))
+    devices = np.asarray(mesh.devices).reshape(tm_size // 4, 2, 2, recv_size)
+    inner = Mesh(devices, ("zhi", "zlo", "xlo", "recv"))
     return jax.shard_map(
         on_device,
         mesh=inner,
-        in_specs=(P(("z", "xlo"), "recv", None), P(("z", "xlo"), "recv"), P()),
-        out_specs=P(("z", "xlo"), None, None, "recv"),
+        in_specs=(P(("zhi", "zlo", "xlo"), "recv", None), P(("zhi", "zlo", "xlo"), "recv"), P()),
+        out_specs=P(("zhi", "zlo", "xlo"), None, None, "recv"),
         check_vma=False,
     )

time: 148 us -> 140 us (0.946)
  the two profiles are of different devices: /device:TPU:4 before, /device:TPU:16 now
where the time goes in v3:
time: 140 us; the launch traced here: 139 us
  waiting for transfers between devices  76.8 us (55%)
  starting transfers between devices  31.9 us (23%)
  between operations  13.7 us (10%)
  matrix products  9.23 us (7%)
  other arithmetic  3.88 us (3%)
  local copies, waits for them, and re-layouts  3.56 us (3%)
    reduce_scatter x1, waiting for transfers between devices, on_device(): out = lax.psum_scatter(totals, 'zhi', scatter_dimension=0, tiled=True)  55.4 us
    ppermute x4, starting transfers between devices, psum_recv(): value = value + lax.ppermute(value, 'recv', pairs)  15.5 us
    ppermute x4, waiting for transfers between devices, psum_recv(): value = value + lax.ppermute(value, 'recv', pairs)  11.1 us
    ppermute x3, waiting for transfers between devices, on_device(): blocks.append(lax.ppermute(theirs, group, pairs))  10.3 us
    ppermute x3, starting transfers between devices, on_device(): lax.ppermute(white, group, pairs)  9.21 us
    ppermute x3, starting transfers between devices, on_device(): blocks.append(lax.ppermute(theirs, group, pairs))  7.26 us
    dot_general x1, matrix products, on_device(): lax.dot_general(basis, traces, (((1,), (2,)), ((), ())), preferred_elemen...  3.72 us
  transfers between devices with their start and end apart: 11, of which 7 were waited for; matrix products, arithmetic and copies ran while one was open for 0% of the time, Pallas kernels for 0%

profile of v3, /device:TPU:16, one launch (start us, length us, event | category | flops | bytes accessed | tf_op | source)
XLA Modules:
  0.0 139.2 jit_solution(5109622698838506664)
XLA Ops:
  6.5 0.0 reduce-scatter.2.cloned.1.call-start
  6.5 0.7 convert_element_type.17
  7.2 2.4 %cosine_convert_fusion = (bf16[61,2048]{1,0:T(8,128)(2,1)S(1)}, bf16[61,2048]{1,0:T(8,128)(2,1)S(1)}) fusion(s32[61]{0:T(128)S(1)} %iota_add_fusion.1), kind=kLoop, calls=%fused_computation.26 | loop fusion | flops 2123776 | bytes 499956 | tf_op jit(solution)/shard_map/convert
  9.7 0.0 copy-start.1
  9.7 3.7 %fusion.17 = f32[122,4,256]{2,0,1:T(8,128)S(1)} fusion(bf16[4,256,2048]{2,1,0:T(8,128)(2,1)} %param.3, bf16[61,2048]{1,0:T(8,128)(2,1)S(1)} %get-tuple-element.12, bf16[61,2048]{1,0:T(8,128)(2,1)S(1)} %get-tuple-element.11), kind=kOutput, calls=%fused_computation.21 | convolution fusion | flops 512704512 | bytes 5193728 | tf_op jit(solution)/shard_map/dot_general | solution.py:73
  13.4 0.1 fusion.33
  13.5 0.0 copy-start
  13.5 0.1 slice_multiply_fusion.1
  13.6 0.0 copy-done.1
  13.6 0.4 fusion.25
  14.0 1.9 %collective-permute-start.3 = (f32[122,4,32]{0,2,1:T(8,128)S(1)}, f32[122,4,32]{0,2,1:T(8,128)S(1)}, u32[]{:S(2)}, u32[]{:S(2)}) collective-permute-start(f32[122,4,32]{0,2,1:T(8,128)S(1)} %fusion.25), channel_id=1, source_target_pairs={{0,1},{1,0},{2,3},{3,2},{4,5},{5,4},{6,7},{7,6},{8,9},{9,8},{10,11... | collective-permute-start | bytes 187400 | tf_op jit(solution)/shard_map/ppermute | solution.py:56
  16.0 1.2 collective-permute-done.3
  17.2 3.2 %collective-permute-start.4 = (f32[122,4,32]{0,2,1:T(8,128)S(1)}, f32[122,4,32]{0,2,1:T(8,128)S(1)}, u32[]{:S(2)}, u32[]{:S(2)}) collective-permute-start(f32[122,4,32]{0,2,1:T(8,128)S(1)} %add.98), channel_id=1, source_target_pairs={{0,2},{1,3},{2,0},{3,1},{4,6},{5,7},{6,4},{7,5},{8,10},{9,11},{10,... | collective-permute-start | bytes 187400 | tf_op jit(solution)/shard_map/ppermute | solution.py:56
  20.4 3.0 %collective-permute-done.4 = f32[122,4,32]{0,2,1:T(8,128)S(1)} collective-permute-done((f32[122,4,32]{0,2,1:T(8,128)S(1)}, f32[122,4,32]{0,2,1:T(8,128)S(1)}, u32[]{:S(2)}, u32[]{:S(2)}) %collective-permute-start.4) | collective-permute-done | bytes 62496 | tf_op jit(solution)/shard_map/ppermute | solution.py:56
  23.4 7.6 %collective-permute-start.5 = (f32[122,4,32]{0,2,1:T(8,128)S(1)}, f32[122,4,32]{0,2,1:T(8,128)S(1)}, u32[]{:S(2)}, u32[]{:S(2)}) collective-permute-start(f32[122,4,32]{0,2,1:T(8,128)S(1)} %add.99), channel_id=1, source_target_pairs={{0,4},{1,5},{2,6},{3,7},{4,0},{5,1},{6,2},{7,3},{8,12},{9,13},{10,... | collective-permute-start | bytes 187400 | tf_op jit(solution)/shard_map/ppermute | solution.py:56
  31.0 2.2 %collective-permute-done.5 = f32[122,4,32]{0,2,1:T(8,128)S(1)} collective-permute-done((f32[122,4,32]{0,2,1:T(8,128)S(1)}, f32[122,4,32]{0,2,1:T(8,128)S(1)}, u32[]{:S(2)}, u32[]{:S(2)}) %collective-permute-start.5) | collective-permute-done | bytes 62496 | tf_op jit(solution)/shard_map/ppermute | solution.py:56
  33.2 2.7 %collective-permute-start.6 = (f32[122,4,32]{0,2,1:T(8,128)S(1)}, f32[122,4,32]{0,2,1:T(8,128)S(1)}, u32[]{:S(2)}, u32[]{:S(2)}) collective-permute-start(f32[122,4,32]{0,2,1:T(8,128)S(1)} %add.100), channel_id=1, source_target_pairs={{0,8},{1,9},{2,10},{3,11},{4,12},{5,13},{6,14},{7,15},{8,0},{9,1},... | collective-permute-start | bytes 187400 | tf_op jit(solution)/shard_map/ppermute | solution.py:56
  36.0 3.9 %collective-permute-start.2 = (f32[122,4,256]{2,0,1:T(8,128)S(1)}, f32[122,4,256]{2,0,1:T(8,128)S(1)}, u32[]{:S(2)}, u32[]{:S(2)}) collective-permute-start(f32[122,4,256]{2,0,1:T(8,128)S(1)} %pad_maximum_fusion.1), channel_id=1, source_target_pairs={{0,48},{16,32},{32,16},{48,0},{1,49},{17,33},{33,17},{49,1},{2,50}... | collective-permute-start | bytes 1499144 | tf_op jit(solution)/shard_map/ppermute | solution.py:80
  39.9 2.0 %collective-permute-start.1 = (f32[122,4,256]{2,0,1:T(8,128)S(1)}, f32[122,4,256]{2,0,1:T(8,128)S(1)}, u32[]{:S(2)}, u32[]{:S(2)}) collective-permute-start(f32[122,4,256]{2,0,1:T(8,128)S(1)} %pad_maximum_fusion.1), channel_id=1, source_target_pairs={{0,32},{16,48},{32,0},{48,16},{1,33},{17,49},{33,1},{49,17},{2,34}... | collective-permute-start | bytes 1499144 | tf_op jit(solution)/shard_map/ppermute | solution.py:80
  41.9 3.3 %collective-permute-start = (f32[122,4,256]{2,0,1:T(8,128)S(1)}, f32[122,4,256]{2,0,1:T(8,128)S(1)}, u32[]{:S(2)}, u32[]{:S(2)}) collective-permute-start(f32[122,4,256]{2,0,1:T(8,128)S(1)} %pad_maximum_fusion.1), channel_id=1, source_target_pairs={{0,16},{16,0},{32,48},{48,32},{1,17},{17,1},{33,49},{49,33},{2,18}... | collective-permute-start | bytes 1499144 | tf_op jit(solution)/shard_map/ppermute | solution.py:80
  45.3 4.7 %collective-permute-done.6 = f32[122,4,32]{0,2,1:T(8,128)S(1)} collective-permute-done((f32[122,4,32]{0,2,1:T(8,128)S(1)}, f32[122,4,32]{0,2,1:T(8,128)S(1)}, u32[]{:S(2)}, u32[]{:S(2)}) %collective-permute-start.6) | collective-permute-done | bytes 62496 | tf_op jit(solution)/shard_map/ppermute | solution.py:56
  50.0 0.1 constant_dynamic-slice_fusion.3
  50.1 2.6 %collective-permute-start.9 = (f32[122,4,8]{0,2,1:T(8,128)S(1)}, f32[122,4,8]{0,2,1:T(8,128)S(1)}, u32[]{:S(2)}, u32[]{:S(2)}) collective-permute-start(f32[122,4,8]{0,2,1:T(8,128)S(1)} %bitcast.29), channel_id=1, source_target_pairs={{0,48},{16,32},{32,16},{48,0},{1,49},{17,33},{33,17},{49,1},{2,50}... | collective-permute-start | bytes 46856 | tf_op jit(solution)/shard_map/ppermute | solution.py:89
  52.6 1.9 %collective-permute-start.8 = (f32[122,4,8]{0,2,1:T(8,128)S(1)}, f32[122,4,8]{0,2,1:T(8,128)S(1)}, u32[]{:S(2)}, u32[]{:S(2)}) collective-permute-start(f32[122,4,8]{0,2,1:T(8,128)S(1)} %bitcast.28), channel_id=1, source_target_pairs={{0,32},{16,48},{32,0},{48,16},{1,33},{17,49},{33,1},{49,17},{2,34}... | collective-permute-start | bytes 46856 | tf_op jit(solution)/shard_map/ppermute | solution.py:89
  54.6 7.5 %collective-permute-done.9 = f32[122,4,8]{0,2,1:T(8,128)S(1)} collective-permute-done((f32[122,4,8]{0,2,1:T(8,128)S(1)}, f32[122,4,8]{0,2,1:T(8,128)S(1)}, u32[]{:S(2)}, u32[]{:S(2)}) %collective-permute-start.9) | collective-permute-done | bytes 15648 | tf_op jit(solution)/shard_map/ppermute | solution.py:89
  62.0 2.7 %collective-permute-start.7 = (f32[122,4,8]{0,2,1:T(8,128)S(1)}, f32[122,4,8]{0,2,1:T(8,128)S(1)}, u32[]{:S(2)}, u32[]{:S(2)}) collective-permute-start(f32[122,4,8]{0,2,1:T(8,128)S(1)} %bitcast.27), channel_id=1, source_target_pairs={{0,16},{16,0},{32,48},{48,32},{1,17},{17,1},{33,49},{49,33},{2,18}... | collective-permute-start | bytes 46856 | tf_op jit(solution)/shard_map/ppermute | solution.py:89
  64.8 0.0 collective-permute-done.8
  64.8 2.9 %collective-permute-done.7 = f32[122,4,8]{0,2,1:T(8,128)S(1)} collective-permute-done((f32[122,4,8]{0,2,1:T(8,128)S(1)}, f32[122,4,8]{0,2,1:T(8,128)S(1)}, u32[]{:S(2)}, u32[]{:S(2)}) %collective-permute-start.7) | collective-permute-done | bytes 15648 | tf_op jit(solution)/shard_map/ppermute | solution.py:89
  67.7 0.1 slice.35
  67.8 0.2 copy.22
  67.9 0.0 copy-done
  68.0 0.2 copy.14
  68.2 0.0 collective-permute-done.2
  68.2 0.0 collective-permute-done.1
  68.2 0.0 collective-permute-done
  68.2 0.2 pad_maximum_fusion
  68.4 0.1 slice.34
  68.5 0.2 slice_select_fusion
  68.7 1.3 fusion.1
  70.0 1.3 fusion.11
  71.3 1.3 fusion.8
  72.6 1.3 fusion
  73.8 0.1 maximum_multiply_fusion
  73.9 1.3 copy.20
  75.2 0.0 reduce-scatter.2.cloned.1.call-update
  75.2 55.4 %reduce-scatter.2.cloned.1.call-done = f32[1,2,64,256]{3,2,1,0:T(8,128)} async-done(((f32[8,2,64,256]{3,2,1,0:T(8,128)}), f32[1,2,64,256]{3,2,1,0:T(8,128)}) %reduce-scatter.2.cloned.1.call-update) | async-done | bytes 131088 | tf_op jit(solution)/shard_map/reduce_scatter | solution.py:93
  130.7 1.6 %copy.21 = f32[1,2,61,256]{3,1,2,0:T(2,128)} copy(f32[1,2,61,256]{3,2,1,0:T(8,128)} %bitcast.25) | data formatting | bytes 249856 | tf_op jit(solution)/shard_map/slice | solution.py:94
  (11 shorter events, 0.1 us)
Async XLA Ops:
  6.5 124.1 %reduce-scatter.2.cloned.1.call-start = ((), (), s32[]{:S(2)}) async-start(), calls=%async_computation.1 | async-start | bytes 1179648 | tf_op jit(solution)/shard_map/reduce_scatter | solution.py:93
  9.7 4.0 %copy-start.1 = (s32[32]{0:T(128)S(1)}, s32[32]{0:T(128)}, u32[]{:S(2)}) copy-start(s32[32]{0:T(128)} %param.5) | copy-start | bytes 388
  13.5 54.5 %copy-start = (pred[64]{0:T(512)(128)(4,1)S(1)}, pred[64]{0:T(512)(128)(4,1)}, u32[]{:S(2)}) copy-start(pred[64]{0:T(512)(128)(4,1)} %constant.46.clone.1) | copy-start | bytes 196
  14.0 3.1 %collective-permute-start.3 = (f32[122,4,32]{0,2,1:T(8,128)S(1)}, f32[122,4,32]{0,2,1:T(8,128)S(1)}, u32[]{:S(2)}, u32[]{:S(2)}) collective-permute-start(f32[122,4,32]{0,2,1:T(8,128)S(1)} %fusion.25), channel_id=1, source_target_pairs={{0,1},{1,0},{2,3},{3,2},{4,5},{5,4},{6,7},{7,6},{8,9},{9,8},{10,11... | collective-permute-start | bytes 187400 | tf_op jit(solution)/shard_map/ppermute | solution.py:56
  17.2 6.2 %collective-permute-start.4 = (f32[122,4,32]{0,2,1:T(8,128)S(1)}, f32[122,4,32]{0,2,1:T(8,128)S(1)}, u32[]{:S(2)}, u32[]{:S(2)}) collective-permute-start(f32[122,4,32]{0,2,1:T(8,128)S(1)} %add.98), channel_id=1, source_target_pairs={{0,2},{1,3},{2,0},{3,1},{4,6},{5,7},{6,4},{7,5},{8,10},{9,11},{10,... | collective-permute-start | bytes 187400 | tf_op jit(solution)/shard_map/ppermute | solution.py:56
  23.4 9.8 %collective-permute-start.5 = (f32[122,4,32]{0,2,1:T(8,128)S(1)}, f32[122,4,32]{0,2,1:T(8,128)S(1)}, u32[]{:S(2)}, u32[]{:S(2)}) collective-permute-start(f32[122,4,32]{0,2,1:T(8,128)S(1)} %add.99), channel_id=1, source_target_pairs={{0,4},{1,5},{2,6},{3,7},{4,0},{5,1},{6,2},{7,3},{8,12},{9,13},{10,... | collective-permute-start | bytes 187400 | tf_op jit(solution)/shard_map/ppermute | solution.py:56
  33.2 16.7 %collective-permute-start.6 = (f32[122,4,32]{0,2,1:T(8,128)S(1)}, f32[122,4,32]{0,2,1:T(8,128)S(1)}, u32[]{:S(2)}, u32[]{:S(2)}) collective-permute-start(f32[122,4,32]{0,2,1:T(8,128)S(1)} %add.100), channel_id=1, source_target_pairs={{0,8},{1,9},{2,10},{3,11},{4,12},{5,13},{6,14},{7,15},{8,0},{9,1},... | collective-permute-start | bytes 187400 | tf_op jit(solution)/shard_map/ppermute | solution.py:56
  36.0 32.1 %collective-permute-start.2 = (f32[122,4,256]{2,0,1:T(8,128)S(1)}, f32[122,4,256]{2,0,1:T(8,128)S(1)}, u32[]{:S(2)}, u32[]{:S(2)}) collective-permute-start(f32[122,4,256]{2,0,1:T(8,128)S(1)} %pad_maximum_fusion.1), channel_id=1, source_target_pairs={{0,48},{16,32},{32,16},{48,0},{1,49},{17,33},{33,17},{49,1},{2,50}... | collective-permute-start | bytes 1499144 | tf_op jit(solution)/shard_map/ppermute | solution.py:80
  39.9 28.3 %collective-permute-start.1 = (f32[122,4,256]{2,0,1:T(8,128)S(1)}, f32[122,4,256]{2,0,1:T(8,128)S(1)}, u32[]{:S(2)}, u32[]{:S(2)}) collective-permute-start(f32[122,4,256]{2,0,1:T(8,128)S(1)} %pad_maximum_fusion.1), channel_id=1, source_target_pairs={{0,32},{16,48},{32,0},{48,16},{1,33},{17,49},{33,1},{49,17},{2,34}... | collective-permute-start | bytes 1499144 | tf_op jit(solution)/shard_map/ppermute | solution.py:80
  41.9 26.3 %collective-permute-start = (f32[122,4,256]{2,0,1:T(8,128)S(1)}, f32[122,4,256]{2,0,1:T(8,128)S(1)}, u32[]{:S(2)}, u32[]{:S(2)}) collective-permute-start(f32[122,4,256]{2,0,1:T(8,128)S(1)} %pad_maximum_fusion.1), channel_id=1, source_target_pairs={{0,16},{16,0},{32,48},{48,32},{1,17},{17,1},{33,49},{49,33},{2,18}... | collective-permute-start | bytes 1499144 | tf_op jit(solution)/shard_map/ppermute | solution.py:80
  50.1 12.0 %collective-permute-start.9 = (f32[122,4,8]{0,2,1:T(8,128)S(1)}, f32[122,4,8]{0,2,1:T(8,128)S(1)}, u32[]{:S(2)}, u32[]{:S(2)}) collective-permute-start(f32[122,4,8]{0,2,1:T(8,128)S(1)} %bitcast.29), channel_id=1, source_target_pairs={{0,48},{16,32},{32,16},{48,0},{1,49},{17,33},{33,17},{49,1},{2,50}... | collective-permute-start | bytes 46856 | tf_op jit(solution)/shard_map/ppermute | solution.py:89
  52.6 12.2 %collective-permute-start.8 = (f32[122,4,8]{0,2,1:T(8,128)S(1)}, f32[122,4,8]{0,2,1:T(8,128)S(1)}, u32[]{:S(2)}, u32[]{:S(2)}) collective-permute-start(f32[122,4,8]{0,2,1:T(8,128)S(1)} %bitcast.28), channel_id=1, source_target_pairs={{0,32},{16,48},{32,0},{48,16},{1,33},{17,49},{33,1},{49,17},{2,34}... | collective-permute-start | bytes 46856 | tf_op jit(solution)/shard_map/ppermute | solution.py:89
  62.0 5.6 %collective-permute-start.7 = (f32[122,4,8]{0,2,1:T(8,128)S(1)}, f32[122,4,8]{0,2,1:T(8,128)S(1)}, u32[]{:S(2)}, u32[]{:S(2)}) collective-permute-start(f32[122,4,8]{0,2,1:T(8,128)S(1)} %bitcast.27), channel_id=1, source_target_pairs={{0,16},{16,0},{32,48},{48,32},{1,17},{17,1},{33,49},{49,33},{2,18}... | collective-permute-start | bytes 46856 | tf_op jit(solution)/shard_map/ppermute | solution.py:89
Sparse Core Ops, SparseCore 0:
  75.4 55.2 reduce-scatter.1

commit v4 on v3

--- a/solution.py
+++ b/solution.py
@@ -76,18 +76,21 @@
     white = whiten_block(spec, valid_float)
     q = lax.axis_index("zlo") * lax.axis_size("xlo") + lax.axis_index("xlo")
     moves = [[(r, r ^ b) for r in range(width)] for b in range(1, width)]
-    white_all = jnp.concatenate(
-        [white] + [lax.ppermute(white, group, pairs) for pairs in moves], axis=1
+    partial_value = jnp.einsum("ktc,sc->kts", white, onehot, precision=lax.Precision.HIGHEST)
+    nsrc = partial_value.shape[2]
+    partial_value = partial_value.reshape(
+        partial_value.shape[0], partial_value.shape[1], nsrc // width, width
     )
-    partial_value = jnp.einsum("ktc,sc->kts", white, onehot, precision=lax.Precision.HIGHEST)
-    panel = psum_recv(partial_value, lax.axis_size("recv"))
-    nsrc = panel.shape[2]
-    panel = panel.reshape(panel.shape[0], panel.shape[1], nsrc // width, width)
-    blocks = [lax.dynamic_index_in_dim(panel, q, axis=3, keepdims=False)]
+    white_parts = [white]
+    value_parts = [lax.dynamic_index_in_dim(partial_value, q, axis=3, keepdims=False)]
     for b, pairs in zip(range(1, width), moves):
-        theirs = lax.dynamic_index_in_dim(panel, q ^ b, axis=3, keepdims=False)
-        blocks.append(lax.ppermute(theirs, group, pairs))
-    panel_own = jnp.concatenate(blocks, axis=1)
+        theirs = lax.dynamic_index_in_dim(partial_value, q ^ b, axis=3, keepdims=False)
+        got_white, got_value = lax.ppermute((white, theirs), group, pairs)
+        white_parts.append(got_white)
+        value_parts.append(got_value)
+    white_parts, value_parts = lax.optimization_barrier((white_parts, value_parts))
+    white_all = jnp.concatenate(white_parts, axis=1)
+    panel_own = psum_recv(jnp.concatenate(value_parts, axis=1), lax.axis_size("recv"))
     factor = 1.0 / math.sqrt(total_segs)
     totals = cross_terms(panel_own, white_all, factor)
     out = lax.psum_scatter(totals, "zhi", scatter_dimension=0, tiled=True)

time: 140 us -> 169 us (1.21)
  waiting for transfers between devices: 76.8 us -> 103 us
  local copies, waits for them, and re-layouts: 3.56 us -> 5.41 us
    ppermute x4, waiting for transfers between devices: 11.1 us -> 36.4 us  [psum_recv(): value = value + lax.ppermute(value, 'recv', pairs)]
    ppermute x6, starting transfers between devices: 16.5 us -> 20.1 us  [on_device(): got_white, got_value = lax.ppermute((white, theirs), group, pairs)]
    ppermute x4, starting transfers between devices: 15.5 us -> 12.5 us  [psum_recv(): value = value + lax.ppermute(value, 'recv', pairs)]
    unnamed x5 -> x11, local copies, waits for them, and re-layouts: 0.2 us -> 1.96 us
  transfers between devices with their start and end apart: 11 -> 11, of which waited for: 7 -> 7; matrix products, arithmetic and copies ran while one was open for 0% -> 1% of each run, Pallas kernels for 0% -> 0%
where the time goes in v4:
time: 169 us; the launch traced here: 168 us
  waiting for transfers between devices  103 us (61%)
  starting transfers between devices  32.5 us (19%)
  between operations  13.7 us (8%)
  matrix products  9.23 us (5%)
  local copies, waits for them, and re-layouts  5.41 us (3%)
  other arithmetic  3.99 us (2%)
    reduce_scatter x1, waiting for transfers between devices, on_device(): out = lax.psum_scatter(totals, 'zhi', scatter_dimension=0, tiled=True)  56.9 us
    ppermute x4, waiting for transfers between devices, psum_recv(): value = value + lax.ppermute(value, 'recv', pairs)  36.4 us
    ppermute x6, starting transfers between devices, on_device(): got_white, got_value = lax.ppermute((white, theirs), group, pairs)  20.1 us
    ppermute x4, starting transfers between devices, psum_recv(): value = value + lax.ppermute(value, 'recv', pairs)  12.5 us
    ppermute x6, waiting for transfers between devices, on_device(): got_white, got_value = lax.ppermute((white, theirs), group, pairs)  10.1 us
    dot_general x1, matrix products, on_device(): lax.dot_general(basis, traces, (((1,), (2,)), ((), ())), preferred_elemen...  3.71 us
  transfers between devices with their start and end apart: 11, of which 7 were waited for; matrix products, arithmetic and copies ran while one was open for 1% of the time, Pallas kernels for 0%

profile of v4, /device:TPU:16, one launch (start us, length us, event | category | flops | bytes accessed | tf_op | source)
XLA Modules:
  0.0 168.3 jit_solution(5417386808590079648)
XLA Ops:
  6.5 0.0 reduce-scatter.2.cloned.1.call-start
  6.5 2.4 %cosine_convert_fusion = (bf16[61,2048]{1,0:T(8,128)(2,1)S(1)}, bf16[61,2048]{1,0:T(8,128)(2,1)S(1)}) fusion(s32[61]{0:T(128)S(1)} %iota_add_fusion.1), kind=kLoop, calls=%fused_computation.24 | loop fusion | flops 2123776 | bytes 499956 | tf_op jit(solution)/shard_map/convert
  9.0 0.7 convert_element_type.17
  9.7 3.7 %fusion.11 = f32[122,4,256]{2,0,1:T(8,128)S(1)} fusion(bf16[4,256,2048]{2,1,0:T(8,128)(2,1)} %param.3, bf16[61,2048]{1,0:T(8,128)(2,1)S(1)} %get-tuple-element.28, bf16[61,2048]{1,0:T(8,128)(2,1)S(1)} %get-tuple-element.27), kind=kOutput, calls=%fused_computation.19 | convolution fusion | flops 512704512 | bytes 5193728 | tf_op jit(solution)/shard_map/dot_general | solution.py:73
  13.4 0.0 copy-start.3
  13.4 0.1 fusion.33
  13.5 0.1 slice_multiply_fusion.1
  13.6 3.4 %collective-permute-start = (f32[122,4,256]{2,0,1:T(8,128)S(1)}, f32[122,4,256]{2,0,1:T(8,128)}, u32[]{:S(2)}, u32[]{:S(2)}) collective-permute-start(f32[122,4,256]{2,0,1:T(8,128)S(1)} %pad_maximum_fusion), channel_id=1, source_target_pairs={{0,16},{16,0},{32,48},{48,32},{1,17},{17,1},{33,49},{49,33},{2,18}... | collective-permute-start | bytes 1499144 | tf_op jit(solution)/shard_map/ppermute | solution.py:88
  17.1 3.8 %collective-permute-start.1 = (f32[122,4,256]{2,0,1:T(8,128)S(1)}, f32[122,4,256]{2,0,1:T(8,128)S(1)}, u32[]{:S(2)}, u32[]{:S(2)}) collective-permute-start(f32[122,4,256]{2,0,1:T(8,128)S(1)} %pad_maximum_fusion), channel_id=1, source_target_pairs={{0,32},{16,48},{32,0},{48,16},{1,33},{17,49},{33,1},{49,17},{2,34}... | collective-permute-start | bytes 1499144 | tf_op jit(solution)/shard_map/ppermute | solution.py:88
  20.9 2.0 %collective-permute-start.2 = (f32[122,4,256]{2,0,1:T(8,128)S(1)}, f32[122,4,256]{2,0,1:T(8,128)S(1)}, u32[]{:S(2)}, u32[]{:S(2)}) collective-permute-start(f32[122,4,256]{2,0,1:T(8,128)S(1)} %pad_maximum_fusion), channel_id=1, source_target_pairs={{0,48},{16,32},{32,16},{48,0},{1,49},{17,33},{33,17},{49,1},{2,50}... | collective-permute-start | bytes 1499144 | tf_op jit(solution)/shard_map/ppermute | solution.py:88
  22.9 0.0 copy-done.3
  22.9 0.4 fusion.23
  23.3 0.1 constant_dynamic-slice_fusion
  23.4 3.4 %collective-permute-start.3 = (f32[122,4,8]{0,2,1:T(8,128)S(1)}, f32[122,4,8]{0,2,1:T(8,128)S(1)}, u32[]{:S(2)}, u32[]{:S(2)}) collective-permute-start(f32[122,4,8]{0,2,1:T(8,128)S(1)} %bitcast.29), channel_id=1, source_target_pairs={{0,16},{16,0},{32,48},{48,32},{1,17},{17,1},{33,49},{49,33},{2,18}... | collective-permute-start | bytes 46856 | tf_op jit(solution)/shard_map/ppermute | solution.py:88
  26.8 3.8 %collective-permute-start.4 = (f32[122,4,8]{0,2,1:T(8,128)S(1)}, f32[122,4,8]{0,2,1:T(8,128)S(1)}, u32[]{:S(2)}, u32[]{:S(2)}) collective-permute-start(f32[122,4,8]{0,2,1:T(8,128)S(1)} %bitcast.28), channel_id=1, source_target_pairs={{0,32},{16,48},{32,0},{48,16},{1,33},{17,49},{33,1},{49,17},{2,34}... | collective-permute-start | bytes 46856 | tf_op jit(solution)/shard_map/ppermute | solution.py:88
  30.7 0.0 collective-permute-done.3
  30.7 3.6 %collective-permute-start.5 = (f32[122,4,8]{0,2,1:T(8,128)S(1)}, f32[122,4,8]{0,2,1:T(8,128)S(1)}, u32[]{:S(2)}, u32[]{:S(2)}) collective-permute-start(f32[122,4,8]{0,2,1:T(8,128)S(1)} %bitcast.27), channel_id=1, source_target_pairs={{0,48},{16,32},{32,16},{48,0},{1,49},{17,33},{33,17},{49,1},{2,50}... | collective-permute-start | bytes 46856 | tf_op jit(solution)/shard_map/ppermute | solution.py:88
  34.3 10.0 %collective-permute-done.4 = f32[122,4,8]{0,2,1:T(8,128)S(1)} collective-permute-done((f32[122,4,8]{0,2,1:T(8,128)S(1)}, f32[122,4,8]{0,2,1:T(8,128)S(1)}, u32[]{:S(2)}, u32[]{:S(2)}) %collective-permute-start.4) | collective-permute-done | bytes 15648 | tf_op jit(solution)/shard_map/ppermute | solution.py:88
  44.3 0.2 collective-permute-done.5
  44.4 0.0 collective-permute-done
  44.4 0.0 collective-permute-done.1
  44.4 0.0 copy-start
  44.4 0.0 collective-permute-done.2
  44.5 0.8 copy-done
  45.3 0.3 copy.14
  45.6 0.0 copy-start.1
  45.6 2.1 %collective-permute-start.6 = (f32[122,16,8]{1,2,0:T(8,128)S(1)}, f32[122,16,8]{1,2,0:T(8,128)S(1)}, u32[]{:S(2)}, u32[]{:S(2)}) collective-permute-start(f32[122,16,8]{1,2,0:T(8,128)S(1)} %copy.14), channel_id=1, source_target_pairs={{0,1},{1,0},{2,3},{3,2},{4,5},{5,4},{6,7},{7,6},{8,9},{9,8},{10,11... | collective-permute-start | bytes 187400 | tf_op jit(solution)/shard_map/ppermute | solution.py:56
  47.6 1.1 constant_dynamic-update-slice_fusion.2
  48.7 0.8 collective-permute-done.6
  49.5 0.1 add.103
  49.5 3.2 %collective-permute-start.7 = (f32[122,16,8]{1,2,0:T(8,128)S(1)}, f32[122,16,8]{1,2,0:T(8,128)S(1)}, u32[]{:S(2)}, u32[]{:S(2)}) collective-permute-start(f32[122,16,8]{1,2,0:T(8,128)S(1)} %add.103), channel_id=1, source_target_pairs={{0,2},{1,3},{2,0},{3,1},{4,6},{5,7},{6,4},{7,5},{8,10},{9,11},{10,... | collective-permute-start | bytes 187400 | tf_op jit(solution)/shard_map/ppermute | solution.py:56
  52.7 0.0 copy-done.1
  52.8 0.0 copy-start.2
  52.8 12.1 %collective-permute-done.7 = f32[122,16,8]{1,2,0:T(8,128)S(1)} collective-permute-done((f32[122,16,8]{1,2,0:T(8,128)S(1)}, f32[122,16,8]{1,2,0:T(8,128)S(1)}, u32[]{:S(2)}, u32[]{:S(2)}) %collective-permute-start.7) | collective-permute-done | bytes 62496 | tf_op jit(solution)/shard_map/ppermute | solution.py:56
  64.9 0.1 add.104
  64.9 2.3 %collective-permute-start.8 = (f32[122,16,8]{1,2,0:T(8,128)S(1)}, f32[122,16,8]{1,2,0:T(8,128)S(1)}, u32[]{:S(2)}, u32[]{:S(2)}) collective-permute-start(f32[122,16,8]{1,2,0:T(8,128)S(1)} %add.104), channel_id=1, source_target_pairs={{0,4},{1,5},{2,6},{3,7},{4,0},{5,1},{6,2},{7,3},{8,12},{9,13},{10,... | collective-permute-start | bytes 187400 | tf_op jit(solution)/shard_map/ppermute | solution.py:56
  67.2 13.7 %collective-permute-done.8 = f32[122,16,8]{1,2,0:T(8,128)S(1)} collective-permute-done((f32[122,16,8]{1,2,0:T(8,128)S(1)}, f32[122,16,8]{1,2,0:T(8,128)S(1)}, u32[]{:S(2)}, u32[]{:S(2)}) %collective-permute-start.8) | collective-permute-done | bytes 62496 | tf_op jit(solution)/shard_map/ppermute | solution.py:56
  80.9 0.1 add.105
  81.0 4.9 %collective-permute-start.9 = (f32[122,16,8]{1,2,0:T(8,128)S(1)}, f32[122,16,8]{1,2,0:T(8,128)S(1)}, u32[]{:S(2)}, u32[]{:S(2)}) collective-permute-start(f32[122,16,8]{1,2,0:T(8,128)S(1)} %add.105), channel_id=1, source_target_pairs={{0,8},{1,9},{2,10},{3,11},{4,12},{5,13},{6,14},{7,15},{8,0},{9,1},... | collective-permute-start | bytes 187400 | tf_op jit(solution)/shard_map/ppermute | solution.py:56
  85.9 0.0 copy-done.2
  85.9 0.2 slice_select_fusion
  86.1 0.1 slice.34
  86.2 9.9 %collective-permute-done.9 = f32[122,16,8]{1,2,0:T(8,128)S(1)} collective-permute-done((f32[122,16,8]{1,2,0:T(8,128)S(1)}, f32[122,16,8]{1,2,0:T(8,128)S(1)}, u32[]{:S(2)}, u32[]{:S(2)}) %collective-permute-start.9) | collective-permute-done | bytes 62496 | tf_op jit(solution)/shard_map/ppermute | solution.py:56
  96.1 0.1 add.106
  96.2 0.1 slice_select_fusion.6
  96.3 1.3 fusion.2
  97.6 1.3 fusion.5
  98.9 1.3 fusion
  100.2 1.3 fusion.1
  101.5 0.1 maximum_multiply_fusion
  101.6 1.3 copy.19
  102.9 0.0 reduce-scatter.2.cloned.1.call-update
  102.9 56.9 %reduce-scatter.2.cloned.1.call-done = f32[1,2,64,256]{3,2,1,0:T(8,128)} async-done(((f32[8,2,64,256]{3,2,1,0:T(8,128)}), f32[1,2,64,256]{3,2,1,0:T(8,128)}) %reduce-scatter.2.cloned.1.call-update) | async-done | bytes 131088 | tf_op jit(solution)/shard_map/reduce_scatter | solution.py:96
  159.8 1.6 copy.20
  (10 shorter events, 0.2 us)
Async XLA Ops:
  6.5 153.2 %reduce-scatter.2.cloned.1.call-start = ((), (), s32[]{:S(2)}) async-start(), calls=%async_computation.1 | async-start | bytes 1179648 | tf_op jit(solution)/shard_map/reduce_scatter | solution.py:96
  13.4 9.5 %copy-start.3 = (s32[32]{0:T(128)S(1)}, s32[32]{0:T(128)}, u32[]{:S(2)}) copy-start(s32[32]{0:T(128)} %param.5) | copy-start | bytes 388
  13.6 30.8 %collective-permute-start = (f32[122,4,256]{2,0,1:T(8,128)S(1)}, f32[122,4,256]{2,0,1:T(8,128)}, u32[]{:S(2)}, u32[]{:S(2)}) collective-permute-start(f32[122,4,256]{2,0,1:T(8,128)S(1)} %pad_maximum_fusion), channel_id=1, source_target_pairs={{0,16},{16,0},{32,48},{48,32},{1,17},{17,1},{33,49},{49,33},{2,18}... | collective-permute-start | bytes 1499144 | tf_op jit(solution)/shard_map/ppermute | solution.py:88
  17.1 27.4 %collective-permute-start.1 = (f32[122,4,256]{2,0,1:T(8,128)S(1)}, f32[122,4,256]{2,0,1:T(8,128)S(1)}, u32[]{:S(2)}, u32[]{:S(2)}) collective-permute-start(f32[122,4,256]{2,0,1:T(8,128)S(1)} %pad_maximum_fusion), channel_id=1, source_target_pairs={{0,32},{16,48},{32,0},{48,16},{1,33},{17,49},{33,1},{49,17},{2,34}... | collective-permute-start | bytes 1499144 | tf_op jit(solution)/shard_map/ppermute | solution.py:88
  20.9 23.6 %collective-permute-start.2 = (f32[122,4,256]{2,0,1:T(8,128)S(1)}, f32[122,4,256]{2,0,1:T(8,128)S(1)}, u32[]{:S(2)}, u32[]{:S(2)}) collective-permute-start(f32[122,4,256]{2,0,1:T(8,128)S(1)} %pad_maximum_fusion), channel_id=1, source_target_pairs={{0,48},{16,32},{32,16},{48,0},{1,49},{17,33},{33,17},{49,1},{2,50}... | collective-permute-start | bytes 1499144 | tf_op jit(solution)/shard_map/ppermute | solution.py:88
  23.4 7.2 %collective-permute-start.3 = (f32[122,4,8]{0,2,1:T(8,128)S(1)}, f32[122,4,8]{0,2,1:T(8,128)S(1)}, u32[]{:S(2)}, u32[]{:S(2)}) collective-permute-start(f32[122,4,8]{0,2,1:T(8,128)S(1)} %bitcast.29), channel_id=1, source_target_pairs={{0,16},{16,0},{32,48},{48,32},{1,17},{17,1},{33,49},{49,33},{2,18}... | collective-permute-start | bytes 46856 | tf_op jit(solution)/shard_map/ppermute | solution.py:88
  26.8 17.4 %collective-permute-start.4 = (f32[122,4,8]{0,2,1:T(8,128)S(1)}, f32[122,4,8]{0,2,1:T(8,128)S(1)}, u32[]{:S(2)}, u32[]{:S(2)}) collective-permute-start(f32[122,4,8]{0,2,1:T(8,128)S(1)} %bitcast.28), channel_id=1, source_target_pairs={{0,32},{16,48},{32,0},{48,16},{1,33},{17,49},{33,1},{49,17},{2,34}... | collective-permute-start | bytes 46856 | tf_op jit(solution)/shard_map/ppermute | solution.py:88
  30.7 13.8 %collective-permute-start.5 = (f32[122,4,8]{0,2,1:T(8,128)S(1)}, f32[122,4,8]{0,2,1:T(8,128)S(1)}, u32[]{:S(2)}, u32[]{:S(2)}) collective-permute-start(f32[122,4,8]{0,2,1:T(8,128)S(1)} %bitcast.27), channel_id=1, source_target_pairs={{0,48},{16,32},{32,16},{48,0},{1,49},{17,33},{33,17},{49,1},{2,50}... | collective-permute-start | bytes 46856 | tf_op jit(solution)/shard_map/ppermute | solution.py:88
  44.4 0.8 copy-start
  45.6 7.2 %copy-start.1 = (f32[122,4,256]{2,0,1:T(8,128)S(1)}, f32[122,4,256]{2,0,1:T(8,128)}, u32[]{:S(2)}) copy-start(f32[122,4,256]{2,0,1:T(8,128)} %copy-done) | copy-start | bytes 1499140
  45.6 3.9 %collective-permute-start.6 = (f32[122,16,8]{1,2,0:T(8,128)S(1)}, f32[122,16,8]{1,2,0:T(8,128)S(1)}, u32[]{:S(2)}, u32[]{:S(2)}) collective-permute-start(f32[122,16,8]{1,2,0:T(8,128)S(1)} %copy.14), channel_id=1, source_target_pairs={{0,1},{1,0},{2,3},{3,2},{4,5},{5,4},{6,7},{7,6},{8,9},{9,8},{10,11... | collective-permute-start | bytes 187400 | tf_op jit(solution)/shard_map/ppermute | solution.py:56
  49.5 15.3 %collective-permute-start.7 = (f32[122,16,8]{1,2,0:T(8,128)S(1)}, f32[122,16,8]{1,2,0:T(8,128)S(1)}, u32[]{:S(2)}, u32[]{:S(2)}) collective-permute-start(f32[122,16,8]{1,2,0:T(8,128)S(1)} %add.103), channel_id=1, source_target_pairs={{0,2},{1,3},{2,0},{3,1},{4,6},{5,7},{6,4},{7,5},{8,10},{9,11},{10,... | collective-permute-start | bytes 187400 | tf_op jit(solution)/shard_map/ppermute | solution.py:56
  52.8 33.2 %copy-start.2 = (pred[64]{0:T(512)(128)(4,1)S(1)}, pred[64]{0:T(512)(128)(4,1)}, u32[]{:S(2)}) copy-start(pred[64]{0:T(512)(128)(4,1)} %constant.46.clone.1) | copy-start | bytes 196
  64.9 16.0 %collective-permute-start.8 = (f32[122,16,8]{1,2,0:T(8,128)S(1)}, f32[122,16,8]{1,2,0:T(8,128)S(1)}, u32[]{:S(2)}, u32[]{:S(2)}) collective-permute-start(f32[122,16,8]{1,2,0:T(8,128)S(1)} %add.104), channel_id=1, source_target_pairs={{0,4},{1,5},{2,6},{3,7},{4,0},{5,1},{6,2},{7,3},{8,12},{9,13},{10,... | collective-permute-start | bytes 187400 | tf_op jit(solution)/shard_map/ppermute | solution.py:56
  81.0 15.1 %collective-permute-start.9 = (f32[122,16,8]{1,2,0:T(8,128)S(1)}, f32[122,16,8]{1,2,0:T(8,128)S(1)}, u32[]{:S(2)}, u32[]{:S(2)}) collective-permute-start(f32[122,16,8]{1,2,0:T(8,128)S(1)} %add.105), channel_id=1, source_target_pairs={{0,8},{1,9},{2,10},{3,11},{4,12},{5,13},{6,14},{7,15},{8,0},{9,1},... | collective-permute-start | bytes 187400 | tf_op jit(solution)/shard_map/ppermute | solution.py:56
Sparse Core Ops, SparseCore 0:
  103.0 56.6 reduce-scatter.1

commit v5 on v3

--- a/solution.py
+++ b/solution.py
@@ -49,13 +49,15 @@
     return jnp.stack([real_sum, imag_sum], axis=1) * factor
 
 
-def psum_recv(value, size):
+def psum_recv(value, size, passengers, hold_bit):
     bit = 1
     while bit < size:
+        if bit == hold_bit:
+            value, passengers = lax.optimization_barrier((value, passengers))
         pairs = [(i, i ^ bit) for i in range(size)]
         value = value + lax.ppermute(value, "recv", pairs)
         bit *= 2
-    return value
+    return value, passengers
 
 
 def on_device(traces, valid, src_idx):
@@ -76,11 +78,12 @@
     white = whiten_block(spec, valid_float)
     q = lax.axis_index("zlo") * lax.axis_size("xlo") + lax.axis_index("xlo")
     moves = [[(r, r ^ b) for r in range(width)] for b in range(1, width)]
-    white_all = jnp.concatenate(
-        [white] + [lax.ppermute(white, group, pairs) for pairs in moves], axis=1
+    white_parts = [lax.ppermute(white, group, pairs) for pairs in moves]
+    partial_value = jnp.einsum("ktc,sc->kts", white, onehot, precision=lax.Precision.HIGHEST)
+    panel, white_parts = psum_recv(
+        partial_value, lax.axis_size("recv"), white_parts, lax.axis_size("recv") // 2
     )
-    partial_value = jnp.einsum("ktc,sc->kts", white, onehot, precision=lax.Precision.HIGHEST)
-    panel = psum_recv(partial_value, lax.axis_size("recv"))
+    white_all = jnp.concatenate([white] + white_parts, axis=1)
     nsrc = panel.shape[2]
     panel = panel.reshape(panel.shape[0], panel.shape[1], nsrc // width, width)
     blocks = [lax.dynamic_index_in_dim(panel, q, axis=3, keepdims=False)]

time: 140 us -> 136 us (0.971)
  the two profiles are of different devices: /device:TPU:16 before, /device:TPU:2 now
where the time goes in v5:
time: 136 us
  waiting for transfers between devices  73.8 us (54%)
  starting transfers between devices  31.8 us (23%)
  between operations  13.7 us (10%)
  matrix products  9.22 us (7%)
  other arithmetic  3.85 us (3%)
  local copies, waits for them, and re-layouts  3.56 us (3%)
    reduce_scatter x1, waiting for transfers between devices, on_device(): out = lax.psum_scatter(totals, 'zhi', scatter_dimension=0, tiled=True)  55.5 us
    ppermute x4, waiting for transfers between devices, psum_recv(): value = value + lax.ppermute(value, 'recv', pairs)  14.9 us
    ppermute x3, starting transfers between devices, on_device(): white_parts = [lax.ppermute(white, group, pairs) for pairs in moves]  13.1 us
    ppermute x4, starting transfers between devices, psum_recv(): value = value + lax.ppermute(value, 'recv', pairs)  9.51 us
    ppermute x3, starting transfers between devices, on_device(): blocks.append(lax.ppermute(theirs, group, pairs))  9.21 us
    dot_general x1, matrix products, on_device(): lax.dot_general(basis, traces, (((1,), (2,)), ((), ())), preferred_elemen...  3.71 us
    ppermute x3, waiting for transfers between devices, on_device(): blocks.append(lax.ppermute(theirs, group, pairs))  3.4 us
  transfers between devices with their start and end apart: 11, of which 6 were waited for; matrix products, arithmetic and copies ran while one was open for 1% of the time, Pallas kernels for 0%

profile of v5, /device:TPU:2, one launch (start us, length us, event | category | flops | bytes accessed | tf_op | source)
XLA Modules:
  0.0 136.0 jit_solution(4650455820622755576)
XLA Ops:
  6.5 0.0 reduce-scatter.2.cloned.1.call-start
  6.5 0.7 convert_element_type.17
  7.2 2.4 %cosine_convert_fusion = (bf16[61,2048]{1,0:T(8,128)(2,1)S(1)}, bf16[61,2048]{1,0:T(8,128)(2,1)S(1)}) fusion(s32[61]{0:T(128)S(1)} %iota_add_fusion.1), kind=kLoop, calls=%fused_computation.25 | loop fusion | flops 2123776 | bytes 499956 | tf_op jit(solution)/shard_map/convert
  9.7 3.7 %fusion.11 = f32[122,4,256]{2,0,1:T(8,128)S(1)} fusion(bf16[4,256,2048]{2,1,0:T(8,128)(2,1)} %param.3, bf16[61,2048]{1,0:T(8,128)(2,1)S(1)} %get-tuple-element.20, bf16[61,2048]{1,0:T(8,128)(2,1)S(1)} %get-tuple-element.19), kind=kOutput, calls=%fused_computation.20 | convolution fusion | flops 512704512 | bytes 5193728 | tf_op jit(solution)/shard_map/dot_general | solution.py:75
  13.4 0.0 copy-start.1
  13.4 0.1 fusion.27
  13.5 0.1 slice_multiply_fusion.1
  13.6 3.8 %collective-permute-start.4 = (f32[122,4,256]{2,0,1:T(8,128)S(1)}, f32[122,4,256]{2,0,1:T(8,128)S(1)}, u32[]{:S(2)}, u32[]{:S(2)}) collective-permute-start(f32[122,4,256]{2,0,1:T(8,128)S(1)} %pad_maximum_fusion.1), channel_id=1, source_target_pairs={{0,32},{16,48},{32,0},{48,16},{1,33},{17,49},{33,1},{49,17},{2,34}... | collective-permute-start | bytes 1499144 | tf_op jit(solution)/shard_map/ppermute | solution.py:81
  17.5 5.9 %collective-permute-start.3 = (f32[122,4,256]{2,0,1:T(8,128)S(1)}, f32[122,4,256]{2,0,1:T(8,128)S(1)}, u32[]{:S(2)}, u32[]{:S(2)}) collective-permute-start(f32[122,4,256]{2,0,1:T(8,128)S(1)} %pad_maximum_fusion.1), channel_id=1, source_target_pairs={{0,16},{16,0},{32,48},{48,32},{1,17},{17,1},{33,49},{49,33},{2,18}... | collective-permute-start | bytes 1499144 | tf_op jit(solution)/shard_map/ppermute | solution.py:81
  23.4 3.4 %collective-permute-start.5 = (f32[122,4,256]{2,0,1:T(8,128)S(1)}, f32[122,4,256]{2,0,1:T(8,128)S(1)}, u32[]{:S(2)}, u32[]{:S(2)}) collective-permute-start(f32[122,4,256]{2,0,1:T(8,128)S(1)} %pad_maximum_fusion.1), channel_id=1, source_target_pairs={{0,48},{16,32},{32,16},{48,0},{1,49},{17,33},{33,17},{49,1},{2,50}... | collective-permute-start | bytes 1499144 | tf_op jit(solution)/shard_map/ppermute | solution.py:81
  26.8 0.0 copy-done.1
  26.8 0.4 fusion.19
  27.2 1.9 %collective-permute-start = (f32[122,4,32]{0,2,1:T(8,128)S(1)}, f32[122,4,32]{0,2,1:T(8,128)S(1)}, u32[]{:S(2)}, u32[]{:S(2)}) collective-permute-start(f32[122,4,32]{0,2,1:T(8,128)S(1)} %fusion.19), channel_id=1, source_target_pairs={{0,1},{1,0},{2,3},{3,2},{4,5},{5,4},{6,7},{7,6},{8,9},{9,8},{10,11... | collective-permute-start | bytes 187400 | tf_op jit(solution)/shard_map/ppermute | solution.py:58
  29.1 1.2 collective-permute-done
  30.4 1.9 %collective-permute-start.1 = (f32[122,4,32]{0,2,1:T(8,128)S(1)}, f32[122,4,32]{0,2,1:T(8,128)S(1)}, u32[]{:S(2)}, u32[]{:S(2)}) collective-permute-start(f32[122,4,32]{0,2,1:T(8,128)S(1)} %add.98), channel_id=1, source_target_pairs={{0,2},{1,3},{2,0},{3,1},{4,6},{5,7},{6,4},{7,5},{8,10},{9,11},{10,... | collective-permute-start | bytes 187400 | tf_op jit(solution)/shard_map/ppermute | solution.py:58
  32.3 4.2 %collective-permute-done.1 = f32[122,4,32]{0,2,1:T(8,128)S(1)} collective-permute-done((f32[122,4,32]{0,2,1:T(8,128)S(1)}, f32[122,4,32]{0,2,1:T(8,128)S(1)}, u32[]{:S(2)}, u32[]{:S(2)}) %collective-permute-start.1) | collective-permute-done | bytes 62496 | tf_op jit(solution)/shard_map/ppermute | solution.py:58
  36.6 1.9 %collective-permute-start.2 = (f32[122,4,32]{0,2,1:T(8,128)S(1)}, f32[122,4,32]{0,2,1:T(8,128)S(1)}, u32[]{:S(2)}, u32[]{:S(2)}) collective-permute-start(f32[122,4,32]{0,2,1:T(8,128)S(1)} %add.99), channel_id=1, source_target_pairs={{0,4},{1,5},{2,6},{3,7},{4,0},{5,1},{6,2},{7,3},{8,12},{9,13},{10,... | collective-permute-start | bytes 187400 | tf_op jit(solution)/shard_map/ppermute | solution.py:58
  38.5 5.7 %collective-permute-done.2 = f32[122,4,32]{0,2,1:T(8,128)S(1)} collective-permute-done((f32[122,4,32]{0,2,1:T(8,128)S(1)}, f32[122,4,32]{0,2,1:T(8,128)S(1)}, u32[]{:S(2)}, u32[]{:S(2)}) %collective-permute-start.2) | collective-permute-done | bytes 62496 | tf_op jit(solution)/shard_map/ppermute | solution.py:58
  44.2 0.0 copy-start
  44.2 0.0 collective-permute-done.4
  44.3 0.0 collective-permute-done.3
  44.3 0.0 collective-permute-done.5
  44.3 3.7 %collective-permute-start.6 = (f32[122,4,32]{0,2,1:T(8,128)S(1)}, f32[122,4,32]{0,2,1:T(8,128)S(1)}, u32[]{:S(2)}, u32[]{:S(2)}) collective-permute-start(f32[122,4,32]{0,2,1:T(8,128)S(1)} %add.100), channel_id=1, source_target_pairs={{0,8},{1,9},{2,10},{3,11},{4,12},{5,13},{6,14},{7,15},{8,0},{9,1},... | collective-permute-start | bytes 187400 | tf_op jit(solution)/shard_map/ppermute | solution.py:58
  48.0 0.2 pad_maximum_fusion
  48.2 3.7 %collective-permute-done.6 = f32[122,4,32]{0,2,1:T(8,128)S(1)} collective-permute-done((f32[122,4,32]{0,2,1:T(8,128)S(1)}, f32[122,4,32]{0,2,1:T(8,128)S(1)}, u32[]{:S(2)}, u32[]{:S(2)}) %collective-permute-start.6) | collective-permute-done | bytes 62496 | tf_op jit(solution)/shard_map/ppermute | solution.py:58
  52.0 0.1 constant_dynamic-slice_fusion.3
  52.0 3.4 %collective-permute-start.9 = (f32[122,4,8]{0,2,1:T(8,128)S(1)}, f32[122,4,8]{0,2,1:T(8,128)S(1)}, u32[]{:S(2)}, u32[]{:S(2)}) collective-permute-start(f32[122,4,8]{0,2,1:T(8,128)S(1)} %bitcast.29), channel_id=1, source_target_pairs={{0,48},{16,32},{32,16},{48,0},{1,49},{17,33},{33,17},{49,1},{2,50}... | collective-permute-start | bytes 46856 | tf_op jit(solution)/shard_map/ppermute | solution.py:92
  55.4 3.9 %collective-permute-start.8 = (f32[122,4,8]{0,2,1:T(8,128)S(1)}, f32[122,4,8]{0,2,1:T(8,128)S(1)}, u32[]{:S(2)}, u32[]{:S(2)}) collective-permute-start(f32[122,4,8]{0,2,1:T(8,128)S(1)} %bitcast.28), channel_id=1, source_target_pairs={{0,32},{16,48},{32,0},{48,16},{1,33},{17,49},{33,1},{49,17},{2,34}... | collective-permute-start | bytes 46856 | tf_op jit(solution)/shard_map/ppermute | solution.py:92
  59.3 1.9 %collective-permute-start.7 = (f32[122,4,8]{0,2,1:T(8,128)S(1)}, f32[122,4,8]{0,2,1:T(8,128)S(1)}, u32[]{:S(2)}, u32[]{:S(2)}) collective-permute-start(f32[122,4,8]{0,2,1:T(8,128)S(1)} %bitcast.27), channel_id=1, source_target_pairs={{0,16},{16,0},{32,48},{48,32},{1,17},{17,1},{33,49},{49,33},{2,18}... | collective-permute-start | bytes 46856 | tf_op jit(solution)/shard_map/ppermute | solution.py:92
  61.3 0.0 copy-done
  61.3 0.2 slice_select_fusion
  61.5 0.1 slice.34
  61.6 0.0 collective-permute-done.9
  61.6 0.0 collective-permute-done.8
  61.6 3.4 %collective-permute-done.7 = f32[122,4,8]{0,2,1:T(8,128)S(1)} collective-permute-done((f32[122,4,8]{0,2,1:T(8,128)S(1)}, f32[122,4,8]{0,2,1:T(8,128)S(1)}, u32[]{:S(2)}, u32[]{:S(2)}) %collective-permute-start.7) | collective-permute-done | bytes 15648 | tf_op jit(solution)/shard_map/ppermute | solution.py:92
  65.0 0.1 slice.35
  65.1 0.2 copy.22
  65.3 0.2 copy.14
  65.5 1.3 fusion.4
  66.7 1.3 fusion.6
  68.0 1.3 fusion.1
  69.3 1.3 fusion
  70.6 0.1 maximum_multiply_fusion
  70.7 1.3 copy.20
  72.0 0.0 reduce-scatter.2.cloned.1.call-update
  72.0 55.5 %reduce-scatter.2.cloned.1.call-done = f32[1,2,64,256]{3,2,1,0:T(8,128)} async-done(((f32[8,2,64,256]{3,2,1,0:T(8,128)}), f32[1,2,64,256]{3,2,1,0:T(8,128)}) %reduce-scatter.2.cloned.1.call-update) | async-done | bytes 131088 | tf_op jit(solution)/shard_map/reduce_scatter | solution.py:96
  127.5 1.6 %copy.21 = f32[1,2,61,256]{3,1,2,0:T(2,128)} copy(f32[1,2,61,256]{3,2,1,0:T(8,128)} %bitcast.25) | data formatting | bytes 249856 | tf_op jit(solution)/shard_map/slice | solution.py:97
  (11 shorter events, 0.1 us)
Async XLA Ops:
  6.5 120.9 %reduce-scatter.2.cloned.1.call-start = ((), (), s32[]{:S(2)}) async-start(), calls=%async_computation.1 | async-start | bytes 1179648 | tf_op jit(solution)/shard_map/reduce_scatter | solution.py:96
  13.4 13.4 %copy-start.1 = (s32[32]{0:T(128)S(1)}, s32[32]{0:T(128)}, u32[]{:S(2)}) copy-start(s32[32]{0:T(128)} %param.5) | copy-start | bytes 388
  13.6 30.6 %collective-permute-start.4 = (f32[122,4,256]{2,0,1:T(8,128)S(1)}, f32[122,4,256]{2,0,1:T(8,128)S(1)}, u32[]{:S(2)}, u32[]{:S(2)}) collective-permute-start(f32[122,4,256]{2,0,1:T(8,128)S(1)} %pad_maximum_fusion.1), channel_id=1, source_target_pairs={{0,32},{16,48},{32,0},{48,16},{1,33},{17,49},{33,1},{49,17},{2,34}... | collective-permute-start | bytes 1499144 | tf_op jit(solution)/shard_map/ppermute | solution.py:81
  17.5 26.8 %collective-permute-start.3 = (f32[122,4,256]{2,0,1:T(8,128)S(1)}, f32[122,4,256]{2,0,1:T(8,128)S(1)}, u32[]{:S(2)}, u32[]{:S(2)}) collective-permute-start(f32[122,4,256]{2,0,1:T(8,128)S(1)} %pad_maximum_fusion.1), channel_id=1, source_target_pairs={{0,16},{16,0},{32,48},{48,32},{1,17},{17,1},{33,49},{49,33},{2,18}... | collective-permute-start | bytes 1499144 | tf_op jit(solution)/shard_map/ppermute | solution.py:81
  23.4 20.9 %collective-permute-start.5 = (f32[122,4,256]{2,0,1:T(8,128)S(1)}, f32[122,4,256]{2,0,1:T(8,128)S(1)}, u32[]{:S(2)}, u32[]{:S(2)}) collective-permute-start(f32[122,4,256]{2,0,1:T(8,128)S(1)} %pad_maximum_fusion.1), channel_id=1, source_target_pairs={{0,48},{16,32},{32,16},{48,0},{1,49},{17,33},{33,17},{49,1},{2,50}... | collective-permute-start | bytes 1499144 | tf_op jit(solution)/shard_map/ppermute | solution.py:81
  27.2 3.1 %collective-permute-start = (f32[122,4,32]{0,2,1:T(8,128)S(1)}, f32[122,4,32]{0,2,1:T(8,128)S(1)}, u32[]{:S(2)}, u32[]{:S(2)}) collective-permute-start(f32[122,4,32]{0,2,1:T(8,128)S(1)} %fusion.19), channel_id=1, source_target_pairs={{0,1},{1,0},{2,3},{3,2},{4,5},{5,4},{6,7},{7,6},{8,9},{9,8},{10,11... | collective-permute-start | bytes 187400 | tf_op jit(solution)/shard_map/ppermute | solution.py:58
  30.4 6.2 %collective-permute-start.1 = (f32[122,4,32]{0,2,1:T(8,128)S(1)}, f32[122,4,32]{0,2,1:T(8,128)S(1)}, u32[]{:S(2)}, u32[]{:S(2)}) collective-permute-start(f32[122,4,32]{0,2,1:T(8,128)S(1)} %add.98), channel_id=1, source_target_pairs={{0,2},{1,3},{2,0},{3,1},{4,6},{5,7},{6,4},{7,5},{8,10},{9,11},{10,... | collective-permute-start | bytes 187400 | tf_op jit(solution)/shard_map/ppermute | solution.py:58
  36.6 7.7 %collective-permute-start.2 = (f32[122,4,32]{0,2,1:T(8,128)S(1)}, f32[122,4,32]{0,2,1:T(8,128)S(1)}, u32[]{:S(2)}, u32[]{:S(2)}) collective-permute-start(f32[122,4,32]{0,2,1:T(8,128)S(1)} %add.99), channel_id=1, source_target_pairs={{0,4},{1,5},{2,6},{3,7},{4,0},{5,1},{6,2},{7,3},{8,12},{9,13},{10,... | collective-permute-start | bytes 187400 | tf_op jit(solution)/shard_map/ppermute | solution.py:58
  44.2 17.0 %copy-start = (pred[64]{0:T(512)(128)(4,1)S(1)}, pred[64]{0:T(512)(128)(4,1)}, u32[]{:S(2)}) copy-start(pred[64]{0:T(512)(128)(4,1)} %constant.46.clone.1) | copy-start | bytes 196
  44.3 7.7 %collective-permute-start.6 = (f32[122,4,32]{0,2,1:T(8,128)S(1)}, f32[122,4,32]{0,2,1:T(8,128)S(1)}, u32[]{:S(2)}, u32[]{:S(2)}) collective-permute-start(f32[122,4,32]{0,2,1:T(8,128)S(1)} %add.100), channel_id=1, source_target_pairs={{0,8},{1,9},{2,10},{3,11},{4,12},{5,13},{6,14},{7,15},{8,0},{9,1},... | collective-permute-start | bytes 187400 | tf_op jit(solution)/shard_map/ppermute | solution.py:58
  52.0 9.5 %collective-permute-start.9 = (f32[122,4,8]{0,2,1:T(8,128)S(1)}, f32[122,4,8]{0,2,1:T(8,128)S(1)}, u32[]{:S(2)}, u32[]{:S(2)}) collective-permute-start(f32[122,4,8]{0,2,1:T(8,128)S(1)} %bitcast.29), channel_id=1, source_target_pairs={{0,48},{16,32},{32,16},{48,0},{1,49},{17,33},{33,17},{49,1},{2,50}... | collective-permute-start | bytes 46856 | tf_op jit(solution)/shard_map/ppermute | solution.py:92
  55.4 6.2 %collective-permute-start.8 = (f32[122,4,8]{0,2,1:T(8,128)S(1)}, f32[122,4,8]{0,2,1:T(8,128)S(1)}, u32[]{:S(2)}, u32[]{:S(2)}) collective-permute-start(f32[122,4,8]{0,2,1:T(8,128)S(1)} %bitcast.28), channel_id=1, source_target_pairs={{0,32},{16,48},{32,0},{48,16},{1,33},{17,49},{33,1},{49,17},{2,34}... | collective-permute-start | bytes 46856 | tf_op jit(solution)/shard_map/ppermute | solution.py:92
  59.3 5.6 %collective-permute-start.7 = (f32[122,4,8]{0,2,1:T(8,128)S(1)}, f32[122,4,8]{0,2,1:T(8,128)S(1)}, u32[]{:S(2)}, u32[]{:S(2)}) collective-permute-start(f32[122,4,8]{0,2,1:T(8,128)S(1)} %bitcast.27), channel_id=1, source_target_pairs={{0,16},{16,0},{32,48},{48,32},{1,17},{17,1},{33,49},{49,33},{2,18}... | collective-permute-start | bytes 46856 | tf_op jit(solution)/shard_map/ppermute | solution.py:92
Sparse Core Ops, SparseCore 0:
  72.1 55.2 reduce-scatter.1

commit v6 on v5

--- a/solution.py
+++ b/solution.py
@@ -14,11 +14,12 @@
 
 
 def basis_table():
-    sample_ids = jnp.arange(NS, dtype=jnp.int32)
-    bin_ids = BIN0 + jnp.arange(NB, dtype=jnp.int32)
-    phase_ids = bin_ids[:, None] * sample_ids[None, :] % NS
-    angle = 2.0 * math.pi / NS * phase_ids.astype(jnp.float32)
-    return jnp.concatenate([jnp.cos(angle), -jnp.sin(angle)], axis=0).astype(jnp.bfloat16)
+    sample_ids = np.arange(NS, dtype=np.int64)
+    bin_ids = BIN0 + np.arange(NB, dtype=np.int64)
+    phase_ids = (bin_ids[:, None] * sample_ids[None, :] % NS).astype(np.float32)
+    angle = (np.float32(2.0 * math.pi / NS) * phase_ids).astype(np.float64)
+    table = np.concatenate([np.cos(angle), -np.sin(angle)], axis=0).astype(np.float32)
+    return jnp.asarray(table.astype(jnp.bfloat16))
 
 
 def whiten_block(spec, valid_float):

time: 136 us -> 134 us (0.985)
  the two profiles are of different devices: /device:TPU:2 before, /device:TPU:64 now
where the time goes in v6:
time: 134 us
  waiting for transfers between devices  71.6 us (53%)
  starting transfers between devices  33.9 us (25%)
  between operations  13.7 us (10%)
  matrix products  9.38 us (7%)
  local copies, waits for them, and re-layouts  3.55 us (3%)
  other arithmetic  1.42 us (1%)
    reduce_scatter x1, waiting for transfers between devices, on_device(): out = lax.psum_scatter(totals, 'zhi', scatter_dimension=0, tiled=True)  56.1 us
    ppermute x4, starting transfers between devices, psum_recv(): value = value + lax.ppermute(value, 'recv', pairs)  15.4 us
    ppermute x3, starting transfers between devices, on_device(): blocks.append(lax.ppermute(theirs, group, pairs))  9.21 us
    ppermute x3, starting transfers between devices, on_device(): white_parts = [lax.ppermute(white, group, pairs) for pairs in moves]  9.21 us
    ppermute x4, waiting for transfers between devices, psum_recv(): value = value + lax.ppermute(value, 'recv', pairs)  8.95 us
    dot_general x1, matrix products, on_device(): lax.dot_general(basis, traces, (((1,), (2,)), ((), ())), preferred_elemen...  3.87 us
    ppermute x3, waiting for transfers between devices, on_device(): white_parts = [lax.ppermute(white, group, pairs) for pairs in moves]  3.64 us
    ppermute x3, waiting for transfers between devices, on_device(): blocks.append(lax.ppermute(theirs, group, pairs))  2.88 us
  transfers between devices with their start and end apart: 11, of which 7 were waited for; matrix products, arithmetic and copies ran while one was open for 1% of the time, Pallas kernels for 0%

profile of v6, /device:TPU:64, one launch (start us, length us, event | category | flops | bytes accessed | tf_op | source)
XLA Modules:
  0.0 133.5 jit_solution(10466947785900946161)
XLA Ops:
  6.5 0.0 reduce-scatter.2.cloned.1.call-start
  6.5 0.7 convert_element_type.10
  7.2 3.9 %fusion.18 = f32[122,4,256]{2,0,1:T(8,128)S(1)} fusion(bf16[122,2048,1]{1,0,2:T(8,128)(2,1)} %constant.56, bf16[4,256,2048]{2,1,0:T(8,128)(2,1)} %param.4), kind=kOutput, calls=%fused_computation.36 | convolution fusion | flops 511705088 | bytes 5193728 | tf_op jit(solution)/shard_map/dot_general | solution.py:76
  11.1 0.0 copy-start.1
  11.1 0.1 fusion.17
  11.2 0.1 slice_multiply_fusion.1
  11.4 3.8 %collective-permute-start.4 = (f32[122,4,256]{2,0,1:T(8,128)S(1)}, f32[122,4,256]{2,0,1:T(8,128)S(1)}, u32[]{:S(2)}, u32[]{:S(2)}) collective-permute-start(f32[122,4,256]{2,0,1:T(8,128)S(1)} %pad_maximum_fusion.1), channel_id=1, source_target_pairs={{0,32},{16,48},{32,0},{48,16},{1,33},{17,49},{33,1},{49,17},{2,34}... | collective-permute-start | bytes 1499144 | tf_op jit(solution)/shard_map/ppermute | solution.py:82
  15.2 3.4 %collective-permute-start.3 = (f32[122,4,256]{2,0,1:T(8,128)S(1)}, f32[122,4,256]{2,0,1:T(8,128)S(1)}, u32[]{:S(2)}, u32[]{:S(2)}) collective-permute-start(f32[122,4,256]{2,0,1:T(8,128)S(1)} %pad_maximum_fusion.1), channel_id=1, source_target_pairs={{0,16},{16,0},{32,48},{48,32},{1,17},{17,1},{33,49},{49,33},{2,18}... | collective-permute-start | bytes 1499144 | tf_op jit(solution)/shard_map/ppermute | solution.py:82
  18.6 2.0 %collective-permute-start.5 = (f32[122,4,256]{2,0,1:T(8,128)S(1)}, f32[122,4,256]{2,0,1:T(8,128)S(1)}, u32[]{:S(2)}, u32[]{:S(2)}) collective-permute-start(f32[122,4,256]{2,0,1:T(8,128)S(1)} %pad_maximum_fusion.1), channel_id=1, source_target_pairs={{0,48},{16,32},{32,16},{48,0},{1,49},{17,33},{33,17},{49,1},{2,50}... | collective-permute-start | bytes 1499144 | tf_op jit(solution)/shard_map/ppermute | solution.py:82
  20.6 0.0 copy-done.1
  20.6 0.4 fusion.10
  21.0 1.9 %collective-permute-start = (f32[122,4,32]{0,2,1:T(8,128)S(1)}, f32[122,4,32]{0,2,1:T(8,128)S(1)}, u32[]{:S(2)}, u32[]{:S(2)}) collective-permute-start(f32[122,4,32]{0,2,1:T(8,128)S(1)} %fusion.10), channel_id=1, source_target_pairs={{0,1},{1,0},{2,3},{3,2},{4,5},{5,4},{6,7},{7,6},{8,9},{9,8},{10,11... | collective-permute-start | bytes 187400 | tf_op jit(solution)/shard_map/ppermute | solution.py:59
  23.0 1.2 collective-permute-done
  24.2 3.5 %collective-permute-start.1 = (f32[122,4,32]{0,2,1:T(8,128)S(1)}, f32[122,4,32]{0,2,1:T(8,128)S(1)}, u32[]{:S(2)}, u32[]{:S(2)}) collective-permute-start(f32[122,4,32]{0,2,1:T(8,128)S(1)} %add.75), channel_id=1, source_target_pairs={{0,2},{1,3},{2,0},{3,1},{4,6},{5,7},{6,4},{7,5},{8,10},{9,11},{10,... | collective-permute-start | bytes 187400 | tf_op jit(solution)/shard_map/ppermute | solution.py:59
  27.7 2.7 %collective-permute-done.1 = f32[122,4,32]{0,2,1:T(8,128)S(1)} collective-permute-done((f32[122,4,32]{0,2,1:T(8,128)S(1)}, f32[122,4,32]{0,2,1:T(8,128)S(1)}, u32[]{:S(2)}, u32[]{:S(2)}) %collective-permute-start.1) | collective-permute-done | bytes 62496 | tf_op jit(solution)/shard_map/ppermute | solution.py:59
  30.4 5.1 %collective-permute-start.2 = (f32[122,4,32]{0,2,1:T(8,128)S(1)}, f32[122,4,32]{0,2,1:T(8,128)S(1)}, u32[]{:S(2)}, u32[]{:S(2)}) collective-permute-start(f32[122,4,32]{0,2,1:T(8,128)S(1)} %add.76), channel_id=1, source_target_pairs={{0,4},{1,5},{2,6},{3,7},{4,0},{5,1},{6,2},{7,3},{8,12},{9,13},{10,... | collective-permute-start | bytes 187400 | tf_op jit(solution)/shard_map/ppermute | solution.py:59
  35.5 2.5 %collective-permute-done.2 = f32[122,4,32]{0,2,1:T(8,128)S(1)} collective-permute-done((f32[122,4,32]{0,2,1:T(8,128)S(1)}, f32[122,4,32]{0,2,1:T(8,128)S(1)}, u32[]{:S(2)}, u32[]{:S(2)}) %collective-permute-start.2) | collective-permute-done | bytes 62496 | tf_op jit(solution)/shard_map/ppermute | solution.py:59
  38.1 0.0 copy-start
  38.1 0.0 collective-permute-done.4
  38.1 3.6 %collective-permute-done.3 = f32[122,4,256]{2,0,1:T(8,128)S(1)} collective-permute-done((f32[122,4,256]{2,0,1:T(8,128)S(1)}, f32[122,4,256]{2,0,1:T(8,128)S(1)}, u32[]{:S(2)}, u32[]{:S(2)}) %collective-permute-start.3) | collective-permute-done | bytes 499744 | tf_op jit(solution)/shard_map/ppermute | solution.py:82
  41.7 0.0 collective-permute-done.5
  41.7 4.9 %collective-permute-start.6 = (f32[122,4,32]{0,2,1:T(8,128)S(1)}, f32[122,4,32]{0,2,1:T(8,128)S(1)}, u32[]{:S(2)}, u32[]{:S(2)}) collective-permute-start(f32[122,4,32]{0,2,1:T(8,128)S(1)} %add.77), channel_id=1, source_target_pairs={{0,8},{1,9},{2,10},{3,11},{4,12},{5,13},{6,14},{7,15},{8,0},{9,1},... | collective-permute-start | bytes 187400 | tf_op jit(solution)/shard_map/ppermute | solution.py:59
  46.6 0.2 pad_maximum_fusion
  46.8 2.5 %collective-permute-done.6 = f32[122,4,32]{0,2,1:T(8,128)S(1)} collective-permute-done((f32[122,4,32]{0,2,1:T(8,128)S(1)}, f32[122,4,32]{0,2,1:T(8,128)S(1)}, u32[]{:S(2)}, u32[]{:S(2)}) %collective-permute-start.6) | collective-permute-done | bytes 62496 | tf_op jit(solution)/shard_map/ppermute | solution.py:59
  49.4 0.1 constant_dynamic-slice_fusion.3
  49.5 3.1 %collective-permute-start.9 = (f32[122,4,8]{0,2,1:T(8,128)S(1)}, f32[122,4,8]{0,2,1:T(8,128)S(1)}, u32[]{:S(2)}, u32[]{:S(2)}) collective-permute-start(f32[122,4,8]{0,2,1:T(8,128)S(1)} %bitcast.28), channel_id=1, source_target_pairs={{0,48},{16,32},{32,16},{48,0},{1,49},{17,33},{33,17},{49,1},{2,50}... | collective-permute-start | bytes 46856 | tf_op jit(solution)/shard_map/ppermute | solution.py:93
  52.6 3.6 %collective-permute-start.8 = (f32[122,4,8]{0,2,1:T(8,128)S(1)}, f32[122,4,8]{0,2,1:T(8,128)S(1)}, u32[]{:S(2)}, u32[]{:S(2)}) collective-permute-start(f32[122,4,8]{0,2,1:T(8,128)S(1)} %bitcast.27), channel_id=1, source_target_pairs={{0,32},{16,48},{32,0},{48,16},{1,33},{17,49},{33,1},{49,17},{2,34}... | collective-permute-start | bytes 46856 | tf_op jit(solution)/shard_map/ppermute | solution.py:93
  56.2 2.4 %collective-permute-start.7 = (f32[122,4,8]{0,2,1:T(8,128)S(1)}, f32[122,4,8]{0,2,1:T(8,128)S(1)}, u32[]{:S(2)}, u32[]{:S(2)}) collective-permute-start(f32[122,4,8]{0,2,1:T(8,128)S(1)} %bitcast.26), channel_id=1, source_target_pairs={{0,16},{16,0},{32,48},{48,32},{1,17},{17,1},{33,49},{49,33},{2,18}... | collective-permute-start | bytes 46856 | tf_op jit(solution)/shard_map/ppermute | solution.py:93
  58.7 0.0 copy-done
  58.7 0.2 slice_select_fusion
  58.9 0.1 slice.34
  59.0 0.0 collective-permute-done.9
  59.0 0.0 collective-permute-done.8
  59.0 2.9 %collective-permute-done.7 = f32[122,4,8]{0,2,1:T(8,128)S(1)} collective-permute-done((f32[122,4,8]{0,2,1:T(8,128)S(1)}, f32[122,4,8]{0,2,1:T(8,128)S(1)}, u32[]{:S(2)}, u32[]{:S(2)}) %collective-permute-start.7) | collective-permute-done | bytes 15648 | tf_op jit(solution)/shard_map/ppermute | solution.py:93
  61.9 0.1 slice.35
  62.0 0.2 copy.23
  62.2 0.2 copy.15
  62.4 1.3 fusion.4
  63.6 1.3 fusion.6
  64.9 1.3 fusion.1
  66.2 1.3 fusion
  67.5 0.1 maximum_multiply_fusion
  67.6 1.3 copy.21
  68.9 0.0 reduce-scatter.2.cloned.1.call-update
  68.9 56.1 %reduce-scatter.2.cloned.1.call-done = f32[1,2,64,256]{3,2,1,0:T(8,128)} async-done(((f32[8,2,64,256]{3,2,1,0:T(8,128)}), f32[1,2,64,256]{3,2,1,0:T(8,128)}) %reduce-scatter.2.cloned.1.call-update) | async-done | bytes 131088 | tf_op jit(solution)/shard_map/reduce_scatter | solution.py:97
  125.0 1.6 %copy.22 = f32[1,2,61,256]{3,1,2,0:T(2,128)} copy(f32[1,2,61,256]{3,2,1,0:T(8,128)} %bitcast.24) | data formatting | bytes 249856 | tf_op jit(solution)/shard_map/slice | solution.py:98
  (10 shorter events, 0.1 us)
Async XLA Ops:
  6.5 118.5 %reduce-scatter.2.cloned.1.call-start = ((), (), s32[]{:S(2)}) async-start(), calls=%async_computation.1 | async-start | bytes 1179648 | tf_op jit(solution)/shard_map/reduce_scatter | solution.py:97
  11.1 9.5 %copy-start.1 = (s32[32]{0:T(128)S(1)}, s32[32]{0:T(128)}, u32[]{:S(2)}) copy-start(s32[32]{0:T(128)} %param.6) | copy-start | bytes 388
  11.4 26.7 %collective-permute-start.4 = (f32[122,4,256]{2,0,1:T(8,128)S(1)}, f32[122,4,256]{2,0,1:T(8,128)S(1)}, u32[]{:S(2)}, u32[]{:S(2)}) collective-permute-start(f32[122,4,256]{2,0,1:T(8,128)S(1)} %pad_maximum_fusion.1), channel_id=1, source_target_pairs={{0,32},{16,48},{32,0},{48,16},{1,33},{17,49},{33,1},{49,17},{2,34}... | collective-permute-start | bytes 1499144 | tf_op jit(solution)/shard_map/ppermute | solution.py:82
  15.2 26.5 %collective-permute-start.3 = (f32[122,4,256]{2,0,1:T(8,128)S(1)}, f32[122,4,256]{2,0,1:T(8,128)S(1)}, u32[]{:S(2)}, u32[]{:S(2)}) collective-permute-start(f32[122,4,256]{2,0,1:T(8,128)S(1)} %pad_maximum_fusion.1), channel_id=1, source_target_pairs={{0,16},{16,0},{32,48},{48,32},{1,17},{17,1},{33,49},{49,33},{2,18}... | collective-permute-start | bytes 1499144 | tf_op jit(solution)/shard_map/ppermute | solution.py:82
  18.6 23.1 %collective-permute-start.5 = (f32[122,4,256]{2,0,1:T(8,128)S(1)}, f32[122,4,256]{2,0,1:T(8,128)S(1)}, u32[]{:S(2)}, u32[]{:S(2)}) collective-permute-start(f32[122,4,256]{2,0,1:T(8,128)S(1)} %pad_maximum_fusion.1), channel_id=1, source_target_pairs={{0,48},{16,32},{32,16},{48,0},{1,49},{17,33},{33,17},{49,1},{2,50}... | collective-permute-start | bytes 1499144 | tf_op jit(solution)/shard_map/ppermute | solution.py:82
  21.0 3.1 %collective-permute-start = (f32[122,4,32]{0,2,1:T(8,128)S(1)}, f32[122,4,32]{0,2,1:T(8,128)S(1)}, u32[]{:S(2)}, u32[]{:S(2)}) collective-permute-start(f32[122,4,32]{0,2,1:T(8,128)S(1)} %fusion.10), channel_id=1, source_target_pairs={{0,1},{1,0},{2,3},{3,2},{4,5},{5,4},{6,7},{7,6},{8,9},{9,8},{10,11... | collective-permute-start | bytes 187400 | tf_op jit(solution)/shard_map/ppermute | solution.py:59
  24.2 6.2 %collective-permute-start.1 = (f32[122,4,32]{0,2,1:T(8,128)S(1)}, f32[122,4,32]{0,2,1:T(8,128)S(1)}, u32[]{:S(2)}, u32[]{:S(2)}) collective-permute-start(f32[122,4,32]{0,2,1:T(8,128)S(1)} %add.75), channel_id=1, source_target_pairs={{0,2},{1,3},{2,0},{3,1},{4,6},{5,7},{6,4},{7,5},{8,10},{9,11},{10,... | collective-permute-start | bytes 187400 | tf_op jit(solution)/shard_map/ppermute | solution.py:59
  30.4 7.7 %collective-permute-start.2 = (f32[122,4,32]{0,2,1:T(8,128)S(1)}, f32[122,4,32]{0,2,1:T(8,128)S(1)}, u32[]{:S(2)}, u32[]{:S(2)}) collective-permute-start(f32[122,4,32]{0,2,1:T(8,128)S(1)} %add.76), channel_id=1, source_target_pairs={{0,4},{1,5},{2,6},{3,7},{4,0},{5,1},{6,2},{7,3},{8,12},{9,13},{10,... | collective-permute-start | bytes 187400 | tf_op jit(solution)/shard_map/ppermute | solution.py:59
  38.1 20.6 %copy-start = (pred[64]{0:T(512)(128)(4,1)S(1)}, pred[64]{0:T(512)(128)(4,1)}, u32[]{:S(2)}) copy-start(pred[64]{0:T(512)(128)(4,1)} %constant.34.clone.1) | copy-start | bytes 196
  41.7 7.7 %collective-permute-start.6 = (f32[122,4,32]{0,2,1:T(8,128)S(1)}, f32[122,4,32]{0,2,1:T(8,128)S(1)}, u32[]{:S(2)}, u32[]{:S(2)}) collective-permute-start(f32[122,4,32]{0,2,1:T(8,128)S(1)} %add.77), channel_id=1, source_target_pairs={{0,8},{1,9},{2,10},{3,11},{4,12},{5,13},{6,14},{7,15},{8,0},{9,1},... | collective-permute-start | bytes 187400 | tf_op jit(solution)/shard_map/ppermute | solution.py:59
  49.5 9.5 %collective-permute-start.9 = (f32[122,4,8]{0,2,1:T(8,128)S(1)}, f32[122,4,8]{0,2,1:T(8,128)S(1)}, u32[]{:S(2)}, u32[]{:S(2)}) collective-permute-start(f32[122,4,8]{0,2,1:T(8,128)S(1)} %bitcast.28), channel_id=1, source_target_pairs={{0,48},{16,32},{32,16},{48,0},{1,49},{17,33},{33,17},{49,1},{2,50}... | collective-permute-start | bytes 46856 | tf_op jit(solution)/shard_map/ppermute | solution.py:93
  52.6 6.4 %collective-permute-start.8 = (f32[122,4,8]{0,2,1:T(8,128)S(1)}, f32[122,4,8]{0,2,1:T(8,128)S(1)}, u32[]{:S(2)}, u32[]{:S(2)}) collective-permute-start(f32[122,4,8]{0,2,1:T(8,128)S(1)} %bitcast.27), channel_id=1, source_target_pairs={{0,32},{16,48},{32,0},{48,16},{1,33},{17,49},{33,1},{49,17},{2,34}... | collective-permute-start | bytes 46856 | tf_op jit(solution)/shard_map/ppermute | solution.py:93
  56.2 5.6 %collective-permute-start.7 = (f32[122,4,8]{0,2,1:T(8,128)S(1)}, f32[122,4,8]{0,2,1:T(8,128)S(1)}, u32[]{:S(2)}, u32[]{:S(2)}) collective-permute-start(f32[122,4,8]{0,2,1:T(8,128)S(1)} %bitcast.26), channel_id=1, source_target_pairs={{0,16},{16,0},{32,48},{48,32},{1,17},{17,1},{33,49},{49,33},{2,18}... | collective-permute-start | bytes 46856 | tf_op jit(solution)/shard_map/ppermute | solution.py:93
Sparse Core Ops, SparseCore 0:
  69.0 55.9 reduce-scatter.1

commit v7 on v6

--- a/solution.py
+++ b/solution.py
@@ -50,15 +50,13 @@
     return jnp.stack([real_sum, imag_sum], axis=1) * factor
 
 
-def psum_recv(value, size, passengers, hold_bit):
+def psum_recv(value, size):
     bit = 1
     while bit < size:
-        if bit == hold_bit:
-            value, passengers = lax.optimization_barrier((value, passengers))
         pairs = [(i, i ^ bit) for i in range(size)]
         value = value + lax.ppermute(value, "recv", pairs)
         bit *= 2
-    return value, passengers
+    return value
 
 
 def on_device(traces, valid, src_idx):
@@ -79,19 +77,25 @@
     white = whiten_block(spec, valid_float)
     q = lax.axis_index("zlo") * lax.axis_size("xlo") + lax.axis_index("xlo")
     moves = [[(r, r ^ b) for r in range(width)] for b in range(1, width)]
-    white_parts = [lax.ppermute(white, group, pairs) for pairs in moves]
     partial_value = jnp.einsum("ktc,sc->kts", white, onehot, precision=lax.Precision.HIGHEST)
-    panel, white_parts = psum_recv(
-        partial_value, lax.axis_size("recv"), white_parts, lax.axis_size("recv") // 2
-    )
-    white_all = jnp.concatenate([white] + white_parts, axis=1)
-    nsrc = panel.shape[2]
-    panel = panel.reshape(panel.shape[0], panel.shape[1], nsrc // width, width)
-    blocks = [lax.dynamic_index_in_dim(panel, q, axis=3, keepdims=False)]
+    rows, segs, nsrc = partial_value.shape
+    partial_value = partial_value.reshape(rows, segs, nsrc // width, width)
+
+    def slot(member):
+        return lax.dynamic_index_in_dim(partial_value, member, axis=3, keepdims=False).reshape(rows, -1)
+
+    slot_width = segs * (nsrc // width)
+    white_parts = [white]
+    value_parts = [slot(q)]
     for b, pairs in zip(range(1, width), moves):
-        theirs = lax.dynamic_index_in_dim(panel, q ^ b, axis=3, keepdims=False)
-        blocks.append(lax.ppermute(theirs, group, pairs))
-    panel_own = jnp.concatenate(blocks, axis=1)
+        row = jnp.pad(slot(q ^ b), ((0, 0), (0, white.shape[2] - slot_width)))
+        message = jnp.concatenate([white, row[:, None, :]], axis=1)
+        got = lax.ppermute(message, group, pairs)
+        white_parts.append(got[:, :segs, :])
+        value_parts.append(got[:, segs, :slot_width])
+    white_all = jnp.concatenate(white_parts, axis=1)
+    panel = psum_recv(jnp.concatenate(value_parts, axis=1), lax.axis_size("recv"))
+    panel_own = panel.reshape(rows, width * segs, nsrc // width)
     factor = 1.0 / math.sqrt(total_segs)
     totals = cross_terms(panel_own, white_all, factor)
     out = lax.psum_scatter(totals, "zhi", scatter_dimension=0, tiled=True)

time: 134 us -> 147 us (1.097)
  the two profiles are of different devices: /device:TPU:64 before, /device:TPU:2 now
where the time goes in v7:
time: 147 us
  waiting for transfers between devices  84.8 us (58%)
  starting transfers between devices  27.4 us (19%)
  between operations  13.7 us (9%)
  local copies, waits for them, and re-layouts  9.96 us (7%)
  matrix products  9.39 us (6%)
  other arithmetic  1.68 us (1%)
    reduce_scatter x1, waiting for transfers between devices, on_device(): out = lax.psum_scatter(totals, 'zhi', scatter_dimension=0, tiled=True)  56.7 us
    ppermute x3, waiting for transfers between devices, on_device(): got = lax.ppermute(message, group, pairs)  20.9 us
    ppermute x4, starting transfers between devices, psum_recv(): value = value + lax.ppermute(value, 'recv', pairs)  14.2 us
    ppermute x3, starting transfers between devices, on_device(): got = lax.ppermute(message, group, pairs)  13.1 us
    ppermute x4, waiting for transfers between devices, psum_recv(): value = value + lax.ppermute(value, 'recv', pairs)  7.2 us
    dot_general x1, matrix products, on_device(): lax.dot_general(basis, traces, (((1,), (2,)), ((), ())), preferred_elemen...  3.88 us
    slice x3, local copies, waits for them, and re-layouts, on_device(): white_parts.append(got[:, :segs, :])  3.23 us
  transfers between devices with their start and end apart: 8, of which 7 were waited for; matrix products, arithmetic and copies ran while one was open for 4% of the time, Pallas kernels for 0%

profile of v7, /device:TPU:2, one launch (start us, length us, event | category | flops | bytes accessed | tf_op | source)
XLA Modules:
  0.0 146.9 jit_solution(8948369258044609042)
XLA Ops:
  6.5 0.0 reduce-scatter.2.cloned.1.call-start
  6.5 0.7 convert_element_type.14
  7.2 0.0 copy-start.1
  7.2 3.9 %fusion.27 = f32[122,4,256]{2,0,1:T(8,128)S(1)} fusion(bf16[122,2048,1]{1,0,2:T(8,128)(2,1)} %constant.63, bf16[4,256,2048]{2,1,0:T(8,128)(2,1)} %param.4), kind=kOutput, calls=%fused_computation.53 | convolution fusion | flops 511705088 | bytes 5193728 | tf_op jit(solution)/shard_map/dot_general | solution.py:74
  11.1 0.1 fusion.25
  11.2 0.1 slice_multiply_fusion.1
  11.3 0.0 copy-done.1
  11.3 0.4 fusion.8
  11.8 0.1 constant_dynamic-slice_fusion
  11.8 0.1 copy.38
  11.9 0.1 copy.36
  12.0 0.1 copy.34
  12.2 0.2 pad_maximum_fusion.1
  12.4 7.8 %collective-permute-start = (f32[122,5,256]{2,0,1:T(8,128)S(1)}, f32[122,5,256]{2,0,1:T(8,128)}, u32[]{:S(2)}, u32[]{:S(2)}) collective-permute-start(f32[122,5,256]{2,0,1:T(8,128)S(1)} %get-tuple-element.7), channel_id=1, source_target_pairs={{0,16},{16,0},{32,48},{48,32},{1,17},{17,1},{33,49},{49,33},{2,18}... | collective-permute-start | bytes 1873928 | tf_op jit(solution)/shard_map/ppermute | solution.py:93
  20.2 1.9 %collective-permute-start.1 = (f32[122,5,256]{2,0,1:T(8,128)S(1)}, f32[122,5,256]{2,0,1:T(8,128)}, u32[]{:S(2)}, u32[]{:S(2)}) collective-permute-start(f32[122,5,256]{2,0,1:T(8,128)S(1)} %get-tuple-element.8), channel_id=1, source_target_pairs={{0,32},{16,48},{32,0},{48,16},{1,33},{17,49},{33,1},{49,17},{2,34}... | collective-permute-start | bytes 1873928 | tf_op jit(solution)/shard_map/ppermute | solution.py:93
  22.2 3.4 %collective-permute-start.2 = (f32[122,5,256]{2,0,1:T(8,128)S(1)}, f32[122,5,256]{2,0,1:T(8,128)}, u32[]{:S(2)}, u32[]{:S(2)}) collective-permute-start(f32[122,5,256]{2,0,1:T(8,128)S(1)} %get-tuple-element.9), channel_id=1, source_target_pairs={{0,48},{16,32},{32,16},{48,0},{1,49},{17,33},{33,17},{49,1},{2,50}... | collective-permute-start | bytes 1873928 | tf_op jit(solution)/shard_map/ppermute | solution.py:93
  25.5 0.1 copy.40
  25.6 7.1 %collective-permute-done = f32[122,5,256]{2,0,1:T(8,128)} collective-permute-done((f32[122,5,256]{2,0,1:T(8,128)S(1)}, f32[122,5,256]{2,0,1:T(8,128)}, u32[]{:S(2)}, u32[]{:S(2)}) %collective-permute-start) | collective-permute-done | bytes 624672 | tf_op jit(solution)/shard_map/ppermute | solution.py:93
  32.8 0.8 slice_bitcast_fusion.2
  33.6 6.3 %collective-permute-done.1 = f32[122,5,256]{2,0,1:T(8,128)} collective-permute-done((f32[122,5,256]{2,0,1:T(8,128)S(1)}, f32[122,5,256]{2,0,1:T(8,128)}, u32[]{:S(2)}, u32[]{:S(2)}) %collective-permute-start.1) | collective-permute-done | bytes 624672 | tf_op jit(solution)/shard_map/ppermute | solution.py:93
  39.9 0.8 slice_bitcast_fusion.1
  40.7 7.5 %collective-permute-done.2 = f32[122,5,256]{2,0,1:T(8,128)} collective-permute-done((f32[122,5,256]{2,0,1:T(8,128)S(1)}, f32[122,5,256]{2,0,1:T(8,128)}, u32[]{:S(2)}, u32[]{:S(2)}) %collective-permute-start.2) | collective-permute-done | bytes 624672 | tf_op jit(solution)/shard_map/ppermute | solution.py:93
  48.2 0.8 slice_bitcast_fusion
  49.0 0.1 pad_maximum_fusion.5
  49.2 1.9 %collective-permute-start.3 = (f32[122,128]{1,0:T(8,128)S(1)}, f32[122,128]{1,0:T(8,128)S(1)}, u32[]{:S(2)}, u32[]{:S(2)}) collective-permute-start(f32[122,128]{1,0:T(8,128)S(1)} %pad_maximum_fusion.5), channel_id=1, source_target_pairs={{0,1},{1,0},{2,3},{3,2},{4,5},{5,4},{6,7},{7,6},{8,9},{9,8},{10,11... | collective-permute-start | bytes 187400 | tf_op jit(solution)/shard_map/ppermute | solution.py:57
  51.1 1.2 collective-permute-done.3
  52.3 3.5 %collective-permute-start.4 = (f32[122,128]{1,0:T(8,128)S(1)}, f32[122,128]{1,0:T(8,128)S(1)}, u32[]{:S(2)}, u32[]{:S(2)}) collective-permute-start(f32[122,128]{1,0:T(8,128)S(1)} %add.88), channel_id=1, source_target_pairs={{0,2},{1,3},{2,0},{3,1},{4,6},{5,7},{6,4},{7,5},{8,10},{9,11},{10,... | collective-permute-start | bytes 187400 | tf_op jit(solution)/shard_map/ppermute | solution.py:57
  55.8 1.1 slice.63
  56.9 1.1 slice.64
  58.0 1.1 slice.65
  59.1 0.0 collective-permute-done.4
  59.1 0.0 copy-start
  59.1 4.8 %collective-permute-start.5 = (f32[122,128]{1,0:T(8,128)S(1)}, f32[122,128]{1,0:T(8,128)S(1)}, u32[]{:S(2)}, u32[]{:S(2)}) collective-permute-start(f32[122,128]{1,0:T(8,128)S(1)} %add.89), channel_id=1, source_target_pairs={{0,4},{1,5},{2,6},{3,7},{4,0},{5,1},{6,2},{7,3},{8,12},{9,13},{10,... | collective-permute-start | bytes 187400 | tf_op jit(solution)/shard_map/ppermute | solution.py:57
  63.9 0.2 pad_maximum_fusion
  64.1 2.6 %collective-permute-done.5 = f32[122,128]{1,0:T(8,128)S(1)} collective-permute-done((f32[122,128]{1,0:T(8,128)S(1)}, f32[122,128]{1,0:T(8,128)S(1)}, u32[]{:S(2)}, u32[]{:S(2)}) %collective-permute-start.5) | collective-permute-done | bytes 62496 | tf_op jit(solution)/shard_map/ppermute | solution.py:57
  66.8 4.0 %collective-permute-start.6 = (f32[122,128]{1,0:T(8,128)S(1)}, f32[122,128]{1,0:T(8,128)S(1)}, u32[]{:S(2)}, u32[]{:S(2)}) collective-permute-start(f32[122,128]{1,0:T(8,128)S(1)} %add.90), channel_id=1, source_target_pairs={{0,8},{1,9},{2,10},{3,11},{4,12},{5,13},{6,14},{7,15},{8,0},{9,1},... | collective-permute-start | bytes 187400 | tf_op jit(solution)/shard_map/ppermute | solution.py:57
  70.8 0.0 copy-done
  70.8 0.2 slice_select_fusion
  71.0 0.1 slice.71
  71.1 3.3 %collective-permute-done.6 = f32[122,128]{1,0:T(8,128)S(1)} collective-permute-done((f32[122,128]{1,0:T(8,128)S(1)}, f32[122,128]{1,0:T(8,128)S(1)}, u32[]{:S(2)}, u32[]{:S(2)}) %collective-permute-start.6) | collective-permute-done | bytes 62496 | tf_op jit(solution)/shard_map/ppermute | solution.py:57
  74.5 0.1 copy.41
  74.6 0.1 copy.44
  74.7 0.2 copy.45
  74.9 0.2 copy.42
  75.1 1.3 fusion.2
  76.4 1.3 fusion.4
  77.7 1.3 fusion.1
  79.0 1.3 fusion
  80.2 0.1 maximum_multiply_fusion
  80.3 1.3 copy.49
  81.6 0.0 reduce-scatter.2.cloned.1.call-update
  81.7 56.7 %reduce-scatter.2.cloned.1.call-done = f32[1,2,64,256]{3,2,1,0:T(8,128)} async-done(((f32[8,2,64,256]{3,2,1,0:T(8,128)}), f32[1,2,64,256]{3,2,1,0:T(8,128)}) %reduce-scatter.2.cloned.1.call-update) | async-done | bytes 131088 | tf_op jit(solution)/shard_map/reduce_scatter | solution.py:101
  138.4 1.6 %copy.50 = f32[1,2,61,256]{3,1,2,0:T(2,128)} copy(f32[1,2,61,256]{3,2,1,0:T(8,128)} %bitcast.49) | data formatting | bytes 249856 | tf_op jit(solution)/shard_map/slice | solution.py:102
  (11 shorter events, 0.1 us)
Async XLA Ops:
  6.5 131.8 %reduce-scatter.2.cloned.1.call-start = ((), (), s32[]{:S(2)}) async-start(), calls=%async_computation.1 | async-start | bytes 1179648 | tf_op jit(solution)/shard_map/reduce_scatter | solution.py:101
  7.2 4.1 %copy-start.1 = (s32[32]{0:T(128)S(1)}, s32[32]{0:T(128)}, u32[]{:S(2)}) copy-start(s32[32]{0:T(128)} %param.6) | copy-start | bytes 388
  12.4 20.4 %collective-permute-start = (f32[122,5,256]{2,0,1:T(8,128)S(1)}, f32[122,5,256]{2,0,1:T(8,128)}, u32[]{:S(2)}, u32[]{:S(2)}) collective-permute-start(f32[122,5,256]{2,0,1:T(8,128)S(1)} %get-tuple-element.7), channel_id=1, source_target_pairs={{0,16},{16,0},{32,48},{48,32},{1,17},{17,1},{33,49},{49,33},{2,18}... | collective-permute-start | bytes 1873928 | tf_op jit(solution)/shard_map/ppermute | solution.py:93
  20.2 19.7 %collective-permute-start.1 = (f32[122,5,256]{2,0,1:T(8,128)S(1)}, f32[122,5,256]{2,0,1:T(8,128)}, u32[]{:S(2)}, u32[]{:S(2)}) collective-permute-start(f32[122,5,256]{2,0,1:T(8,128)S(1)} %get-tuple-element.8), channel_id=1, source_target_pairs={{0,32},{16,48},{32,0},{48,16},{1,33},{17,49},{33,1},{49,17},{2,34}... | collective-permute-start | bytes 1873928 | tf_op jit(solution)/shard_map/ppermute | solution.py:93
  22.2 26.0 %collective-permute-start.2 = (f32[122,5,256]{2,0,1:T(8,128)S(1)}, f32[122,5,256]{2,0,1:T(8,128)}, u32[]{:S(2)}, u32[]{:S(2)}) collective-permute-start(f32[122,5,256]{2,0,1:T(8,128)S(1)} %get-tuple-element.9), channel_id=1, source_target_pairs={{0,48},{16,32},{32,16},{48,0},{1,49},{17,33},{33,17},{49,1},{2,50}... | collective-permute-start | bytes 1873928 | tf_op jit(solution)/shard_map/ppermute | solution.py:93
  49.2 3.1 %collective-permute-start.3 = (f32[122,128]{1,0:T(8,128)S(1)}, f32[122,128]{1,0:T(8,128)S(1)}, u32[]{:S(2)}, u32[]{:S(2)}) collective-permute-start(f32[122,128]{1,0:T(8,128)S(1)} %pad_maximum_fusion.5), channel_id=1, source_target_pairs={{0,1},{1,0},{2,3},{3,2},{4,5},{5,4},{6,7},{7,6},{8,9},{9,8},{10,11... | collective-permute-start | bytes 187400 | tf_op jit(solution)/shard_map/ppermute | solution.py:57
  52.3 6.7 %collective-permute-start.4 = (f32[122,128]{1,0:T(8,128)S(1)}, f32[122,128]{1,0:T(8,128)S(1)}, u32[]{:S(2)}, u32[]{:S(2)}) collective-permute-start(f32[122,128]{1,0:T(8,128)S(1)} %add.88), channel_id=1, source_target_pairs={{0,2},{1,3},{2,0},{3,1},{4,6},{5,7},{6,4},{7,5},{8,10},{9,11},{10,... | collective-permute-start | bytes 187400 | tf_op jit(solution)/shard_map/ppermute | solution.py:57
  59.1 11.7 %copy-start = (pred[64]{0:T(512)(128)(4,1)S(1)}, pred[64]{0:T(512)(128)(4,1)}, u32[]{:S(2)}) copy-start(pred[64]{0:T(512)(128)(4,1)} %constant.33.clone.1) | copy-start | bytes 196
  59.1 7.7 %collective-permute-start.5 = (f32[122,128]{1,0:T(8,128)S(1)}, f32[122,128]{1,0:T(8,128)S(1)}, u32[]{:S(2)}, u32[]{:S(2)}) collective-permute-start(f32[122,128]{1,0:T(8,128)S(1)} %add.89), channel_id=1, source_target_pairs={{0,4},{1,5},{2,6},{3,7},{4,0},{5,1},{6,2},{7,3},{8,12},{9,13},{10,... | collective-permute-start | bytes 187400 | tf_op jit(solution)/shard_map/ppermute | solution.py:57
  66.8 7.7 %collective-permute-start.6 = (f32[122,128]{1,0:T(8,128)S(1)}, f32[122,128]{1,0:T(8,128)S(1)}, u32[]{:S(2)}, u32[]{:S(2)}) collective-permute-start(f32[122,128]{1,0:T(8,128)S(1)} %add.90), channel_id=1, source_target_pairs={{0,8},{1,9},{2,10},{3,11},{4,12},{5,13},{6,14},{7,15},{8,0},{9,1},... | collective-permute-start | bytes 187400 | tf_op jit(solution)/shard_map/ppermute | solution.py:57
Sparse Core Ops, SparseCore 0:
  81.8 56.5 reduce-scatter.1

commit v8 on v6

--- a/solution.py
+++ b/solution.py
@@ -85,12 +85,10 @@
         partial_value, lax.axis_size("recv"), white_parts, lax.axis_size("recv") // 2
     )
     white_all = jnp.concatenate([white] + white_parts, axis=1)
-    nsrc = panel.shape[2]
-    panel = panel.reshape(panel.shape[0], panel.shape[1], nsrc // width, width)
-    blocks = [lax.dynamic_index_in_dim(panel, q, axis=3, keepdims=False)]
-    for b, pairs in zip(range(1, width), moves):
-        theirs = lax.dynamic_index_in_dim(panel, q ^ b, axis=3, keepdims=False)
-        blocks.append(lax.ppermute(theirs, group, pairs))
+    rows, segs, nsrc = panel.shape
+    panel = panel.reshape(rows, segs, nsrc // width, width).transpose(3, 0, 1, 2)
+    panel = lax.all_to_all(panel, group, 0, 0, tiled=True)
+    blocks = [lax.dynamic_index_in_dim(panel, q ^ b, axis=0, keepdims=False) for b in range(width)]
     panel_own = jnp.concatenate(blocks, axis=1)
     factor = 1.0 / math.sqrt(total_segs)
     totals = cross_terms(panel_own, white_all, factor)

time: 134 us -> 130 us (0.970)
  the two profiles are of different devices: /device:TPU:64 before, /device:TPU:20 now
where the time goes in v8:
time: 130 us
  waiting for transfers between devices  76.4 us (59%)
  starting transfers between devices  22.3 us (17%)
  between operations  13.7 us (11%)
  matrix products  9.38 us (7%)
  local copies, waits for them, and re-layouts  5.44 us (4%)
  other arithmetic  2.68 us (2%)
    reduce_scatter x1, waiting for transfers between devices, on_device(): out = lax.psum_scatter(totals, 'zhi', scatter_dimension=0, tiled=True)  56.2 us
    ppermute x4, waiting for transfers between devices, psum_recv(): value = value + lax.ppermute(value, 'recv', pairs)  13.2 us
    ppermute x4, starting transfers between devices, psum_recv(): value = value + lax.ppermute(value, 'recv', pairs)  9.77 us
    ppermute x3, starting transfers between devices, on_device(): white_parts = [lax.ppermute(white, group, pairs) for pairs in moves]  9.21 us
    dot_general x1, matrix products, on_device(): lax.dot_general(basis, traces, (((1,), (2,)), ((), ())), preferred_elemen...  3.87 us
    ppermute x3, waiting for transfers between devices, on_device(): white_parts = [lax.ppermute(white, group, pairs) for pairs in moves]  3.65 us
    all_to_all x1, waiting for transfers between devices, on_device(): panel = lax.all_to_all(panel, group, 0, 0, tiled=True)  3.31 us
    all_to_all x1, starting transfers between devices, on_device(): panel = lax.all_to_all(panel, group, 0, 0, tiled=True)  3.28 us
  transfers between devices with their start and end apart: 9, of which 7 were waited for; matrix products, arithmetic and copies ran while one was open for 2% of the time, Pallas kernels for 0%

profile of v8, /device:TPU:20, one launch (start us, length us, event | category | flops | bytes accessed | tf_op | source)
XLA Modules:
  0.0 129.9 jit_solution(17819321797061007642)
XLA Ops:
  6.5 0.7 convert_element_type.10
  7.2 3.9 %fusion.18 = f32[122,4,256]{2,0,1:T(8,128)S(1)} fusion(bf16[122,2048,1]{1,0,2:T(8,128)(2,1)} %constant.56, bf16[4,256,2048]{2,1,0:T(8,128)(2,1)} %param.4), kind=kOutput, calls=%fused_computation.37 | convolution fusion | flops 511705088 | bytes 5193728 | tf_op jit(solution)/shard_map/dot_general | solution.py:76
  11.1 0.0 copy-start.2
  11.1 0.1 fusion.17
  11.2 0.1 slice_multiply_fusion.1
  11.4 3.8 %collective-permute-start.4 = (f32[122,4,256]{2,0,1:T(8,128)S(1)}, f32[122,4,256]{2,0,1:T(8,128)S(1)}, u32[]{:S(2)}, u32[]{:S(2)}) collective-permute-start(f32[122,4,256]{2,0,1:T(8,128)S(1)} %pad_maximum_fusion.1), channel_id=1, source_target_pairs={{0,32},{16,48},{32,0},{48,16},{1,33},{17,49},{33,1},{49,17},{2,34}... | collective-permute-start | bytes 1499144 | tf_op jit(solution)/shard_map/ppermute | solution.py:82
  15.2 3.1 %collective-permute-start.3 = (f32[122,4,256]{2,0,1:T(8,128)S(1)}, f32[122,4,256]{2,0,1:T(8,128)S(1)}, u32[]{:S(2)}, u32[]{:S(2)}) collective-permute-start(f32[122,4,256]{2,0,1:T(8,128)S(1)} %pad_maximum_fusion.1), channel_id=1, source_target_pairs={{0,16},{16,0},{32,48},{48,32},{1,17},{17,1},{33,49},{49,33},{2,18}... | collective-permute-start | bytes 1499144 | tf_op jit(solution)/shard_map/ppermute | solution.py:82
  18.3 2.3 %collective-permute-start.5 = (f32[122,4,256]{2,0,1:T(8,128)S(1)}, f32[122,4,256]{2,0,1:T(8,128)S(1)}, u32[]{:S(2)}, u32[]{:S(2)}) collective-permute-start(f32[122,4,256]{2,0,1:T(8,128)S(1)} %pad_maximum_fusion.1), channel_id=1, source_target_pairs={{0,48},{16,32},{32,16},{48,0},{1,49},{17,33},{33,17},{49,1},{2,50}... | collective-permute-start | bytes 1499144 | tf_op jit(solution)/shard_map/ppermute | solution.py:82
  20.6 0.0 copy-done.2
  20.6 0.4 fusion.10
  21.0 1.9 %collective-permute-start = (f32[122,4,32]{0,2,1:T(8,128)S(1)}, f32[122,4,32]{0,2,1:T(8,128)S(1)}, u32[]{:S(2)}, u32[]{:S(2)}) collective-permute-start(f32[122,4,32]{0,2,1:T(8,128)S(1)} %fusion.10), channel_id=1, source_target_pairs={{0,1},{1,0},{2,3},{3,2},{4,5},{5,4},{6,7},{7,6},{8,9},{9,8},{10,11... | collective-permute-start | bytes 187400 | tf_op jit(solution)/shard_map/ppermute | solution.py:59
  23.0 1.2 collective-permute-done
  24.2 3.2 %collective-permute-start.1 = (f32[122,4,32]{0,2,1:T(8,128)S(1)}, f32[122,4,32]{0,2,1:T(8,128)S(1)}, u32[]{:S(2)}, u32[]{:S(2)}) collective-permute-start(f32[122,4,32]{0,2,1:T(8,128)S(1)} %add.75), channel_id=1, source_target_pairs={{0,2},{1,3},{2,0},{3,1},{4,6},{5,7},{6,4},{7,5},{8,10},{9,11},{10,... | collective-permute-start | bytes 187400 | tf_op jit(solution)/shard_map/ppermute | solution.py:59
  27.4 3.0 %collective-permute-done.1 = f32[122,4,32]{0,2,1:T(8,128)S(1)} collective-permute-done((f32[122,4,32]{0,2,1:T(8,128)S(1)}, f32[122,4,32]{0,2,1:T(8,128)S(1)}, u32[]{:S(2)}, u32[]{:S(2)}) %collective-permute-start.1) | collective-permute-done | bytes 62496 | tf_op jit(solution)/shard_map/ppermute | solution.py:59
  30.4 2.2 %collective-permute-start.2 = (f32[122,4,32]{0,2,1:T(8,128)S(1)}, f32[122,4,32]{0,2,1:T(8,128)S(1)}, u32[]{:S(2)}, u32[]{:S(2)}) collective-permute-start(f32[122,4,32]{0,2,1:T(8,128)S(1)} %add.76), channel_id=1, source_target_pairs={{0,4},{1,5},{2,6},{3,7},{4,0},{5,1},{6,2},{7,3},{8,12},{9,13},{10,... | collective-permute-start | bytes 187400 | tf_op jit(solution)/shard_map/ppermute | solution.py:59
  32.6 5.4 %collective-permute-done.2 = f32[122,4,32]{0,2,1:T(8,128)S(1)} collective-permute-done((f32[122,4,32]{0,2,1:T(8,128)S(1)}, f32[122,4,32]{0,2,1:T(8,128)S(1)}, u32[]{:S(2)}, u32[]{:S(2)}) %collective-permute-start.2) | collective-permute-done | bytes 62496 | tf_op jit(solution)/shard_map/ppermute | solution.py:59
  38.0 0.0 collective-permute-done.4
  38.1 3.6 %collective-permute-done.3 = f32[122,4,256]{2,0,1:T(8,128)S(1)} collective-permute-done((f32[122,4,256]{2,0,1:T(8,128)S(1)}, f32[122,4,256]{2,0,1:T(8,128)S(1)}, u32[]{:S(2)}, u32[]{:S(2)}) %collective-permute-start.3) | collective-permute-done | bytes 499744 | tf_op jit(solution)/shard_map/ppermute | solution.py:82
  41.7 0.0 collective-permute-done.5
  41.7 2.4 %collective-permute-start.6 = (f32[122,4,32]{0,2,1:T(8,128)S(1)}, f32[122,4,32]{0,2,1:T(8,128)S(1)}, u32[]{:S(2)}, u32[]{:S(2)}) collective-permute-start(f32[122,4,32]{0,2,1:T(8,128)S(1)} %add.77), channel_id=1, source_target_pairs={{0,8},{1,9},{2,10},{3,11},{4,12},{5,13},{6,14},{7,15},{8,0},{9,1},... | collective-permute-start | bytes 187400 | tf_op jit(solution)/shard_map/ppermute | solution.py:59
  44.1 0.2 pad_maximum_fusion
  44.3 0.0 copy-start
  44.3 1.3 %copy-done = f32[122,16,256]{2,0,1:T(8,128)} copy-done((f32[122,16,256]{2,0,1:T(8,128)}, f32[122,16,256]{2,0,1:T(8,128)S(1)}, u32[]{:S(2)}) %copy-start) | copy-done | bytes 1998872
  45.6 0.0 copy-start.1
  45.6 0.1 slice.34
  45.7 3.6 %collective-permute-done.6 = f32[122,4,32]{0,2,1:T(8,128)S(1)} collective-permute-done((f32[122,4,32]{0,2,1:T(8,128)S(1)}, f32[122,4,32]{0,2,1:T(8,128)S(1)}, u32[]{:S(2)}, u32[]{:S(2)}) %collective-permute-start.6) | collective-permute-done | bytes 62496 | tf_op jit(solution)/shard_map/ppermute | solution.py:59
  49.4 0.6 copy.36
  50.0 3.3 %all-to-all-start = ((f32[4,122,4,8]{1,3,2,0:T(8,128)}), f32[4,122,4,8]{1,3,2,0:T(8,128)S(1)}, u32[]{:S(2)}, u32[]{:S(2)}) async-start(f32[4,122,4,8]{1,3,2,0:T(8,128)} %bitcast.28), calls=%async_computation | async-start | bytes 131072 | tf_op jit(solution)/shard_map/all_to_all | solution.py:90
  53.3 0.0 reduce-scatter.2.cloned.1.call-start
  53.4 0.0 copy-done.1
  53.4 1.4 %slice_select_fusion = f32[64,16,256]{2,0,1:T(8,128)S(1)} fusion(f32[122,16,256]{2,0,1:T(8,128)} %copy-done, pred[64]{0:T(512)(128)(4,1)S(1)} %copy-done.1), kind=kLoop, calls=%fused_computation.5 | loop fusion | flops 262144 | bytes 2097216 | tf_op jit(solution)/shard_map/jit(_pad)/pad | solution.py:35
  54.8 3.3 %all-to-all-done = f32[4,122,4,8]{1,3,2,0:T(8,128)S(1)} async-done(((f32[4,122,4,8]{1,3,2,0:T(8,128)}), f32[4,122,4,8]{1,3,2,0:T(8,128)S(1)}, u32[]{:S(2)}, u32[]{:S(2)}) %all-to-all-start) | async-done | bytes 62496 | tf_op jit(solution)/shard_map/all_to_all | solution.py:90
  58.1 0.1 slice.35
  58.2 0.2 copy.24
  58.4 0.2 copy.16
  58.6 1.3 fusion.4
  59.9 1.3 fusion.6
  61.1 1.3 fusion.1
  62.4 1.3 %fusion = f32[8,1,64,256]{3,0,2,1:T(8,128)S(1)} fusion(f32[64,256,8]{1,2,0:T(8,128)S(1)} %fusion.6, f32[64,16,256]{2,0,1:T(8,128)S(1)} %slice_select_fusion, f32[61,16,8]{1,2,0:T(8,128)S(1)} %copy.24), kind=kOutput, calls=%fused_computation.2 | convolution fusion | flops 25296896 | bytes 2128384 | tf_op jit(solution)/shard_map/fts,ftc->sfc/dot_general | solution.py:47
  63.7 0.1 maximum_multiply_fusion
  63.8 1.3 copy.22
  65.1 0.0 reduce-scatter.2.cloned.1.call-update
  65.2 56.2 %reduce-scatter.2.cloned.1.call-done = f32[1,2,64,256]{3,2,1,0:T(8,128)} async-done(((f32[8,2,64,256]{3,2,1,0:T(8,128)}), f32[1,2,64,256]{3,2,1,0:T(8,128)}) %reduce-scatter.2.cloned.1.call-update) | async-done | bytes 131088 | tf_op jit(solution)/shard_map/reduce_scatter | solution.py:95
  121.4 1.6 %copy.23 = f32[1,2,61,256]{3,1,2,0:T(2,128)} copy(f32[1,2,61,256]{3,2,1,0:T(8,128)} %bitcast.31) | data formatting | bytes 249856 | tf_op jit(solution)/shard_map/slice | solution.py:96
  (11 shorter events, 0.1 us)
Async XLA Ops:
  11.1 9.5 %copy-start.2 = (s32[32]{0:T(128)S(1)}, s32[32]{0:T(128)}, u32[]{:S(2)}) copy-start(s32[32]{0:T(128)} %param.6) | copy-start | bytes 388
  11.4 26.7 %collective-permute-start.4 = (f32[122,4,256]{2,0,1:T(8,128)S(1)}, f32[122,4,256]{2,0,1:T(8,128)S(1)}, u32[]{:S(2)}, u32[]{:S(2)}) collective-permute-start(f32[122,4,256]{2,0,1:T(8,128)S(1)} %pad_maximum_fusion.1), channel_id=1, source_target_pairs={{0,32},{16,48},{32,0},{48,16},{1,33},{17,49},{33,1},{49,17},{2,34}... | collective-permute-start | bytes 1499144 | tf_op jit(solution)/shard_map/ppermute | solution.py:82
  15.2 26.5 %collective-permute-start.3 = (f32[122,4,256]{2,0,1:T(8,128)S(1)}, f32[122,4,256]{2,0,1:T(8,128)S(1)}, u32[]{:S(2)}, u32[]{:S(2)}) collective-permute-start(f32[122,4,256]{2,0,1:T(8,128)S(1)} %pad_maximum_fusion.1), channel_id=1, source_target_pairs={{0,16},{16,0},{32,48},{48,32},{1,17},{17,1},{33,49},{49,33},{2,18}... | collective-permute-start | bytes 1499144 | tf_op jit(solution)/shard_map/ppermute | solution.py:82
  18.3 23.4 %collective-permute-start.5 = (f32[122,4,256]{2,0,1:T(8,128)S(1)}, f32[122,4,256]{2,0,1:T(8,128)S(1)}, u32[]{:S(2)}, u32[]{:S(2)}) collective-permute-start(f32[122,4,256]{2,0,1:T(8,128)S(1)} %pad_maximum_fusion.1), channel_id=1, source_target_pairs={{0,48},{16,32},{32,16},{48,0},{1,49},{17,33},{33,17},{49,1},{2,50}... | collective-permute-start | bytes 1499144 | tf_op jit(solution)/shard_map/ppermute | solution.py:82
  21.0 3.1 %collective-permute-start = (f32[122,4,32]{0,2,1:T(8,128)S(1)}, f32[122,4,32]{0,2,1:T(8,128)S(1)}, u32[]{:S(2)}, u32[]{:S(2)}) collective-permute-start(f32[122,4,32]{0,2,1:T(8,128)S(1)} %fusion.10), channel_id=1, source_target_pairs={{0,1},{1,0},{2,3},{3,2},{4,5},{5,4},{6,7},{7,6},{8,9},{9,8},{10,11... | collective-permute-start | bytes 187400 | tf_op jit(solution)/shard_map/ppermute | solution.py:59
  24.2 6.2 %collective-permute-start.1 = (f32[122,4,32]{0,2,1:T(8,128)S(1)}, f32[122,4,32]{0,2,1:T(8,128)S(1)}, u32[]{:S(2)}, u32[]{:S(2)}) collective-permute-start(f32[122,4,32]{0,2,1:T(8,128)S(1)} %add.75), channel_id=1, source_target_pairs={{0,2},{1,3},{2,0},{3,1},{4,6},{5,7},{6,4},{7,5},{8,10},{9,11},{10,... | collective-permute-start | bytes 187400 | tf_op jit(solution)/shard_map/ppermute | solution.py:59
  30.4 7.7 %collective-permute-start.2 = (f32[122,4,32]{0,2,1:T(8,128)S(1)}, f32[122,4,32]{0,2,1:T(8,128)S(1)}, u32[]{:S(2)}, u32[]{:S(2)}) collective-permute-start(f32[122,4,32]{0,2,1:T(8,128)S(1)} %add.76), channel_id=1, source_target_pairs={{0,4},{1,5},{2,6},{3,7},{4,0},{5,1},{6,2},{7,3},{8,12},{9,13},{10,... | collective-permute-start | bytes 187400 | tf_op jit(solution)/shard_map/ppermute | solution.py:59
  41.7 7.7 %collective-permute-start.6 = (f32[122,4,32]{0,2,1:T(8,128)S(1)}, f32[122,4,32]{0,2,1:T(8,128)S(1)}, u32[]{:S(2)}, u32[]{:S(2)}) collective-permute-start(f32[122,4,32]{0,2,1:T(8,128)S(1)} %add.77), channel_id=1, source_target_pairs={{0,8},{1,9},{2,10},{3,11},{4,12},{5,13},{6,14},{7,15},{8,0},{9,1},... | collective-permute-start | bytes 187400 | tf_op jit(solution)/shard_map/ppermute | solution.py:59
  44.3 1.3 %copy-start = (f32[122,16,256]{2,0,1:T(8,128)}, f32[122,16,256]{2,0,1:T(8,128)S(1)}, u32[]{:S(2)}) copy-start(f32[122,16,256]{2,0,1:T(8,128)S(1)} %pad_maximum_fusion) | copy-start | bytes 5996548
  45.6 7.7 %copy-start.1 = (pred[64]{0:T(512)(128)(4,1)S(1)}, pred[64]{0:T(512)(128)(4,1)}, u32[]{:S(2)}) copy-start(pred[64]{0:T(512)(128)(4,1)} %constant.34.clone.1) | copy-start | bytes 196
  50.0 8.1 %all-to-all-start = ((f32[4,122,4,8]{1,3,2,0:T(8,128)}), f32[4,122,4,8]{1,3,2,0:T(8,128)S(1)}, u32[]{:S(2)}, u32[]{:S(2)}) async-start(f32[4,122,4,8]{1,3,2,0:T(8,128)} %bitcast.28), calls=%async_computation | async-start | bytes 131072 | tf_op jit(solution)/shard_map/all_to_all | solution.py:90
  53.3 68.1 %reduce-scatter.2.cloned.1.call-start = ((), (), s32[]{:S(2)}) async-start(), calls=%async_computation.2 | async-start | bytes 1179648 | tf_op jit(solution)/shard_map/reduce_scatter | solution.py:95
Sparse Core Ops, SparseCore 0:
  65.3 56.0 reduce-scatter.1

commit v9 on v8

--- a/solution.py
+++ b/solution.py
@@ -77,19 +77,18 @@
         basis, traces, (((1,), (2,)), ((), ())), preferred_element_type=jnp.float32
     )
     white = whiten_block(spec, valid_float)
-    q = lax.axis_index("zlo") * lax.axis_size("xlo") + lax.axis_index("xlo")
-    moves = [[(r, r ^ b) for r in range(width)] for b in range(1, width)]
-    white_parts = [lax.ppermute(white, group, pairs) for pairs in moves]
+    spread = jnp.broadcast_to(white[None], (width,) + white.shape)
+    white_parts = lax.all_to_all(spread, group, 0, 0, tiled=True)
     partial_value = jnp.einsum("ktc,sc->kts", white, onehot, precision=lax.Precision.HIGHEST)
     panel, white_parts = psum_recv(
         partial_value, lax.axis_size("recv"), white_parts, lax.axis_size("recv") // 2
     )
-    white_all = jnp.concatenate([white] + white_parts, axis=1)
-    rows, segs, nsrc = panel.shape
+    rows, segs, nchan = white.shape
+    white_all = white_parts.transpose(1, 0, 2, 3).reshape(rows, width * segs, nchan)
+    nsrc = panel.shape[2]
     panel = panel.reshape(rows, segs, nsrc // width, width).transpose(3, 0, 1, 2)
     panel = lax.all_to_all(panel, group, 0, 0, tiled=True)
-    blocks = [lax.dynamic_index_in_dim(panel, q ^ b, axis=0, keepdims=False) for b in range(width)]
-    panel_own = jnp.concatenate(blocks, axis=1)
+    panel_own = panel.transpose(1, 0, 2, 3).reshape(rows, width * segs, nsrc // width)
     factor = 1.0 / math.sqrt(total_segs)
     totals = cross_terms(panel_own, white_all, factor)
     out = lax.psum_scatter(totals, "zhi", scatter_dimension=0, tiled=True)

time: 130 us -> 128 us (0.985)
  the two profiles are of different devices: /device:TPU:20 before, /device:TPU:18 now
where the time goes in v9:
time: 128 us
  waiting for transfers between devices  71.8 us (56%)
  starting transfers between devices  24.7 us (19%)
  between operations  13.6 us (11%)
  local copies, waits for them, and re-layouts  9.77 us (8%)
  matrix products  7.07 us (6%)
    reduce_scatter x1, waiting for transfers between devices, on_device(): out = lax.psum_scatter(totals, 'zhi', scatter_dimension=0, tiled=True)  57.6 us
    ppermute x4, starting transfers between devices, psum_recv(): value = value + lax.ppermute(value, 'recv', pairs)  16.2 us
    ppermute x4, waiting for transfers between devices, psum_recv(): value = value + lax.ppermute(value, 'recv', pairs)  10 us
    all_to_all x1, starting transfers between devices, on_device(): white_parts = lax.all_to_all(spread, group, 0, 0, tiled=True)  4.65 us
    all_to_all x1, waiting for transfers between devices, on_device(): white_parts = lax.all_to_all(spread, group, 0, 0, tiled=True)  4.18 us
    dot_general x1, matrix products, on_device(): lax.dot_general(basis, traces, (((1,), (2,)), ((), ())), preferred_elemen...  3.87 us
    all_to_all x1, starting transfers between devices, on_device(): panel = lax.all_to_all(panel, group, 0, 0, tiled=True)  3.82 us
    slice x3, local copies, waits for them, and re-layouts, cross_terms(): own_real = pad_bins(white[:NB])  3.15 us
  transfers between devices with their start and end apart: 7, of which 6 were waited for; matrix products, arithmetic and copies ran while one was open for 3% of the time, Pallas kernels for 0%

profile of v9, /device:TPU:18, one launch (start us, length us, event | category | flops | bytes accessed | tf_op | source)
XLA Modules:
  0.0 128.0 jit_solution(8906128896573471703)
XLA Ops:
  6.5 0.7 convert_element_type.10
  7.2 3.9 %fusion.20 = f32[122,4,256]{2,0,1:T(8,128)S(1)} fusion(bf16[122,2048,1]{1,0,2:T(8,128)(2,1)} %constant.30, bf16[4,256,2048]{2,1,0:T(8,128)(2,1)} %param.4), kind=kOutput, calls=%fused_computation.31 | convolution fusion | flops 511705088 | bytes 5193728 | tf_op jit(solution)/shard_map/dot_general | solution.py:76
  11.1 0.1 fusion.17
  11.2 0.1 slice_multiply_fusion.1
  11.3 0.0 copy-start
  11.4 0.3 copy.14
  11.7 1.6 %broadcast_in_dim.2 = f32[4,122,4,256]{3,2,1,0:T(4,128)} broadcast(f32[122,4,256]{2,1,0:T(4,128)S(1)} %copy.14), dimensions={1,2,3} | broadcast | bytes 2498560 | tf_op jit(solution)/shard_map/broadcast_in_dim | solution.py:80
  13.3 4.6 %all-to-all-start = ((f32[4,122,4,256]{3,2,1,0:T(4,128)}), f32[4,122,4,256]{3,2,1,0:T(4,128)S(1)}, u32[]{:S(2)}, u32[]{:S(2)}) async-start(f32[4,122,4,256]{3,2,1,0:T(4,128)} %broadcast_in_dim.2), calls=%async_computation | async-start | bytes 3997696 | tf_op jit(solution)/shard_map/all_to_all | solution.py:81
  17.9 0.0 copy-done
  17.9 0.4 fusion.8
  18.3 1.9 %collective-permute-start = (f32[122,4,32]{0,2,1:T(8,128)S(1)}, f32[122,4,32]{0,2,1:T(8,128)S(1)}, u32[]{:S(2)}, u32[]{:S(2)}) collective-permute-start(f32[122,4,32]{0,2,1:T(8,128)S(1)} %fusion.8), channel_id=1, source_target_pairs={{0,1},{1,0},{2,3},{3,2},{4,5},{5,4},{6,7},{7,6},{8,9},{9,8},{10,11... | collective-permute-start | bytes 187400 | tf_op jit(solution)/shard_map/ppermute | solution.py:59
  20.2 1.2 collective-permute-done
  21.5 3.2 %collective-permute-start.1 = (f32[122,4,32]{0,2,1:T(8,128)S(1)}, f32[122,4,32]{0,2,1:T(8,128)S(1)}, u32[]{:S(2)}, u32[]{:S(2)}) collective-permute-start(f32[122,4,32]{0,2,1:T(8,128)S(1)} %add.63), channel_id=1, source_target_pairs={{0,2},{1,3},{2,0},{3,1},{4,6},{5,7},{6,4},{7,5},{8,10},{9,11},{10,... | collective-permute-start | bytes 187400 | tf_op jit(solution)/shard_map/ppermute | solution.py:59
  24.7 3.0 %collective-permute-done.1 = f32[122,4,32]{0,2,1:T(8,128)S(1)} collective-permute-done((f32[122,4,32]{0,2,1:T(8,128)S(1)}, f32[122,4,32]{0,2,1:T(8,128)S(1)}, u32[]{:S(2)}, u32[]{:S(2)}) %collective-permute-start.1) | collective-permute-done | bytes 62496 | tf_op jit(solution)/shard_map/ppermute | solution.py:59
  27.7 7.1 %collective-permute-start.2 = (f32[122,4,32]{0,2,1:T(8,128)S(1)}, f32[122,4,32]{0,2,1:T(8,128)S(1)}, u32[]{:S(2)}, u32[]{:S(2)}) collective-permute-start(f32[122,4,32]{0,2,1:T(8,128)S(1)} %add.64), channel_id=1, source_target_pairs={{0,4},{1,5},{2,6},{3,7},{4,0},{5,1},{6,2},{7,3},{8,12},{9,13},{10,... | collective-permute-start | bytes 187400 | tf_op jit(solution)/shard_map/ppermute | solution.py:59
  34.7 2.2 %collective-permute-done.2 = f32[122,4,32]{0,2,1:T(8,128)S(1)} collective-permute-done((f32[122,4,32]{0,2,1:T(8,128)S(1)}, f32[122,4,32]{0,2,1:T(8,128)S(1)}, u32[]{:S(2)}, u32[]{:S(2)}) %collective-permute-start.2) | collective-permute-done | bytes 62496 | tf_op jit(solution)/shard_map/ppermute | solution.py:59
  37.0 4.2 %all-to-all-done = f32[4,122,4,256]{3,2,1,0:T(4,128)S(1)} async-done(((f32[4,122,4,256]{3,2,1,0:T(4,128)}), f32[4,122,4,256]{3,2,1,0:T(4,128)S(1)}, u32[]{:S(2)}, u32[]{:S(2)}) %all-to-all-start) | async-done | bytes 1998880 | tf_op jit(solution)/shard_map/all_to_all | solution.py:81
  41.2 4.1 %collective-permute-start.3 = (f32[122,4,32]{0,2,1:T(8,128)S(1)}, f32[122,4,32]{0,2,1:T(8,128)S(1)}, u32[]{:S(2)}, u32[]{:S(2)}) collective-permute-start(f32[122,4,32]{0,2,1:T(8,128)S(1)} %add.65), channel_id=1, source_target_pairs={{0,8},{1,9},{2,10},{3,11},{4,12},{5,13},{6,14},{7,15},{8,0},{9,1},... | collective-permute-start | bytes 187400 | tf_op jit(solution)/shard_map/ppermute | solution.py:59
  45.2 3.6 %collective-permute-done.3 = f32[122,4,32]{0,2,1:T(8,128)S(1)} collective-permute-done((f32[122,4,32]{0,2,1:T(8,128)S(1)}, f32[122,4,32]{0,2,1:T(8,128)S(1)}, u32[]{:S(2)}, u32[]{:S(2)}) %collective-permute-start.3) | collective-permute-done | bytes 62496 | tf_op jit(solution)/shard_map/ppermute | solution.py:59
  48.8 0.6 copy.23
  49.5 3.8 %all-to-all-start.1 = ((f32[4,122,4,8]{1,3,2,0:T(8,128)}), f32[4,122,4,8]{1,3,2,0:T(8,128)S(1)}, u32[]{:S(2)}, u32[]{:S(2)}) async-start(f32[4,122,4,8]{1,3,2,0:T(8,128)} %bitcast.34), calls=%async_computation.1 | async-start | bytes 131072 | tf_op jit(solution)/shard_map/all_to_all | solution.py:90
  53.3 0.0 reduce-scatter.2.cloned.1.call-start
  53.3 1.3 %fusion.18 = (f32[61,4,4,256]{3,2,0,1:T(4,128)}, f32[61,4,4,256]{3,2,0,1:T(4,128)S(1)}) fusion(f32[122,4,4,256]{3,2,0,1:T(4,128)S(1)} %bitcast.36), kind=kLoop, calls=%fused_computation.29 | loop fusion | bytes 3997696 | tf_op jit(solution)/shard_map/slice | solution.py:42
  54.6 0.3 copy.18
  54.9 0.3 slice.40
  55.2 1.5 %copy.15 = f32[61,4,4,256]{3,2,1,0:T(4,128)S(1)} copy(f32[61,4,4,256]{3,2,0,1:T(4,128)} %get-tuple-element.9) | data formatting | bytes 1998848 | tf_op jit(solution)/shard_map/slice | solution.py:42
  56.7 0.3 slice.36
  57.1 0.0 all-to-all-done.1
  57.1 0.1 fusion.19
  57.2 0.2 copy.17
  57.4 0.2 copy.19
  57.7 0.7 fusion.4
  58.4 0.7 fusion.6
  59.1 0.7 fusion
  59.8 0.7 fusion.1
  60.5 0.1 maximum_multiply_fusion
  60.6 1.3 %copy.20 = f32[8,2,64,256]{3,2,1,0:T(8,128)} copy(f32[8,2,64,256]{3,0,2,1:T(8,128)S(1)} %maximum_multiply_fusion) | data formatting | bytes 2097152 | tf_op jit(solution)/shard_map/mul | solution.py:50
  61.9 0.0 reduce-scatter.2.cloned.1.call-update
  61.9 57.6 %reduce-scatter.2.cloned.1.call-done = f32[1,2,64,256]{3,2,1,0:T(8,128)} async-done(((f32[8,2,64,256]{3,2,1,0:T(8,128)}), f32[1,2,64,256]{3,2,1,0:T(8,128)}) %reduce-scatter.2.cloned.1.call-update) | async-done | bytes 131088 | tf_op jit(solution)/shard_map/reduce_scatter | solution.py:94
  119.5 1.6 %copy.21 = f32[1,2,61,256]{3,1,2,0:T(2,128)} copy(f32[1,2,61,256]{3,2,1,0:T(8,128)} %bitcast.41) | data formatting | bytes 249856 | tf_op jit(solution)/shard_map/slice | solution.py:95
  (11 shorter events, 0.2 us)
Async XLA Ops:
  11.3 6.6 %copy-start = (s32[32]{0:T(128)S(1)}, s32[32]{0:T(128)}, u32[]{:S(2)}) copy-start(s32[32]{0:T(128)} %param.6) | copy-start | bytes 388
  13.3 27.9 %all-to-all-start = ((f32[4,122,4,256]{3,2,1,0:T(4,128)}), f32[4,122,4,256]{3,2,1,0:T(4,128)S(1)}, u32[]{:S(2)}, u32[]{:S(2)}) async-start(f32[4,122,4,256]{3,2,1,0:T(4,128)} %broadcast_in_dim.2), calls=%async_computation | async-start | bytes 3997696 | tf_op jit(solution)/shard_map/all_to_all | solution.py:81
  18.3 3.1 %collective-permute-start = (f32[122,4,32]{0,2,1:T(8,128)S(1)}, f32[122,4,32]{0,2,1:T(8,128)S(1)}, u32[]{:S(2)}, u32[]{:S(2)}) collective-permute-start(f32[122,4,32]{0,2,1:T(8,128)S(1)} %fusion.8), channel_id=1, source_target_pairs={{0,1},{1,0},{2,3},{3,2},{4,5},{5,4},{6,7},{7,6},{8,9},{9,8},{10,11... | collective-permute-start | bytes 187400 | tf_op jit(solution)/shard_map/ppermute | solution.py:59
  21.5 6.2 %collective-permute-start.1 = (f32[122,4,32]{0,2,1:T(8,128)S(1)}, f32[122,4,32]{0,2,1:T(8,128)S(1)}, u32[]{:S(2)}, u32[]{:S(2)}) collective-permute-start(f32[122,4,32]{0,2,1:T(8,128)S(1)} %add.63), channel_id=1, source_target_pairs={{0,2},{1,3},{2,0},{3,1},{4,6},{5,7},{6,4},{7,5},{8,10},{9,11},{10,... | collective-permute-start | bytes 187400 | tf_op jit(solution)/shard_map/ppermute | solution.py:59
  27.7 9.3 %collective-permute-start.2 = (f32[122,4,32]{0,2,1:T(8,128)S(1)}, f32[122,4,32]{0,2,1:T(8,128)S(1)}, u32[]{:S(2)}, u32[]{:S(2)}) collective-permute-start(f32[122,4,32]{0,2,1:T(8,128)S(1)} %add.64), channel_id=1, source_target_pairs={{0,4},{1,5},{2,6},{3,7},{4,0},{5,1},{6,2},{7,3},{8,12},{9,13},{10,... | collective-permute-start | bytes 187400 | tf_op jit(solution)/shard_map/ppermute | solution.py:59
  41.2 7.7 %collective-permute-start.3 = (f32[122,4,32]{0,2,1:T(8,128)S(1)}, f32[122,4,32]{0,2,1:T(8,128)S(1)}, u32[]{:S(2)}, u32[]{:S(2)}) collective-permute-start(f32[122,4,32]{0,2,1:T(8,128)S(1)} %add.65), channel_id=1, source_target_pairs={{0,8},{1,9},{2,10},{3,11},{4,12},{5,13},{6,14},{7,15},{8,0},{9,1},... | collective-permute-start | bytes 187400 | tf_op jit(solution)/shard_map/ppermute | solution.py:59
  49.5 7.6 %all-to-all-start.1 = ((f32[4,122,4,8]{1,3,2,0:T(8,128)}), f32[4,122,4,8]{1,3,2,0:T(8,128)S(1)}, u32[]{:S(2)}, u32[]{:S(2)}) async-start(f32[4,122,4,8]{1,3,2,0:T(8,128)} %bitcast.34), calls=%async_computation.1 | async-start | bytes 131072 | tf_op jit(solution)/shard_map/all_to_all | solution.py:90
  53.3 66.2 %reduce-scatter.2.cloned.1.call-start = ((), (), s32[]{:S(2)}) async-start(), calls=%async_computation.3 | async-start | bytes 1179648 | tf_op jit(solution)/shard_map/reduce_scatter | solution.py:94
Sparse Core Ops, SparseCore 0:
  62.0 57.4 reduce-scatter.1

commit v10 on v9

--- a/solution.py
+++ b/solution.py
@@ -77,18 +77,18 @@
         basis, traces, (((1,), (2,)), ((), ())), preferred_element_type=jnp.float32
     )
     white = whiten_block(spec, valid_float)
-    spread = jnp.broadcast_to(white[None], (width,) + white.shape)
-    white_parts = lax.all_to_all(spread, group, 0, 0, tiled=True)
+    rows, segs, nchan = white.shape
+    spread = jnp.broadcast_to(white[:, None], (rows, width, segs, nchan)).reshape(rows, width * segs, nchan)
+    white_parts = lax.all_to_all(spread, group, 1, 1, tiled=True)
     partial_value = jnp.einsum("ktc,sc->kts", white, onehot, precision=lax.Precision.HIGHEST)
     panel, white_parts = psum_recv(
         partial_value, lax.axis_size("recv"), white_parts, lax.axis_size("recv") // 2
     )
-    rows, segs, nchan = white.shape
-    white_all = white_parts.transpose(1, 0, 2, 3).reshape(rows, width * segs, nchan)
+    white_all = white_parts
     nsrc = panel.shape[2]
-    panel = panel.reshape(rows, segs, nsrc // width, width).transpose(3, 0, 1, 2)
-    panel = lax.all_to_all(panel, group, 0, 0, tiled=True)
-    panel_own = panel.transpose(1, 0, 2, 3).reshape(rows, width * segs, nsrc // width)
+    panel = panel.reshape(rows, segs, nsrc // width, width).transpose(0, 3, 1, 2)
+    panel = panel.reshape(rows, width * segs, nsrc // width)
+    panel_own = lax.all_to_all(panel, group, 1, 1, tiled=True)
     factor = 1.0 / math.sqrt(total_segs)
     totals = cross_terms(panel_own, white_all, factor)
     out = lax.psum_scatter(totals, "zhi", scatter_dimension=0, tiled=True)

time: 128 us -> 132 us (1.031)
  the two profiles are of different devices: /device:TPU:18 before, /device:TPU:14 now
where the time goes in v10:
time: 132 us
  waiting for transfers between devices  76.9 us (58%)
  starting transfers between devices  20.5 us (16%)
  between operations  13.6 us (10%)
  local copies, waits for them, and re-layouts  9.73 us (7%)
  matrix products  8.27 us (6%)
  other arithmetic  2.89 us (2%)
    reduce_scatter x1, waiting for transfers between devices, on_device(): out = lax.psum_scatter(totals, 'zhi', scatter_dimension=0, tiled=True)  57.6 us
    ppermute x4, starting transfers between devices, psum_recv(): value = value + lax.ppermute(value, 'recv', pairs)  11.7 us
    ppermute x4, waiting for transfers between devices, psum_recv(): value = value + lax.ppermute(value, 'recv', pairs)  8.88 us
    all_to_all x1, waiting for transfers between devices, on_device(): white_parts = lax.all_to_all(spread, group, 1, 1, tiled=True)  6.92 us
    all_to_all x1, starting transfers between devices, on_device(): white_parts = lax.all_to_all(spread, group, 1, 1, tiled=True)  4.78 us
    all_to_all x1, starting transfers between devices, on_device(): panel_own = lax.all_to_all(panel, group, 1, 1, tiled=True)  4 us
    dot_general x1, matrix products, on_device(): lax.dot_general(basis, traces, (((1,), (2,)), ((), ())), preferred_elemen...  3.87 us
    all_to_all x1, waiting for transfers between devices, on_device(): panel_own = lax.all_to_all(panel, group, 1, 1, tiled=True)  3.49 us
  transfers between devices with their start and end apart: 7, of which 7 were waited for; matrix products, arithmetic and copies ran while one was open for 3% of the time, Pallas kernels for 0%

profile of v10, /device:TPU:14, one launch (start us, length us, event | category | flops | bytes accessed | tf_op | source)
XLA Modules:
  0.0 131.9 jit_solution(696949909126531547)
XLA Ops:
  6.5 0.7 convert_element_type.10
  7.2 3.9 %fusion.18 = f32[122,4,256]{2,0,1:T(8,128)S(1)} fusion(bf16[122,2048,1]{1,0,2:T(8,128)(2,1)} %constant.29, bf16[4,256,2048]{2,1,0:T(8,128)(2,1)} %param.4), kind=kOutput, calls=%fused_computation.30 | convolution fusion | flops 511705088 | bytes 5193728 | tf_op jit(solution)/shard_map/dot_general | solution.py:76
  11.1 0.1 fusion.17
  11.2 0.1 slice_multiply_fusion.1
  11.4 1.5 %broadcast_in_dim.2 = f32[122,4,4,256]{3,0,2,1:T(8,128)} broadcast(f32[122,4,256]{2,0,1:T(8,128)S(1)} %pad_maximum_fusion), dimensions={0,2,3} | broadcast | bytes 2498560 | tf_op jit(solution)/shard_map/broadcast_in_dim | solution.py:81
  12.9 0.0 copy-start.3
  12.9 0.0 copy-start.2
  12.9 4.8 %all-to-all-start = ((f32[122,16,256]{2,0,1:T(8,128)}), f32[122,16,256]{2,0,1:T(8,128)S(1)}, u32[]{:S(2)}, u32[]{:S(2)}) async-start(f32[122,16,256]{2,0,1:T(8,128)} %bitcast.25), calls=%async_computation | async-start | bytes 4194304 | tf_op jit(solution)/shard_map/all_to_all | solution.py:82
  17.7 0.0 copy-done.3
  17.7 0.4 fusion.10
  18.1 1.9 %collective-permute-start = (f32[122,4,32]{0,2,1:T(8,128)S(1)}, f32[122,4,32]{0,2,1:T(8,128)S(1)}, u32[]{:S(2)}, u32[]{:S(2)}) collective-permute-start(f32[122,4,32]{0,2,1:T(8,128)S(1)} %fusion.10), channel_id=1, source_target_pairs={{0,1},{1,0},{2,3},{3,2},{4,5},{5,4},{6,7},{7,6},{8,9},{9,8},{10,11... | collective-permute-start | bytes 187400 | tf_op jit(solution)/shard_map/ppermute | solution.py:59
  20.0 1.2 collective-permute-done
  21.3 2.4 %collective-permute-start.1 = (f32[122,4,32]{0,2,1:T(8,128)S(1)}, f32[122,4,32]{0,2,1:T(8,128)S(1)}, u32[]{:S(2)}, u32[]{:S(2)}) collective-permute-start(f32[122,4,32]{0,2,1:T(8,128)S(1)} %add.59), channel_id=1, source_target_pairs={{0,2},{1,3},{2,0},{3,1},{4,6},{5,7},{6,4},{7,5},{8,10},{9,11},{10,... | collective-permute-start | bytes 187400 | tf_op jit(solution)/shard_map/ppermute | solution.py:59
  23.6 3.8 %collective-permute-done.1 = f32[122,4,32]{0,2,1:T(8,128)S(1)} collective-permute-done((f32[122,4,32]{0,2,1:T(8,128)S(1)}, f32[122,4,32]{0,2,1:T(8,128)S(1)}, u32[]{:S(2)}, u32[]{:S(2)}) %collective-permute-start.1) | collective-permute-done | bytes 62496 | tf_op jit(solution)/shard_map/ppermute | solution.py:59
  27.4 4.2 %collective-permute-start.2 = (f32[122,4,32]{0,2,1:T(8,128)S(1)}, f32[122,4,32]{0,2,1:T(8,128)S(1)}, u32[]{:S(2)}, u32[]{:S(2)}) collective-permute-start(f32[122,4,32]{0,2,1:T(8,128)S(1)} %add.60), channel_id=1, source_target_pairs={{0,4},{1,5},{2,6},{3,7},{4,0},{5,1},{6,2},{7,3},{8,12},{9,13},{10,... | collective-permute-start | bytes 187400 | tf_op jit(solution)/shard_map/ppermute | solution.py:59
  31.6 3.5 %collective-permute-done.2 = f32[122,4,32]{0,2,1:T(8,128)S(1)} collective-permute-done((f32[122,4,32]{0,2,1:T(8,128)S(1)}, f32[122,4,32]{0,2,1:T(8,128)S(1)}, u32[]{:S(2)}, u32[]{:S(2)}) %collective-permute-start.2) | collective-permute-done | bytes 62496 | tf_op jit(solution)/shard_map/ppermute | solution.py:59
  35.1 6.9 %all-to-all-done = f32[122,16,256]{2,0,1:T(8,128)S(1)} async-done(((f32[122,16,256]{2,0,1:T(8,128)}), f32[122,16,256]{2,0,1:T(8,128)S(1)}, u32[]{:S(2)}, u32[]{:S(2)}) %all-to-all-start) | async-done | bytes 1998880 | tf_op jit(solution)/shard_map/all_to_all | solution.py:82
  42.0 0.0 copy-start
  42.0 3.3 %collective-permute-start.3 = (f32[122,4,32]{0,2,1:T(8,128)S(1)}, f32[122,4,32]{0,2,1:T(8,128)S(1)}, u32[]{:S(2)}, u32[]{:S(2)}) collective-permute-start(f32[122,4,32]{0,2,1:T(8,128)S(1)} %add.61), channel_id=1, source_target_pairs={{0,8},{1,9},{2,10},{3,11},{4,12},{5,13},{6,14},{7,15},{8,0},{9,1},... | collective-permute-start | bytes 187400 | tf_op jit(solution)/shard_map/ppermute | solution.py:59
  45.3 0.0 copy-done
  45.3 0.0 copy-done.2
  45.3 1.2 slice_select_fusion
  46.5 2.8 %copy.15 = f32[122,16,256]{2,1,0:T(8,128)S(1)} copy(f32[122,16,256]{2,0,1:T(8,128)} %copy-done) | data formatting | bytes 3997696 | tf_op jit(solution)/shard_map/optimization_barrier | solution.py:57
  49.3 0.4 collective-permute-done.3
  49.7 0.6 copy.12
  50.3 4.0 %all-to-all-start.1 = ((f32[122,16,8]{0,2,1:T(8,128)}), f32[122,16,8]{0,2,1:T(8,128)S(1)}, u32[]{:S(2)}, u32[]{:S(2)}) async-start(f32[122,16,8]{0,2,1:T(8,128)} %bitcast.5), calls=%async_computation.1 | async-start | bytes 131072 | tf_op jit(solution)/shard_map/all_to_all | solution.py:91
  54.3 0.0 reduce-scatter.2.cloned.1.call-start
  54.3 0.1 fusion.34
  54.4 3.5 %all-to-all-done.1 = f32[122,16,8]{0,2,1:T(8,128)S(1)} async-done(((f32[122,16,8]{0,2,1:T(8,128)}), f32[122,16,8]{0,2,1:T(8,128)S(1)}, u32[]{:S(2)}, u32[]{:S(2)}) %all-to-all-start.1) | async-done | bytes 62496 | tf_op jit(solution)/shard_map/all_to_all | solution.py:91
  57.9 0.1 slice.34
  58.0 0.2 copy.21
  58.2 0.6 slice_select_fusion.1
  58.8 1.0 copy.14
  59.8 0.7 fusion.4
  60.5 0.0 copy-start.1
  60.5 0.7 fusion.6
  61.2 0.5 copy-done.1
  61.8 1.3 fusion.1
  63.1 1.3 fusion
  64.4 0.1 maximum_multiply_fusion
  64.5 1.3 copy.19
  65.8 0.0 reduce-scatter.2.cloned.1.call-update
  65.8 57.6 %reduce-scatter.2.cloned.1.call-done = f32[1,2,64,256]{3,2,1,0:T(8,128)} async-done(((f32[8,2,64,256]{3,2,1,0:T(8,128)}), f32[1,2,64,256]{3,2,1,0:T(8,128)}) %reduce-scatter.2.cloned.1.call-update) | async-done | bytes 131088 | tf_op jit(solution)/shard_map/reduce_scatter | solution.py:94
  123.4 1.6 %copy.20 = f32[1,2,61,256]{3,1,2,0:T(2,128)} copy(f32[1,2,61,256]{3,2,1,0:T(8,128)} %bitcast.27) | data formatting | bytes 249856 | tf_op jit(solution)/shard_map/slice | solution.py:95
  (8 shorter events, 0.1 us)
Async XLA Ops:
  12.9 4.8 %copy-start.3 = (s32[32]{0:T(128)S(1)}, s32[32]{0:T(128)}, u32[]{:S(2)}) copy-start(s32[32]{0:T(128)} %param.6) | copy-start | bytes 388
  12.9 32.4 %copy-start.2 = (pred[64]{0:T(512)(128)(4,1)S(1)}, pred[64]{0:T(512)(128)(4,1)}, u32[]{:S(2)}) copy-start(pred[64]{0:T(512)(128)(4,1)} %constant.8.clone.1) | copy-start | bytes 196
  12.9 29.1 %all-to-all-start = ((f32[122,16,256]{2,0,1:T(8,128)}), f32[122,16,256]{2,0,1:T(8,128)S(1)}, u32[]{:S(2)}, u32[]{:S(2)}) async-start(f32[122,16,256]{2,0,1:T(8,128)} %bitcast.25), calls=%async_computation | async-start | bytes 4194304 | tf_op jit(solution)/shard_map/all_to_all | solution.py:82
  18.1 3.1 %collective-permute-start = (f32[122,4,32]{0,2,1:T(8,128)S(1)}, f32[122,4,32]{0,2,1:T(8,128)S(1)}, u32[]{:S(2)}, u32[]{:S(2)}) collective-permute-start(f32[122,4,32]{0,2,1:T(8,128)S(1)} %fusion.10), channel_id=1, source_target_pairs={{0,1},{1,0},{2,3},{3,2},{4,5},{5,4},{6,7},{7,6},{8,9},{9,8},{10,11... | collective-permute-start | bytes 187400 | tf_op jit(solution)/shard_map/ppermute | solution.py:59
  21.3 6.2 %collective-permute-start.1 = (f32[122,4,32]{0,2,1:T(8,128)S(1)}, f32[122,4,32]{0,2,1:T(8,128)S(1)}, u32[]{:S(2)}, u32[]{:S(2)}) collective-permute-start(f32[122,4,32]{0,2,1:T(8,128)S(1)} %add.59), channel_id=1, source_target_pairs={{0,2},{1,3},{2,0},{3,1},{4,6},{5,7},{6,4},{7,5},{8,10},{9,11},{10,... | collective-permute-start | bytes 187400 | tf_op jit(solution)/shard_map/ppermute | solution.py:59
  27.4 7.7 %collective-permute-start.2 = (f32[122,4,32]{0,2,1:T(8,128)S(1)}, f32[122,4,32]{0,2,1:T(8,128)S(1)}, u32[]{:S(2)}, u32[]{:S(2)}) collective-permute-start(f32[122,4,32]{0,2,1:T(8,128)S(1)} %add.60), channel_id=1, source_target_pairs={{0,4},{1,5},{2,6},{3,7},{4,0},{5,1},{6,2},{7,3},{8,12},{9,13},{10,... | collective-permute-start | bytes 187400 | tf_op jit(solution)/shard_map/ppermute | solution.py:59
  42.0 3.3 %copy-start = (f32[122,16,256]{2,0,1:T(8,128)}, f32[122,16,256]{2,0,1:T(8,128)S(1)}, u32[]{:S(2)}) copy-start(f32[122,16,256]{2,0,1:T(8,128)S(1)} %all-to-all-done) | copy-start | bytes 5996548
  42.0 7.7 %collective-permute-start.3 = (f32[122,4,32]{0,2,1:T(8,128)S(1)}, f32[122,4,32]{0,2,1:T(8,128)S(1)}, u32[]{:S(2)}, u32[]{:S(2)}) collective-permute-start(f32[122,4,32]{0,2,1:T(8,128)S(1)} %add.61), channel_id=1, source_target_pairs={{0,8},{1,9},{2,10},{3,11},{4,12},{5,13},{6,14},{7,15},{8,0},{9,1},... | collective-permute-start | bytes 187400 | tf_op jit(solution)/shard_map/ppermute | solution.py:59
  50.3 7.6 %all-to-all-start.1 = ((f32[122,16,8]{0,2,1:T(8,128)}), f32[122,16,8]{0,2,1:T(8,128)S(1)}, u32[]{:S(2)}, u32[]{:S(2)}) async-start(f32[122,16,8]{0,2,1:T(8,128)} %bitcast.5), calls=%async_computation.1 | async-start | bytes 131072 | tf_op jit(solution)/shard_map/all_to_all | solution.py:91
  54.3 69.1 %reduce-scatter.2.cloned.1.call-start = ((), (), s32[]{:S(2)}) async-start(), calls=%async_computation.3 | async-start | bytes 1179648 | tf_op jit(solution)/shard_map/reduce_scatter | solution.py:94
  60.5 1.2 copy-start.1
Sparse Core Ops, SparseCore 0:
  65.9 57.4 reduce-scatter.1

commit v11 on v9

--- a/solution.py
+++ b/solution.py
@@ -50,15 +50,13 @@
     return jnp.stack([real_sum, imag_sum], axis=1) * factor
 
 
-def psum_recv(value, size, passengers, hold_bit):
+def psum_recv(value, size, passengers):
     bit = 1
     while bit < size:
-        if bit == hold_bit:
-            value, passengers = lax.optimization_barrier((value, passengers))
         pairs = [(i, i ^ bit) for i in range(size)]
         value = value + lax.ppermute(value, "recv", pairs)
         bit *= 2
-    return value, passengers
+    return lax.optimization_barrier((value, passengers))
 
 
 def on_device(traces, valid, src_idx):
@@ -80,9 +78,7 @@
     spread = jnp.broadcast_to(white[None], (width,) + white.shape)
     white_parts = lax.all_to_all(spread, group, 0, 0, tiled=True)
     partial_value = jnp.einsum("ktc,sc->kts", white, onehot, precision=lax.Precision.HIGHEST)
-    panel, white_parts = psum_recv(
-        partial_value, lax.axis_size("recv"), white_parts, lax.axis_size("recv") // 2
-    )
+    panel, white_parts = psum_recv(partial_value, lax.axis_size("recv"), white_parts)
     rows, segs, nchan = white.shape
     white_all = white_parts.transpose(1, 0, 2, 3).reshape(rows, width * segs, nchan)
     nsrc = panel.shape[2]

time: 128 us -> 122 us (0.953)
  the two profiles are of different devices: /device:TPU:18 before, /device:TPU:10 now
where the time goes in v11:
time: 122 us
  waiting for transfers between devices  69 us (57%)
  starting transfers between devices  21.8 us (18%)
  between operations  13.6 us (11%)
  local copies, waits for them, and re-layouts  9.78 us (8%)
  matrix products  7.08 us (6%)
    reduce_scatter x1, waiting for transfers between devices, on_device(): out = lax.psum_scatter(totals, 'zhi', scatter_dimension=0, tiled=True)  53.9 us
    ppermute x4, waiting for transfers between devices, psum_recv(): value = value + lax.ppermute(value, 'recv', pairs)  15.1 us
    ppermute x4, starting transfers between devices, psum_recv(): value = value + lax.ppermute(value, 'recv', pairs)  12.9 us
    all_to_all x1, starting transfers between devices, on_device(): white_parts = lax.all_to_all(spread, group, 0, 0, tiled=True)  4.65 us
    all_to_all x1, starting transfers between devices, on_device(): panel = lax.all_to_all(panel, group, 0, 0, tiled=True)  4.2 us
    dot_general x1, matrix products, on_device(): lax.dot_general(basis, traces, (((1,), (2,)), ((), ())), preferred_elemen...  3.88 us
  transfers between devices with their start and end apart: 7, of which 5 were waited for; matrix products, arithmetic and copies ran while one was open for 3% of the time, Pallas kernels for 0%

profile of v11, /device:TPU:10, one launch (start us, length us, event | category | flops | bytes accessed | tf_op | source)
XLA Modules:
  0.0 121.6 jit_solution(15357538555764415926)
XLA Ops:
  6.5 0.0 copy-start
  6.5 3.9 %fusion.20 = f32[122,4,256]{2,0,1:T(8,128)S(1)} fusion(bf16[122,2048,1]{1,0,2:T(8,128)(2,1)} %constant.30, bf16[4,256,2048]{2,1,0:T(8,128)(2,1)} %param.4), kind=kOutput, calls=%fused_computation.31 | convolution fusion | flops 511705088 | bytes 5193728 | tf_op jit(solution)/shard_map/dot_general | solution.py:74
  10.4 0.1 fusion.17
  10.5 0.0 copy-done
  10.5 0.1 slice_multiply_fusion.1
  10.6 0.0 copy-start.1
  10.7 0.3 copy.14
  11.0 1.6 %broadcast_in_dim.2 = f32[4,122,4,256]{3,2,1,0:T(4,128)} broadcast(f32[122,4,256]{2,1,0:T(4,128)S(1)} %copy.14), dimensions={1,2,3} | broadcast | bytes 2498560 | tf_op jit(solution)/shard_map/broadcast_in_dim | solution.py:78
  12.6 4.6 %all-to-all-start = ((f32[4,122,4,256]{3,2,1,0:T(4,128)}), f32[4,122,4,256]{3,2,1,0:T(4,128)S(1)}, u32[]{:S(2)}, u32[]{:S(2)}) async-start(f32[4,122,4,256]{3,2,1,0:T(4,128)} %broadcast_in_dim.2), calls=%async_computation | async-start | bytes 3997696 | tf_op jit(solution)/shard_map/all_to_all | solution.py:79
  17.2 0.0 copy-done.1
  17.2 0.4 fusion.8
  17.7 1.9 %collective-permute-start = (f32[122,4,32]{0,2,1:T(8,128)S(1)}, f32[122,4,32]{0,2,1:T(8,128)S(1)}, u32[]{:S(2)}, u32[]{:S(2)}) collective-permute-start(f32[122,4,32]{0,2,1:T(8,128)S(1)} %fusion.8), channel_id=1, source_target_pairs={{0,1},{1,0},{2,3},{3,2},{4,5},{5,4},{6,7},{7,6},{8,9},{9,8},{10,11... | collective-permute-start | bytes 187400 | tf_op jit(solution)/shard_map/ppermute | solution.py:57
  19.6 1.2 %collective-permute-done = f32[122,4,32]{0,2,1:T(8,128)S(1)} collective-permute-done((f32[122,4,32]{0,2,1:T(8,128)S(1)}, f32[122,4,32]{0,2,1:T(8,128)S(1)}, u32[]{:S(2)}, u32[]{:S(2)}) %collective-permute-start) | collective-permute-done | bytes 62496 | tf_op jit(solution)/shard_map/ppermute | solution.py:57
  20.8 7.2 %collective-permute-start.1 = (f32[122,4,32]{0,2,1:T(8,128)S(1)}, f32[122,4,32]{0,2,1:T(8,128)S(1)}, u32[]{:S(2)}, u32[]{:S(2)}) collective-permute-start(f32[122,4,32]{0,2,1:T(8,128)S(1)} %add.63), channel_id=1, source_target_pairs={{0,2},{1,3},{2,0},{3,1},{4,6},{5,7},{6,4},{7,5},{8,10},{9,11},{10,... | collective-permute-start | bytes 187400 | tf_op jit(solution)/shard_map/ppermute | solution.py:57
  28.0 2.4 %collective-permute-done.1 = f32[122,4,32]{0,2,1:T(8,128)S(1)} collective-permute-done((f32[122,4,32]{0,2,1:T(8,128)S(1)}, f32[122,4,32]{0,2,1:T(8,128)S(1)}, u32[]{:S(2)}, u32[]{:S(2)}) %collective-permute-start.1) | collective-permute-done | bytes 62496 | tf_op jit(solution)/shard_map/ppermute | solution.py:57
  30.4 1.9 %collective-permute-start.2 = (f32[122,4,32]{0,2,1:T(8,128)S(1)}, f32[122,4,32]{0,2,1:T(8,128)S(1)}, u32[]{:S(2)}, u32[]{:S(2)}) collective-permute-start(f32[122,4,32]{0,2,1:T(8,128)S(1)} %add.64), channel_id=1, source_target_pairs={{0,4},{1,5},{2,6},{3,7},{4,0},{5,1},{6,2},{7,3},{8,12},{9,13},{10,... | collective-permute-start | bytes 187400 | tf_op jit(solution)/shard_map/ppermute | solution.py:57
  32.4 5.7 %collective-permute-done.2 = f32[122,4,32]{0,2,1:T(8,128)S(1)} collective-permute-done((f32[122,4,32]{0,2,1:T(8,128)S(1)}, f32[122,4,32]{0,2,1:T(8,128)S(1)}, u32[]{:S(2)}, u32[]{:S(2)}) %collective-permute-start.2) | collective-permute-done | bytes 62496 | tf_op jit(solution)/shard_map/ppermute | solution.py:57
  38.1 1.9 %collective-permute-start.3 = (f32[122,4,32]{0,2,1:T(8,128)S(1)}, f32[122,4,32]{0,2,1:T(8,128)S(1)}, u32[]{:S(2)}, u32[]{:S(2)}) collective-permute-start(f32[122,4,32]{0,2,1:T(8,128)S(1)} %add.65), channel_id=1, source_target_pairs={{0,8},{1,9},{2,10},{3,11},{4,12},{5,13},{6,14},{7,15},{8,0},{9,1},... | collective-permute-start | bytes 187400 | tf_op jit(solution)/shard_map/ppermute | solution.py:57
  40.0 5.7 %collective-permute-done.3 = f32[122,4,32]{0,2,1:T(8,128)S(1)} collective-permute-done((f32[122,4,32]{0,2,1:T(8,128)S(1)}, f32[122,4,32]{0,2,1:T(8,128)S(1)}, u32[]{:S(2)}, u32[]{:S(2)}) %collective-permute-start.3) | collective-permute-done | bytes 62496 | tf_op jit(solution)/shard_map/ppermute | solution.py:57
  45.8 0.0 all-to-all-done
  45.8 0.6 copy.23
  46.4 4.2 %all-to-all-start.1 = ((f32[4,122,4,8]{1,3,2,0:T(8,128)}), f32[4,122,4,8]{1,3,2,0:T(8,128)S(1)}, u32[]{:S(2)}, u32[]{:S(2)}) async-start(f32[4,122,4,8]{1,3,2,0:T(8,128)} %bitcast.34), calls=%async_computation.1 | async-start | bytes 131072 | tf_op jit(solution)/shard_map/all_to_all | solution.py:86
  50.6 0.0 reduce-scatter.2.cloned.1.call-start
  50.6 1.3 %fusion.18 = (f32[61,4,4,256]{3,2,0,1:T(4,128)S(1)}, f32[61,4,4,256]{3,2,0,1:T(4,128)}) fusion(f32[122,4,4,256]{3,2,0,1:T(4,128)S(1)} %bitcast.36), kind=kLoop, calls=%fused_computation.29 | loop fusion | bytes 3997696 | tf_op jit(solution)/shard_map/slice | solution.py:42
  51.9 0.3 copy.15
  52.2 0.3 slice.36
  52.6 1.5 %copy.18 = f32[61,4,4,256]{3,2,1,0:T(4,128)S(1)} copy(f32[61,4,4,256]{3,2,0,1:T(4,128)} %get-tuple-element.10) | data formatting | bytes 1998848 | tf_op jit(solution)/shard_map/slice | solution.py:43
  54.1 0.3 slice.40
  54.4 0.0 all-to-all-done.1
  54.5 0.1 fusion.19
  54.5 0.2 copy.17
  54.8 0.2 copy.19
  55.0 0.7 fusion.6
  55.7 0.7 fusion.4
  56.4 0.7 fusion.1
  57.1 0.7 fusion
  57.8 0.1 maximum_multiply_fusion
  57.9 1.3 %copy.20 = f32[8,2,64,256]{3,2,1,0:T(8,128)} copy(f32[8,2,64,256]{3,0,2,1:T(8,128)S(1)} %maximum_multiply_fusion) | data formatting | bytes 2097152 | tf_op jit(solution)/shard_map/mul | solution.py:50
  59.2 0.0 reduce-scatter.2.cloned.1.call-update
  59.3 53.9 %reduce-scatter.2.cloned.1.call-done = f32[1,2,64,256]{3,2,1,0:T(8,128)} async-done(((f32[8,2,64,256]{3,2,1,0:T(8,128)}), f32[1,2,64,256]{3,2,1,0:T(8,128)}) %reduce-scatter.2.cloned.1.call-update) | async-done | bytes 131088 | tf_op jit(solution)/shard_map/reduce_scatter | solution.py:90
  113.2 1.6 %copy.21 = f32[1,2,61,256]{3,1,2,0:T(2,128)} copy(f32[1,2,61,256]{3,2,1,0:T(8,128)} %bitcast.41) | data formatting | bytes 249856 | tf_op jit(solution)/shard_map/slice | solution.py:91
  (12 shorter events, 0.2 us)
Async XLA Ops:
  6.5 4.0 %copy-start = (s32[4,256]{1,0:T(4,128)S(1)}, s32[4,256]{1,0:T(4,128)}, u32[]{:S(2)}) copy-start(s32[4,256]{1,0:T(4,128)} %param.5) | copy-start | bytes 12292
  10.6 6.6 %copy-start.1 = (s32[32]{0:T(128)S(1)}, s32[32]{0:T(128)}, u32[]{:S(2)}) copy-start(s32[32]{0:T(128)} %param.6) | copy-start | bytes 388
  12.6 33.2 %all-to-all-start = ((f32[4,122,4,256]{3,2,1,0:T(4,128)}), f32[4,122,4,256]{3,2,1,0:T(4,128)S(1)}, u32[]{:S(2)}, u32[]{:S(2)}) async-start(f32[4,122,4,256]{3,2,1,0:T(4,128)} %broadcast_in_dim.2), calls=%async_computation | async-start | bytes 3997696 | tf_op jit(solution)/shard_map/all_to_all | solution.py:79
  17.7 3.1 %collective-permute-start = (f32[122,4,32]{0,2,1:T(8,128)S(1)}, f32[122,4,32]{0,2,1:T(8,128)S(1)}, u32[]{:S(2)}, u32[]{:S(2)}) collective-permute-start(f32[122,4,32]{0,2,1:T(8,128)S(1)} %fusion.8), channel_id=1, source_target_pairs={{0,1},{1,0},{2,3},{3,2},{4,5},{5,4},{6,7},{7,6},{8,9},{9,8},{10,11... | collective-permute-start | bytes 187400 | tf_op jit(solution)/shard_map/ppermute | solution.py:57
  20.8 9.6 %collective-permute-start.1 = (f32[122,4,32]{0,2,1:T(8,128)S(1)}, f32[122,4,32]{0,2,1:T(8,128)S(1)}, u32[]{:S(2)}, u32[]{:S(2)}) collective-permute-start(f32[122,4,32]{0,2,1:T(8,128)S(1)} %add.63), channel_id=1, source_target_pairs={{0,2},{1,3},{2,0},{3,1},{4,6},{5,7},{6,4},{7,5},{8,10},{9,11},{10,... | collective-permute-start | bytes 187400 | tf_op jit(solution)/shard_map/ppermute | solution.py:57
  30.4 7.7 %collective-permute-start.2 = (f32[122,4,32]{0,2,1:T(8,128)S(1)}, f32[122,4,32]{0,2,1:T(8,128)S(1)}, u32[]{:S(2)}, u32[]{:S(2)}) collective-permute-start(f32[122,4,32]{0,2,1:T(8,128)S(1)} %add.64), channel_id=1, source_target_pairs={{0,4},{1,5},{2,6},{3,7},{4,0},{5,1},{6,2},{7,3},{8,12},{9,13},{10,... | collective-permute-start | bytes 187400 | tf_op jit(solution)/shard_map/ppermute | solution.py:57
  38.1 7.7 %collective-permute-start.3 = (f32[122,4,32]{0,2,1:T(8,128)S(1)}, f32[122,4,32]{0,2,1:T(8,128)S(1)}, u32[]{:S(2)}, u32[]{:S(2)}) collective-permute-start(f32[122,4,32]{0,2,1:T(8,128)S(1)} %add.65), channel_id=1, source_target_pairs={{0,8},{1,9},{2,10},{3,11},{4,12},{5,13},{6,14},{7,15},{8,0},{9,1},... | collective-permute-start | bytes 187400 | tf_op jit(solution)/shard_map/ppermute | solution.py:57
  46.4 8.0 %all-to-all-start.1 = ((f32[4,122,4,8]{1,3,2,0:T(8,128)}), f32[4,122,4,8]{1,3,2,0:T(8,128)S(1)}, u32[]{:S(2)}, u32[]{:S(2)}) async-start(f32[4,122,4,8]{1,3,2,0:T(8,128)} %bitcast.34), calls=%async_computation.1 | async-start | bytes 131072 | tf_op jit(solution)/shard_map/all_to_all | solution.py:86
  50.6 62.5 %reduce-scatter.2.cloned.1.call-start = ((), (), s32[]{:S(2)}) async-start(), calls=%async_computation.3 | async-start | bytes 1179648 | tf_op jit(solution)/shard_map/reduce_scatter | solution.py:90
Sparse Core Ops, SparseCore 0:
  59.4 53.7 reduce-scatter.1

commit v12 on v11

--- a/solution.py
+++ b/solution.py
@@ -10,7 +10,6 @@
 NS = 2048
 NB = 61
 BIN0 = 40
-NB_PAD = 64
 
 
 def basis_table():
@@ -31,16 +30,12 @@
     return jnp.concatenate([real_part * scale, imag_part * scale], axis=0)
 
 
-def pad_bins(part):
-    return jnp.pad(part, [(0, NB_PAD - NB)] + [(0, 0)] * (part.ndim - 1))
-
-
 def cross_terms(panel, white, factor):
     high = lax.Precision.HIGHEST
-    src_real = pad_bins(panel[:NB])
-    src_imag = pad_bins(panel[NB:])
-    own_real = pad_bins(white[:NB])
-    own_imag = pad_bins(white[NB:])
+    src_real = panel[:NB]
+    src_imag = panel[NB:]
+    own_real = white[:NB]
+    own_imag = white[NB:]
     real_sum = jnp.einsum("fts,ftc->sfc", src_real, own_real, precision=high) + jnp.einsum(
         "fts,ftc->sfc", src_imag, own_imag, precision=high
     )
@@ -87,8 +82,8 @@
     panel_own = panel.transpose(1, 0, 2, 3).reshape(rows, width * segs, nsrc // width)
     factor = 1.0 / math.sqrt(total_segs)
     totals = cross_terms(panel_own, white_all, factor)
-    out = lax.psum_scatter(totals, "zhi", scatter_dimension=0, tiled=True)
-    return out[:, :, :NB, :]
+    arrived = lax.all_to_all(totals, "zhi", 0, 0, tiled=True)
+    return jnp.sum(arrived, axis=0, keepdims=True)
 
 
 def solution(mesh):

time: 122 us -> 117 us (0.959)
  the two profiles are of different devices: /device:TPU:10 before, /device:TPU:34 now
where the time goes in v12:
time: 117 us
  blocking collectives  62.4 us (53%)
  starting transfers between devices  20.9 us (18%)
  waiting for transfers between devices  16.9 us (14%)
  local copies, waits for them, and re-layouts  8.05 us (7%)
  matrix products  7.03 us (6%)
  other arithmetic  1.43 us (1%)
    all_to_all x1, blocking collectives, on_device(): arrived = lax.all_to_all(totals, 'zhi', 0, 0, tiled=True)  62.4 us
    ppermute x4, waiting for transfers between devices, psum_recv(): value = value + lax.ppermute(value, 'recv', pairs)  16.9 us
    all_to_all x1, starting transfers between devices, on_device(): white_parts = lax.all_to_all(spread, group, 0, 0, tiled=True)  9.02 us
    ppermute x4, starting transfers between devices, psum_recv(): value = value + lax.ppermute(value, 'recv', pairs)  7.68 us
    all_to_all x1, starting transfers between devices, on_device(): panel = lax.all_to_all(panel, group, 0, 0, tiled=True)  4.19 us
    dot_general x1, matrix products, on_device(): lax.dot_general(basis, traces, (((1,), (2,)), ((), ())), preferred_elemen...  3.87 us
  transfers between devices with their start and end apart: 6, of which 4 were waited for; matrix products, arithmetic and copies ran while one was open for 4% of the time, Pallas kernels for 0%

profile of v12, /device:TPU:34, one launch (start us, length us, event | category | flops | bytes accessed | tf_op | source)
XLA Modules:
  0.0 116.9 jit_solution(11307006943721281859)
XLA Ops:
  0.0 0.7 convert_element_type.4
  0.7 3.9 %fusion.10 = f32[122,4,256]{2,0,1:T(8,128)S(1)} fusion(bf16[122,2048,1]{1,0,2:T(8,128)(2,1)} %constant.20, bf16[4,256,2048]{2,1,0:T(8,128)(2,1)} %param.4), kind=kOutput, calls=%fused_computation.22 | convolution fusion | flops 511705088 | bytes 5193728 | tf_op jit(solution)/shard_map/dot_general | solution.py:69
  4.6 0.1 fusion.7
  4.7 0.1 slice_multiply_fusion.1
  4.8 0.0 copy-start
  4.8 0.3 copy.25
  5.2 1.6 %broadcast_in_dim.4 = f32[4,122,4,256]{3,2,1,0:T(4,128)} broadcast(f32[122,4,256]{2,1,0:T(4,128)S(1)} %copy.25), dimensions={1,2,3} | broadcast | bytes 2498560 | tf_op jit(solution)/shard_map/broadcast_in_dim | solution.py:73
  6.7 9.0 %all-to-all-start = ((f32[4,122,4,256]{3,2,1,0:T(4,128)}), f32[4,122,4,256]{3,2,1,0:T(4,128)S(1)}, u32[]{:S(2)}, u32[]{:S(2)}) async-start(f32[4,122,4,256]{3,2,1,0:T(4,128)} %broadcast_in_dim.4), calls=%async_computation | async-start | bytes 3997696 | tf_op jit(solution)/shard_map/all_to_all | solution.py:74
  15.8 0.0 copy-done
  15.8 0.4 fusion.2
  16.2 1.9 %collective-permute-start = (f32[122,4,32]{0,2,1:T(8,128)S(1)}, f32[122,4,32]{0,2,1:T(8,128)S(1)}, u32[]{:S(2)}, u32[]{:S(2)}) collective-permute-start(f32[122,4,32]{0,2,1:T(8,128)S(1)} %fusion.2), channel_id=1, source_target_pairs={{0,1},{1,0},{2,3},{3,2},{4,5},{5,4},{6,7},{7,6},{8,9},{9,8},{10,11... | collective-permute-start | bytes 187400 | tf_op jit(solution)/shard_map/ppermute | solution.py:52
  18.1 1.2 %collective-permute-done = f32[122,4,32]{0,2,1:T(8,128)S(1)} collective-permute-done((f32[122,4,32]{0,2,1:T(8,128)S(1)}, f32[122,4,32]{0,2,1:T(8,128)S(1)}, u32[]{:S(2)}, u32[]{:S(2)}) %collective-permute-start) | collective-permute-done | bytes 62496 | tf_op jit(solution)/shard_map/ppermute | solution.py:52
  19.3 1.9 %collective-permute-start.1 = (f32[122,4,32]{0,2,1:T(8,128)S(1)}, f32[122,4,32]{0,2,1:T(8,128)S(1)}, u32[]{:S(2)}, u32[]{:S(2)}) collective-permute-start(f32[122,4,32]{0,2,1:T(8,128)S(1)} %add.53), channel_id=1, source_target_pairs={{0,2},{1,3},{2,0},{3,1},{4,6},{5,7},{6,4},{7,5},{8,10},{9,11},{10,... | collective-permute-start | bytes 187400 | tf_op jit(solution)/shard_map/ppermute | solution.py:52
  21.3 4.2 %collective-permute-done.1 = f32[122,4,32]{0,2,1:T(8,128)S(1)} collective-permute-done((f32[122,4,32]{0,2,1:T(8,128)S(1)}, f32[122,4,32]{0,2,1:T(8,128)S(1)}, u32[]{:S(2)}, u32[]{:S(2)}) %collective-permute-start.1) | collective-permute-done | bytes 62496 | tf_op jit(solution)/shard_map/ppermute | solution.py:52
  25.5 1.9 %collective-permute-start.2 = (f32[122,4,32]{0,2,1:T(8,128)S(1)}, f32[122,4,32]{0,2,1:T(8,128)S(1)}, u32[]{:S(2)}, u32[]{:S(2)}) collective-permute-start(f32[122,4,32]{0,2,1:T(8,128)S(1)} %add.54), channel_id=1, source_target_pairs={{0,4},{1,5},{2,6},{3,7},{4,0},{5,1},{6,2},{7,3},{8,12},{9,13},{10,... | collective-permute-start | bytes 187400 | tf_op jit(solution)/shard_map/ppermute | solution.py:52
  27.4 5.7 %collective-permute-done.2 = f32[122,4,32]{0,2,1:T(8,128)S(1)} collective-permute-done((f32[122,4,32]{0,2,1:T(8,128)S(1)}, f32[122,4,32]{0,2,1:T(8,128)S(1)}, u32[]{:S(2)}, u32[]{:S(2)}) %collective-permute-start.2) | collective-permute-done | bytes 62496 | tf_op jit(solution)/shard_map/ppermute | solution.py:52
  33.2 1.9 %collective-permute-start.3 = (f32[122,4,32]{0,2,1:T(8,128)S(1)}, f32[122,4,32]{0,2,1:T(8,128)S(1)}, u32[]{:S(2)}, u32[]{:S(2)}) collective-permute-start(f32[122,4,32]{0,2,1:T(8,128)S(1)} %add.55), channel_id=1, source_target_pairs={{0,8},{1,9},{2,10},{3,11},{4,12},{5,13},{6,14},{7,15},{8,0},{9,1},... | collective-permute-start | bytes 187400 | tf_op jit(solution)/shard_map/ppermute | solution.py:52
  35.1 5.7 %collective-permute-done.3 = f32[122,4,32]{0,2,1:T(8,128)S(1)} collective-permute-done((f32[122,4,32]{0,2,1:T(8,128)S(1)}, f32[122,4,32]{0,2,1:T(8,128)S(1)}, u32[]{:S(2)}, u32[]{:S(2)}) %collective-permute-start.3) | collective-permute-done | bytes 62496 | tf_op jit(solution)/shard_map/ppermute | solution.py:52
  40.9 0.0 all-to-all-done
  40.9 0.6 copy.40
  41.5 4.2 %all-to-all-start.1 = ((f32[4,122,4,8]{1,3,2,0:T(8,128)}), f32[4,122,4,8]{1,3,2,0:T(8,128)S(1)}, u32[]{:S(2)}, u32[]{:S(2)}) async-start(f32[4,122,4,8]{1,3,2,0:T(8,128)} %bitcast.32), calls=%async_computation.1 | async-start | bytes 131072 | tf_op jit(solution)/shard_map/all_to_all | solution.py:81
  45.7 1.3 %fusion.8 = (f32[61,4,4,256]{3,2,0,1:T(4,128)S(1)}, f32[61,4,4,256]{3,2,0,1:T(4,128)}) fusion(f32[122,4,4,256]{3,2,0,1:T(4,128)S(1)} %bitcast.33), kind=kLoop, calls=%fused_computation.20 | loop fusion | bytes 3997696 | tf_op jit(solution)/shard_map/slice | solution.py:37
  47.0 0.3 copy.26
  47.3 0.3 slice.33
  47.7 1.5 %copy.29 = f32[61,4,4,256]{3,2,1,0:T(4,128)S(1)} copy(f32[61,4,4,256]{3,2,0,1:T(4,128)} %get-tuple-element.10) | data formatting | bytes 1998848 | tf_op jit(solution)/shard_map/slice | solution.py:38
  49.2 0.3 slice.37
  49.5 0.0 all-to-all-done.1
  49.5 0.1 fusion.9
  49.6 0.2 copy.28
  49.8 0.2 copy.30
  50.0 0.7 fusion.11
  50.7 0.7 fusion.12
  51.4 0.7 fusion
  52.1 0.7 fusion.1
  52.8 0.1 maximum_multiply_fusion
  52.9 0.5 copy.33
  53.4 62.4 %all_to_all.15 = f32[8,2,61,256]{3,1,2,0:T(2,128)S(1)} all-to-all(f32[8,2,61,256]{3,1,2,0:T(2,128)S(1)} %copy.33), channel_id=1, replica_groups=mesh['zhi'=8,'zlo'=2,'xlo'=2,'recv'=16] {'zhi'}, dimensions={0} | all-to-all | bytes 1998848 | tf_op jit(solution)/shard_map/all_to_all | solution.py:85
  115.7 0.4 reduce_sum.19
  116.2 0.7 copy.35
  (8 shorter events, 0.1 us)
Async XLA Ops:
  4.8 11.0 %copy-start = (s32[32]{0:T(128)S(1)}, s32[32]{0:T(128)}, u32[]{:S(2)}) copy-start(s32[32]{0:T(128)} %param.6) | copy-start | bytes 388
  6.7 34.1 %all-to-all-start = ((f32[4,122,4,256]{3,2,1,0:T(4,128)}), f32[4,122,4,256]{3,2,1,0:T(4,128)S(1)}, u32[]{:S(2)}, u32[]{:S(2)}) async-start(f32[4,122,4,256]{3,2,1,0:T(4,128)} %broadcast_in_dim.4), calls=%async_computation | async-start | bytes 3997696 | tf_op jit(solution)/shard_map/all_to_all | solution.py:74
  16.2 3.1 %collective-permute-start = (f32[122,4,32]{0,2,1:T(8,128)S(1)}, f32[122,4,32]{0,2,1:T(8,128)S(1)}, u32[]{:S(2)}, u32[]{:S(2)}) collective-permute-start(f32[122,4,32]{0,2,1:T(8,128)S(1)} %fusion.2), channel_id=1, source_target_pairs={{0,1},{1,0},{2,3},{3,2},{4,5},{5,4},{6,7},{7,6},{8,9},{9,8},{10,11... | collective-permute-start | bytes 187400 | tf_op jit(solution)/shard_map/ppermute | solution.py:52
  19.3 6.2 %collective-permute-start.1 = (f32[122,4,32]{0,2,1:T(8,128)S(1)}, f32[122,4,32]{0,2,1:T(8,128)S(1)}, u32[]{:S(2)}, u32[]{:S(2)}) collective-permute-start(f32[122,4,32]{0,2,1:T(8,128)S(1)} %add.53), channel_id=1, source_target_pairs={{0,2},{1,3},{2,0},{3,1},{4,6},{5,7},{6,4},{7,5},{8,10},{9,11},{10,... | collective-permute-start | bytes 187400 | tf_op jit(solution)/shard_map/ppermute | solution.py:52
  25.5 7.7 %collective-permute-start.2 = (f32[122,4,32]{0,2,1:T(8,128)S(1)}, f32[122,4,32]{0,2,1:T(8,128)S(1)}, u32[]{:S(2)}, u32[]{:S(2)}) collective-permute-start(f32[122,4,32]{0,2,1:T(8,128)S(1)} %add.54), channel_id=1, source_target_pairs={{0,4},{1,5},{2,6},{3,7},{4,0},{5,1},{6,2},{7,3},{8,12},{9,13},{10,... | collective-permute-start | bytes 187400 | tf_op jit(solution)/shard_map/ppermute | solution.py:52
  33.2 7.7 %collective-permute-start.3 = (f32[122,4,32]{0,2,1:T(8,128)S(1)}, f32[122,4,32]{0,2,1:T(8,128)S(1)}, u32[]{:S(2)}, u32[]{:S(2)}) collective-permute-start(f32[122,4,32]{0,2,1:T(8,128)S(1)} %add.55), channel_id=1, source_target_pairs={{0,8},{1,9},{2,10},{3,11},{4,12},{5,13},{6,14},{7,15},{8,0},{9,1},... | collective-permute-start | bytes 187400 | tf_op jit(solution)/shard_map/ppermute | solution.py:52
  41.5 8.0 %all-to-all-start.1 = ((f32[4,122,4,8]{1,3,2,0:T(8,128)}), f32[4,122,4,8]{1,3,2,0:T(8,128)S(1)}, u32[]{:S(2)}, u32[]{:S(2)}) async-start(f32[4,122,4,8]{1,3,2,0:T(8,128)} %bitcast.32), calls=%async_computation.1 | async-start | bytes 131072 | tf_op jit(solution)/shard_map/all_to_all | solution.py:81

commit v13 on v12

--- a/solution.py
+++ b/solution.py
@@ -83,7 +83,10 @@
     factor = 1.0 / math.sqrt(total_segs)
     totals = cross_terms(panel_own, white_all, factor)
     arrived = lax.all_to_all(totals, "zhi", 0, 0, tiled=True)
-    return jnp.sum(arrived, axis=0, keepdims=True)
+    total = arrived[0:1]
+    for k in range(1, arrived.shape[0]):
+        total = total + arrived[k : k + 1]
+    return total
 
 
 def solution(mesh):

time: 117 us -> 117 us (level)
  no operation moved by 1% of the time
where the time goes in v13:
time: 117 us
  blocking collectives  62.4 us (53%)
  starting transfers between devices  20.9 us (18%)
  waiting for transfers between devices  16.9 us (14%)
  local copies, waits for them, and re-layouts  7.28 us (6%)
  matrix products  7.03 us (6%)
  other arithmetic  1.89 us (2%)
    all_to_all x1, blocking collectives, on_device(): arrived = lax.all_to_all(totals, 'zhi', 0, 0, tiled=True)  62.4 us
    ppermute x4, waiting for transfers between devices, psum_recv(): value = value + lax.ppermute(value, 'recv', pairs)  16.9 us
    all_to_all x1, starting transfers between devices, on_device(): white_parts = lax.all_to_all(spread, group, 0, 0, tiled=True)  9.02 us
    ppermute x4, starting transfers between devices, psum_recv(): value = value + lax.ppermute(value, 'recv', pairs)  7.68 us
    all_to_all x1, starting transfers between devices, on_device(): panel = lax.all_to_all(panel, group, 0, 0, tiled=True)  4.19 us
    dot_general x1, matrix products, on_device(): lax.dot_general(basis, traces, (((1,), (2,)), ((), ())), preferred_elemen...  3.87 us
  transfers between devices with their start and end apart: 6, of which 4 were waited for; matrix products, arithmetic and copies ran while one was open for 4% of the time, Pallas kernels for 0%

profile of v13, /device:TPU:34, one launch (start us, length us, event | category | flops | bytes accessed | tf_op | source)
XLA Modules:
  0.0 116.6 jit_solution(902796753059118663)
XLA Ops:
  0.0 0.7 convert_element_type.4
  0.7 3.9 %fusion.10 = f32[122,4,256]{2,0,1:T(8,128)S(1)} fusion(bf16[122,2048,1]{1,0,2:T(8,128)(2,1)} %constant.20, bf16[4,256,2048]{2,1,0:T(8,128)(2,1)} %param.4), kind=kOutput, calls=%fused_computation.28 | convolution fusion | flops 511705088 | bytes 5193728 | tf_op jit(solution)/shard_map/dot_general | solution.py:69
  4.6 0.1 fusion.7
  4.7 0.1 slice_multiply_fusion.1
  4.8 0.0 copy-start
  4.8 0.3 copy.26
  5.2 1.6 %broadcast_in_dim.2 = f32[4,122,4,256]{3,2,1,0:T(4,128)} broadcast(f32[122,4,256]{2,1,0:T(4,128)S(1)} %copy.26), dimensions={1,2,3} | broadcast | bytes 2498560 | tf_op jit(solution)/shard_map/broadcast_in_dim | solution.py:73
  6.7 9.0 %all-to-all-start = ((f32[4,122,4,256]{3,2,1,0:T(4,128)}), f32[4,122,4,256]{3,2,1,0:T(4,128)S(1)}, u32[]{:S(2)}, u32[]{:S(2)}) async-start(f32[4,122,4,256]{3,2,1,0:T(4,128)} %broadcast_in_dim.2), calls=%async_computation | async-start | bytes 3997696 | tf_op jit(solution)/shard_map/all_to_all | solution.py:74
  15.8 0.0 copy-done
  15.8 0.4 fusion.2
  16.2 1.9 %collective-permute-start = (f32[122,4,32]{0,2,1:T(8,128)S(1)}, f32[122,4,32]{0,2,1:T(8,128)S(1)}, u32[]{:S(2)}, u32[]{:S(2)}) collective-permute-start(f32[122,4,32]{0,2,1:T(8,128)S(1)} %fusion.2), channel_id=1, source_target_pairs={{0,1},{1,0},{2,3},{3,2},{4,5},{5,4},{6,7},{7,6},{8,9},{9,8},{10,11... | collective-permute-start | bytes 187400 | tf_op jit(solution)/shard_map/ppermute | solution.py:52
  18.1 1.2 %collective-permute-done = f32[122,4,32]{0,2,1:T(8,128)S(1)} collective-permute-done((f32[122,4,32]{0,2,1:T(8,128)S(1)}, f32[122,4,32]{0,2,1:T(8,128)S(1)}, u32[]{:S(2)}, u32[]{:S(2)}) %collective-permute-start) | collective-permute-done | bytes 62496 | tf_op jit(solution)/shard_map/ppermute | solution.py:52
  19.3 1.9 %collective-permute-start.1 = (f32[122,4,32]{0,2,1:T(8,128)S(1)}, f32[122,4,32]{0,2,1:T(8,128)S(1)}, u32[]{:S(2)}, u32[]{:S(2)}) collective-permute-start(f32[122,4,32]{0,2,1:T(8,128)S(1)} %add.74), channel_id=1, source_target_pairs={{0,2},{1,3},{2,0},{3,1},{4,6},{5,7},{6,4},{7,5},{8,10},{9,11},{10,... | collective-permute-start | bytes 187400 | tf_op jit(solution)/shard_map/ppermute | solution.py:52
  21.3 4.2 %collective-permute-done.1 = f32[122,4,32]{0,2,1:T(8,128)S(1)} collective-permute-done((f32[122,4,32]{0,2,1:T(8,128)S(1)}, f32[122,4,32]{0,2,1:T(8,128)S(1)}, u32[]{:S(2)}, u32[]{:S(2)}) %collective-permute-start.1) | collective-permute-done | bytes 62496 | tf_op jit(solution)/shard_map/ppermute | solution.py:52
  25.5 1.9 %collective-permute-start.2 = (f32[122,4,32]{0,2,1:T(8,128)S(1)}, f32[122,4,32]{0,2,1:T(8,128)S(1)}, u32[]{:S(2)}, u32[]{:S(2)}) collective-permute-start(f32[122,4,32]{0,2,1:T(8,128)S(1)} %add.75), channel_id=1, source_target_pairs={{0,4},{1,5},{2,6},{3,7},{4,0},{5,1},{6,2},{7,3},{8,12},{9,13},{10,... | collective-permute-start | bytes 187400 | tf_op jit(solution)/shard_map/ppermute | solution.py:52
  27.4 5.7 %collective-permute-done.2 = f32[122,4,32]{0,2,1:T(8,128)S(1)} collective-permute-done((f32[122,4,32]{0,2,1:T(8,128)S(1)}, f32[122,4,32]{0,2,1:T(8,128)S(1)}, u32[]{:S(2)}, u32[]{:S(2)}) %collective-permute-start.2) | collective-permute-done | bytes 62496 | tf_op jit(solution)/shard_map/ppermute | solution.py:52
  33.2 1.9 %collective-permute-start.3 = (f32[122,4,32]{0,2,1:T(8,128)S(1)}, f32[122,4,32]{0,2,1:T(8,128)S(1)}, u32[]{:S(2)}, u32[]{:S(2)}) collective-permute-start(f32[122,4,32]{0,2,1:T(8,128)S(1)} %add.76), channel_id=1, source_target_pairs={{0,8},{1,9},{2,10},{3,11},{4,12},{5,13},{6,14},{7,15},{8,0},{9,1},... | collective-permute-start | bytes 187400 | tf_op jit(solution)/shard_map/ppermute | solution.py:52
  35.1 5.7 %collective-permute-done.3 = f32[122,4,32]{0,2,1:T(8,128)S(1)} collective-permute-done((f32[122,4,32]{0,2,1:T(8,128)S(1)}, f32[122,4,32]{0,2,1:T(8,128)S(1)}, u32[]{:S(2)}, u32[]{:S(2)}) %collective-permute-start.3) | collective-permute-done | bytes 62496 | tf_op jit(solution)/shard_map/ppermute | solution.py:52
  40.9 0.0 all-to-all-done
  40.9 0.6 copy.36
  41.5 4.2 %all-to-all-start.1 = ((f32[4,122,4,8]{1,3,2,0:T(8,128)}), f32[4,122,4,8]{1,3,2,0:T(8,128)S(1)}, u32[]{:S(2)}, u32[]{:S(2)}) async-start(f32[4,122,4,8]{1,3,2,0:T(8,128)} %bitcast.29), calls=%async_computation.1 | async-start | bytes 131072 | tf_op jit(solution)/shard_map/all_to_all | solution.py:81
  45.7 1.3 %fusion.8 = (f32[61,4,4,256]{3,2,0,1:T(4,128)S(1)}, f32[61,4,4,256]{3,2,0,1:T(4,128)}) fusion(f32[122,4,4,256]{3,2,0,1:T(4,128)S(1)} %bitcast.30), kind=kLoop, calls=%fused_computation.26 | loop fusion | bytes 3997696 | tf_op jit(solution)/shard_map/slice | solution.py:37
  47.0 0.3 copy.27
  47.3 0.3 slice.57
  47.6 1.5 %copy.30 = f32[61,4,4,256]{3,2,1,0:T(4,128)S(1)} copy(f32[61,4,4,256]{3,2,0,1:T(4,128)} %get-tuple-element.10) | data formatting | bytes 1998848 | tf_op jit(solution)/shard_map/slice | solution.py:38
  49.2 0.3 slice.61
  49.5 0.0 all-to-all-done.1
  49.5 0.1 fusion.9
  49.6 0.2 copy.29
  49.8 0.2 copy.31
  50.0 0.7 fusion.11
  50.7 0.7 fusion.12
  51.4 0.7 fusion
  52.1 0.7 fusion.1
  52.7 0.1 maximum_multiply_fusion
  52.8 0.5 copy.34
  53.4 62.4 %all_to_all.15 = f32[8,2,61,256]{3,1,2,0:T(2,128)S(1)} all-to-all(f32[8,2,61,256]{3,1,2,0:T(2,128)S(1)} %copy.34), channel_id=1, replica_groups=mesh['zhi'=8,'zlo'=2,'xlo'=2,'recv'=16] {'zhi'}, dimensions={0} | all-to-all | bytes 1998848 | tf_op jit(solution)/shard_map/all_to_all | solution.py:85
  115.7 0.8 slice_add_fusion
  (7 shorter events, 0.1 us)
Async XLA Ops:
  4.8 11.0 %copy-start = (s32[32]{0:T(128)S(1)}, s32[32]{0:T(128)}, u32[]{:S(2)}) copy-start(s32[32]{0:T(128)} %param.6) | copy-start | bytes 388
  6.7 34.1 %all-to-all-start = ((f32[4,122,4,256]{3,2,1,0:T(4,128)}), f32[4,122,4,256]{3,2,1,0:T(4,128)S(1)}, u32[]{:S(2)}, u32[]{:S(2)}) async-start(f32[4,122,4,256]{3,2,1,0:T(4,128)} %broadcast_in_dim.2), calls=%async_computation | async-start | bytes 3997696 | tf_op jit(solution)/shard_map/all_to_all | solution.py:74
  16.2 3.1 %collective-permute-start = (f32[122,4,32]{0,2,1:T(8,128)S(1)}, f32[122,4,32]{0,2,1:T(8,128)S(1)}, u32[]{:S(2)}, u32[]{:S(2)}) collective-permute-start(f32[122,4,32]{0,2,1:T(8,128)S(1)} %fusion.2), channel_id=1, source_target_pairs={{0,1},{1,0},{2,3},{3,2},{4,5},{5,4},{6,7},{7,6},{8,9},{9,8},{10,11... | collective-permute-start | bytes 187400 | tf_op jit(solution)/shard_map/ppermute | solution.py:52
  19.3 6.2 %collective-permute-start.1 = (f32[122,4,32]{0,2,1:T(8,128)S(1)}, f32[122,4,32]{0,2,1:T(8,128)S(1)}, u32[]{:S(2)}, u32[]{:S(2)}) collective-permute-start(f32[122,4,32]{0,2,1:T(8,128)S(1)} %add.74), channel_id=1, source_target_pairs={{0,2},{1,3},{2,0},{3,1},{4,6},{5,7},{6,4},{7,5},{8,10},{9,11},{10,... | collective-permute-start | bytes 187400 | tf_op jit(solution)/shard_map/ppermute | solution.py:52
  25.5 7.7 %collective-permute-start.2 = (f32[122,4,32]{0,2,1:T(8,128)S(1)}, f32[122,4,32]{0,2,1:T(8,128)S(1)}, u32[]{:S(2)}, u32[]{:S(2)}) collective-permute-start(f32[122,4,32]{0,2,1:T(8,128)S(1)} %add.75), channel_id=1, source_target_pairs={{0,4},{1,5},{2,6},{3,7},{4,0},{5,1},{6,2},{7,3},{8,12},{9,13},{10,... | collective-permute-start | bytes 187400 | tf_op jit(solution)/shard_map/ppermute | solution.py:52
  33.2 7.7 %collective-permute-start.3 = (f32[122,4,32]{0,2,1:T(8,128)S(1)}, f32[122,4,32]{0,2,1:T(8,128)S(1)}, u32[]{:S(2)}, u32[]{:S(2)}) collective-permute-start(f32[122,4,32]{0,2,1:T(8,128)S(1)} %add.76), channel_id=1, source_target_pairs={{0,8},{1,9},{2,10},{3,11},{4,12},{5,13},{6,14},{7,15},{8,0},{9,1},... | collective-permute-start | bytes 187400 | tf_op jit(solution)/shard_map/ppermute | solution.py:52
  41.5 8.0 %all-to-all-start.1 = ((f32[4,122,4,8]{1,3,2,0:T(8,128)}), f32[4,122,4,8]{1,3,2,0:T(8,128)S(1)}, u32[]{:S(2)}, u32[]{:S(2)}) async-start(f32[4,122,4,8]{1,3,2,0:T(8,128)} %bitcast.29), calls=%async_computation.1 | async-start | bytes 131072 | tf_op jit(solution)/shard_map/all_to_all | solution.py:81

commit v14 on v13

--- a/solution.py
+++ b/solution.py
@@ -21,12 +21,12 @@
     return jnp.asarray(table.astype(jnp.bfloat16))
 
 
-def whiten_block(spec, valid_float):
+def whiten_block(spec, valid):
     real_part = spec[:NB]
     imag_part = spec[NB:]
     power = real_part * real_part + imag_part * imag_part
     level = jnp.sum(power, axis=0) / (2.0 * NB)
-    scale = lax.rsqrt(power + level[None] + 1e-06) * valid_float[None]
+    scale = jnp.where(valid[None] != 0, lax.rsqrt(power + level[None] + 1e-06), 0.0)
     return jnp.concatenate([real_part * scale, imag_part * scale], axis=0)
 
 
@@ -61,7 +61,6 @@
     width = lax.axis_size("zlo") * lax.axis_size("xlo")
     total_segs = seg_count * width * lax.axis_size("zhi")
     basis = basis_table()
-    valid_float = valid.astype(jnp.float32)
     offset = lax.axis_index("recv") * chan_count
     onehot = (src_idx[:, None] == offset + jnp.arange(chan_count, dtype=jnp.int32)[None, :]).astype(
         jnp.float32
@@ -69,7 +68,7 @@
     spec = lax.dot_general(
         basis, traces, (((1,), (2,)), ((), ())), preferred_element_type=jnp.float32
     )
-    white = whiten_block(spec, valid_float)
+    white = whiten_block(spec, valid)
     spread = jnp.broadcast_to(white[None], (width,) + white.shape)
     white_parts = lax.all_to_all(spread, group, 0, 0, tiled=True)
     partial_value = jnp.einsum("ktc,sc->kts", white, onehot, precision=lax.Precision.HIGHEST)

time: 117 us -> 117 us (level)
  the two profiles are of different devices: /device:TPU:34 before, /device:TPU:58 now
where the time goes in v14:
time: 117 us
  blocking collectives  66 us (56%)
  starting transfers between devices  22.4 us (19%)
  waiting for transfers between devices  11.7 us (10%)
  local copies, waits for them, and re-layouts  7.28 us (6%)
  matrix products  7.03 us (6%)
  other arithmetic  1.89 us (2%)
    all_to_all x1, blocking collectives, on_device(): arrived = lax.all_to_all(totals, 'zhi', 0, 0, tiled=True)  66 us
    ppermute x4, starting transfers between devices, psum_recv(): value = value + lax.ppermute(value, 'recv', pairs)  14 us
    ppermute x4, waiting for transfers between devices, psum_recv(): value = value + lax.ppermute(value, 'recv', pairs)  11.7 us
    all_to_all x1, starting transfers between devices, on_device(): panel = lax.all_to_all(panel, group, 0, 0, tiled=True)  4.19 us
    all_to_all x1, starting transfers between devices, on_device(): white_parts = lax.all_to_all(spread, group, 0, 0, tiled=True)  4.19 us
    dot_general x1, matrix products, on_device(): lax.dot_general(basis, traces, (((1,), (2,)), ((), ())), preferred_elemen...  3.87 us
  transfers between devices with their start and end apart: 6, of which 4 were waited for; matrix products, arithmetic and copies ran while one was open for 4% of the time, Pallas kernels for 0%

profile of v14, /device:TPU:58, one launch (start us, length us, event | category | flops | bytes accessed | tf_op | source)
XLA Modules:
  0.0 116.6 jit_solution(9358145377716084531)
XLA Ops:
  0.0 0.7 broadcast_compare_fusion
  0.7 3.9 %fusion.10 = f32[122,4,256]{2,0,1:T(8,128)S(1)} fusion(bf16[122,2048,1]{1,0,2:T(8,128)(2,1)} %constant.22, bf16[4,256,2048]{2,1,0:T(8,128)(2,1)} %param.4), kind=kOutput, calls=%fused_computation.29 | convolution fusion | flops 511705088 | bytes 5193728 | tf_op jit(solution)/shard_map/dot_general | solution.py:68
  4.6 0.1 fusion.7
  4.7 0.1 slice_multiply_fusion.1
  4.8 0.0 copy-start
  4.8 0.3 copy.26
  5.2 1.6 %broadcast_in_dim.24 = f32[4,122,4,256]{3,2,1,0:T(4,128)} broadcast(f32[122,4,256]{2,1,0:T(4,128)S(1)} %copy.26), dimensions={1,2,3} | broadcast | bytes 2498560 | tf_op jit(solution)/shard_map/broadcast_in_dim | solution.py:72
  6.7 4.2 %all-to-all-start = ((f32[4,122,4,256]{3,2,1,0:T(4,128)}), f32[4,122,4,256]{3,2,1,0:T(4,128)S(1)}, u32[]{:S(2)}, u32[]{:S(2)}) async-start(f32[4,122,4,256]{3,2,1,0:T(4,128)} %broadcast_in_dim.24), calls=%async_computation | async-start | bytes 3997696 | tf_op jit(solution)/shard_map/all_to_all | solution.py:73
  10.9 0.0 copy-done
  10.9 0.4 fusion.2
  11.3 1.9 %collective-permute-start = (f32[122,4,32]{0,2,1:T(8,128)S(1)}, f32[122,4,32]{0,2,1:T(8,128)S(1)}, u32[]{:S(2)}, u32[]{:S(2)}) collective-permute-start(f32[122,4,32]{0,2,1:T(8,128)S(1)} %fusion.2), channel_id=1, source_target_pairs={{0,1},{1,0},{2,3},{3,2},{4,5},{5,4},{6,7},{7,6},{8,9},{9,8},{10,11... | collective-permute-start | bytes 187400 | tf_op jit(solution)/shard_map/ppermute | solution.py:52
  13.3 1.2 %collective-permute-done = f32[122,4,32]{0,2,1:T(8,128)S(1)} collective-permute-done((f32[122,4,32]{0,2,1:T(8,128)S(1)}, f32[122,4,32]{0,2,1:T(8,128)S(1)}, u32[]{:S(2)}, u32[]{:S(2)}) %collective-permute-start) | collective-permute-done | bytes 62496 | tf_op jit(solution)/shard_map/ppermute | solution.py:52
  14.5 2.7 %collective-permute-start.1 = (f32[122,4,32]{0,2,1:T(8,128)S(1)}, f32[122,4,32]{0,2,1:T(8,128)S(1)}, u32[]{:S(2)}, u32[]{:S(2)}) collective-permute-start(f32[122,4,32]{0,2,1:T(8,128)S(1)} %add.74), channel_id=1, source_target_pairs={{0,2},{1,3},{2,0},{3,1},{4,6},{5,7},{6,4},{7,5},{8,10},{9,11},{10,... | collective-permute-start | bytes 187400 | tf_op jit(solution)/shard_map/ppermute | solution.py:52
  17.2 3.5 %collective-permute-done.1 = f32[122,4,32]{0,2,1:T(8,128)S(1)} collective-permute-done((f32[122,4,32]{0,2,1:T(8,128)S(1)}, f32[122,4,32]{0,2,1:T(8,128)S(1)}, u32[]{:S(2)}, u32[]{:S(2)}) %collective-permute-start.1) | collective-permute-done | bytes 62496 | tf_op jit(solution)/shard_map/ppermute | solution.py:52
  20.7 6.6 %collective-permute-start.2 = (f32[122,4,32]{0,2,1:T(8,128)S(1)}, f32[122,4,32]{0,2,1:T(8,128)S(1)}, u32[]{:S(2)}, u32[]{:S(2)}) collective-permute-start(f32[122,4,32]{0,2,1:T(8,128)S(1)} %add.75), channel_id=1, source_target_pairs={{0,4},{1,5},{2,6},{3,7},{4,0},{5,1},{6,2},{7,3},{8,12},{9,13},{10,... | collective-permute-start | bytes 187400 | tf_op jit(solution)/shard_map/ppermute | solution.py:52
  27.3 2.2 %collective-permute-done.2 = f32[122,4,32]{0,2,1:T(8,128)S(1)} collective-permute-done((f32[122,4,32]{0,2,1:T(8,128)S(1)}, f32[122,4,32]{0,2,1:T(8,128)S(1)}, u32[]{:S(2)}, u32[]{:S(2)}) %collective-permute-start.2) | collective-permute-done | bytes 62496 | tf_op jit(solution)/shard_map/ppermute | solution.py:52
  29.5 2.9 %collective-permute-start.3 = (f32[122,4,32]{0,2,1:T(8,128)S(1)}, f32[122,4,32]{0,2,1:T(8,128)S(1)}, u32[]{:S(2)}, u32[]{:S(2)}) collective-permute-start(f32[122,4,32]{0,2,1:T(8,128)S(1)} %add.76), channel_id=1, source_target_pairs={{0,8},{1,9},{2,10},{3,11},{4,12},{5,13},{6,14},{7,15},{8,0},{9,1},... | collective-permute-start | bytes 187400 | tf_op jit(solution)/shard_map/ppermute | solution.py:52
  32.4 4.8 %collective-permute-done.3 = f32[122,4,32]{0,2,1:T(8,128)S(1)} collective-permute-done((f32[122,4,32]{0,2,1:T(8,128)S(1)}, f32[122,4,32]{0,2,1:T(8,128)S(1)}, u32[]{:S(2)}, u32[]{:S(2)}) %collective-permute-start.3) | collective-permute-done | bytes 62496 | tf_op jit(solution)/shard_map/ppermute | solution.py:52
  37.2 0.0 all-to-all-done
  37.2 0.6 copy.36
  37.8 4.2 %all-to-all-start.1 = ((f32[4,122,4,8]{1,3,2,0:T(8,128)}), f32[4,122,4,8]{1,3,2,0:T(8,128)S(1)}, u32[]{:S(2)}, u32[]{:S(2)}) async-start(f32[4,122,4,8]{1,3,2,0:T(8,128)} %bitcast.29), calls=%async_computation.1 | async-start | bytes 131072 | tf_op jit(solution)/shard_map/all_to_all | solution.py:80
  42.0 1.3 %fusion.8 = (f32[61,4,4,256]{3,2,0,1:T(4,128)S(1)}, f32[61,4,4,256]{3,2,0,1:T(4,128)}) fusion(f32[122,4,4,256]{3,2,0,1:T(4,128)S(1)} %bitcast.30), kind=kLoop, calls=%fused_computation.27 | loop fusion | bytes 3997696 | tf_op jit(solution)/shard_map/slice | solution.py:37
  43.3 0.3 copy.27
  43.6 0.3 slice.57
  44.0 1.5 %copy.30 = f32[61,4,4,256]{3,2,1,0:T(4,128)S(1)} copy(f32[61,4,4,256]{3,2,0,1:T(4,128)} %get-tuple-element.10) | data formatting | bytes 1998848 | tf_op jit(solution)/shard_map/slice | solution.py:38
  45.5 0.3 slice.61
  45.8 0.0 all-to-all-done.1
  45.8 0.1 fusion.9
  45.9 0.2 copy.29
  46.1 0.2 copy.31
  46.3 0.7 fusion.11
  47.0 0.7 fusion.12
  47.7 0.7 fusion
  48.4 0.7 fusion.1
  49.1 0.1 maximum_multiply_fusion
  49.2 0.5 copy.34
  49.7 66.0 %all_to_all.15 = f32[8,2,61,256]{3,1,2,0:T(2,128)S(1)} all-to-all(f32[8,2,61,256]{3,1,2,0:T(2,128)S(1)} %copy.34), channel_id=1, replica_groups=mesh['zhi'=8,'zlo'=2,'xlo'=2,'recv'=16] {'zhi'}, dimensions={0} | all-to-all | bytes 1998848 | tf_op jit(solution)/shard_map/all_to_all | solution.py:84
  115.7 0.8 slice_add_fusion
  (7 shorter events, 0.1 us)
Async XLA Ops:
  4.8 6.2 %copy-start = (s32[32]{0:T(128)S(1)}, s32[32]{0:T(128)}, u32[]{:S(2)}) copy-start(s32[32]{0:T(128)} %param.6) | copy-start | bytes 388
  6.7 30.5 %all-to-all-start = ((f32[4,122,4,256]{3,2,1,0:T(4,128)}), f32[4,122,4,256]{3,2,1,0:T(4,128)S(1)}, u32[]{:S(2)}, u32[]{:S(2)}) async-start(f32[4,122,4,256]{3,2,1,0:T(4,128)} %broadcast_in_dim.24), calls=%async_computation | async-start | bytes 3997696 | tf_op jit(solution)/shard_map/all_to_all | solution.py:73
  11.3 3.1 %collective-permute-start = (f32[122,4,32]{0,2,1:T(8,128)S(1)}, f32[122,4,32]{0,2,1:T(8,128)S(1)}, u32[]{:S(2)}, u32[]{:S(2)}) collective-permute-start(f32[122,4,32]{0,2,1:T(8,128)S(1)} %fusion.2), channel_id=1, source_target_pairs={{0,1},{1,0},{2,3},{3,2},{4,5},{5,4},{6,7},{7,6},{8,9},{9,8},{10,11... | collective-permute-start | bytes 187400 | tf_op jit(solution)/shard_map/ppermute | solution.py:52
  14.5 6.2 %collective-permute-start.1 = (f32[122,4,32]{0,2,1:T(8,128)S(1)}, f32[122,4,32]{0,2,1:T(8,128)S(1)}, u32[]{:S(2)}, u32[]{:S(2)}) collective-permute-start(f32[122,4,32]{0,2,1:T(8,128)S(1)} %add.74), channel_id=1, source_target_pairs={{0,2},{1,3},{2,0},{3,1},{4,6},{5,7},{6,4},{7,5},{8,10},{9,11},{10,... | collective-permute-start | bytes 187400 | tf_op jit(solution)/shard_map/ppermute | solution.py:52
  20.7 8.8 %collective-permute-start.2 = (f32[122,4,32]{0,2,1:T(8,128)S(1)}, f32[122,4,32]{0,2,1:T(8,128)S(1)}, u32[]{:S(2)}, u32[]{:S(2)}) collective-permute-start(f32[122,4,32]{0,2,1:T(8,128)S(1)} %add.75), channel_id=1, source_target_pairs={{0,4},{1,5},{2,6},{3,7},{4,0},{5,1},{6,2},{7,3},{8,12},{9,13},{10,... | collective-permute-start | bytes 187400 | tf_op jit(solution)/shard_map/ppermute | solution.py:52
  29.5 7.7 %collective-permute-start.3 = (f32[122,4,32]{0,2,1:T(8,128)S(1)}, f32[122,4,32]{0,2,1:T(8,128)S(1)}, u32[]{:S(2)}, u32[]{:S(2)}) collective-permute-start(f32[122,4,32]{0,2,1:T(8,128)S(1)} %add.76), channel_id=1, source_target_pairs={{0,8},{1,9},{2,10},{3,11},{4,12},{5,13},{6,14},{7,15},{8,0},{9,1},... | collective-permute-start | bytes 187400 | tf_op jit(solution)/shard_map/ppermute | solution.py:52
  37.8 8.0 %all-to-all-start.1 = ((f32[4,122,4,8]{1,3,2,0:T(8,128)}), f32[4,122,4,8]{1,3,2,0:T(8,128)S(1)}, u32[]{:S(2)}, u32[]{:S(2)}) async-start(f32[4,122,4,8]{1,3,2,0:T(8,128)} %bitcast.29), calls=%async_computation.1 | async-start | bytes 131072 | tf_op jit(solution)/shard_map/all_to_all | solution.py:80

commit v15 on v13

--- a/solution.py
+++ b/solution.py
@@ -42,7 +42,7 @@
     imag_sum = jnp.einsum("fts,ftc->sfc", src_real, own_imag, precision=high) - jnp.einsum(
         "fts,ftc->sfc", src_imag, own_real, precision=high
     )
-    return jnp.stack([real_sum, imag_sum], axis=1) * factor
+    return jnp.concatenate([real_sum, imag_sum], axis=1) * factor
 
 
 def psum_recv(value, size, passengers):
@@ -86,7 +86,7 @@
     total = arrived[0:1]
     for k in range(1, arrived.shape[0]):
         total = total + arrived[k : k + 1]
-    return total
+    return total.reshape(1, 2, NB, total.shape[2])
 
 
 def solution(mesh):

time: 117 us -> 119 us (1.017)
  blocking collectives: 62.4 us -> 64 us
    all_to_all x1, blocking collectives: 62.4 us -> 64 us  [on_device(): arrived = lax.all_to_all(totals, 'zhi', 0, 0, tiled=True)]
where the time goes in v15:
time: 119 us; the launch traced here: 118 us
  blocking collectives  64 us (54%)
  starting transfers between devices  20.9 us (18%)
  waiting for transfers between devices  16.9 us (14%)
  local copies, waits for them, and re-layouts  7.92 us (7%)
  matrix products  7.03 us (6%)
    all_to_all x1, blocking collectives, on_device(): arrived = lax.all_to_all(totals, 'zhi', 0, 0, tiled=True)  64 us
    ppermute x4, waiting for transfers between devices, psum_recv(): value = value + lax.ppermute(value, 'recv', pairs)  16.9 us
    all_to_all x1, starting transfers between devices, on_device(): white_parts = lax.all_to_all(spread, group, 0, 0, tiled=True)  9.02 us
    ppermute x4, starting transfers between devices, psum_recv(): value = value + lax.ppermute(value, 'recv', pairs)  7.68 us
    all_to_all x1, starting transfers between devices, on_device(): panel = lax.all_to_all(panel, group, 0, 0, tiled=True)  4.19 us
    dot_general x1, matrix products, on_device(): lax.dot_general(basis, traces, (((1,), (2,)), ((), ())), preferred_elemen...  3.87 us
  transfers between devices with their start and end apart: 6, of which 4 were waited for; matrix products, arithmetic and copies ran while one was open for 4% of the time, Pallas kernels for 0%

profile of v15, /device:TPU:34, one launch (start us, length us, event | category | flops | bytes accessed | tf_op | source)
XLA Modules:
  0.0 118.1 jit_solution(12711342850349293240)
XLA Ops:
  0.0 0.7 convert_element_type.4
  0.7 3.9 %fusion.10 = f32[122,4,256]{2,0,1:T(8,128)S(1)} fusion(bf16[122,2048,1]{1,0,2:T(8,128)(2,1)} %constant.20, bf16[4,256,2048]{2,1,0:T(8,128)(2,1)} %param.4), kind=kOutput, calls=%fused_computation.28 | convolution fusion | flops 511705088 | bytes 5193728 | tf_op jit(solution)/shard_map/dot_general | solution.py:69
  4.6 0.1 fusion.7
  4.7 0.1 slice_multiply_fusion.1
  4.8 0.0 copy-start
  4.8 0.3 copy.26
  5.2 1.6 %broadcast_in_dim.2 = f32[4,122,4,256]{3,2,1,0:T(4,128)} broadcast(f32[122,4,256]{2,1,0:T(4,128)S(1)} %copy.26), dimensions={1,2,3} | broadcast | bytes 2498560 | tf_op jit(solution)/shard_map/broadcast_in_dim | solution.py:73
  6.7 9.0 %all-to-all-start = ((f32[4,122,4,256]{3,2,1,0:T(4,128)}), f32[4,122,4,256]{3,2,1,0:T(4,128)S(1)}, u32[]{:S(2)}, u32[]{:S(2)}) async-start(f32[4,122,4,256]{3,2,1,0:T(4,128)} %broadcast_in_dim.2), calls=%async_computation | async-start | bytes 3997696 | tf_op jit(solution)/shard_map/all_to_all | solution.py:74
  15.8 0.0 copy-done
  15.8 0.4 fusion.2
  16.2 1.9 %collective-permute-start = (f32[122,4,32]{0,2,1:T(8,128)S(1)}, f32[122,4,32]{0,2,1:T(8,128)S(1)}, u32[]{:S(2)}, u32[]{:S(2)}) collective-permute-start(f32[122,4,32]{0,2,1:T(8,128)S(1)} %fusion.2), channel_id=1, source_target_pairs={{0,1},{1,0},{2,3},{3,2},{4,5},{5,4},{6,7},{7,6},{8,9},{9,8},{10,11... | collective-permute-start | bytes 187400 | tf_op jit(solution)/shard_map/ppermute | solution.py:52
  18.1 1.2 %collective-permute-done = f32[122,4,32]{0,2,1:T(8,128)S(1)} collective-permute-done((f32[122,4,32]{0,2,1:T(8,128)S(1)}, f32[122,4,32]{0,2,1:T(8,128)S(1)}, u32[]{:S(2)}, u32[]{:S(2)}) %collective-permute-start) | collective-permute-done | bytes 62496 | tf_op jit(solution)/shard_map/ppermute | solution.py:52
  19.3 1.9 %collective-permute-start.1 = (f32[122,4,32]{0,2,1:T(8,128)S(1)}, f32[122,4,32]{0,2,1:T(8,128)S(1)}, u32[]{:S(2)}, u32[]{:S(2)}) collective-permute-start(f32[122,4,32]{0,2,1:T(8,128)S(1)} %add.74), channel_id=1, source_target_pairs={{0,2},{1,3},{2,0},{3,1},{4,6},{5,7},{6,4},{7,5},{8,10},{9,11},{10,... | collective-permute-start | bytes 187400 | tf_op jit(solution)/shard_map/ppermute | solution.py:52
  21.3 4.2 %collective-permute-done.1 = f32[122,4,32]{0,2,1:T(8,128)S(1)} collective-permute-done((f32[122,4,32]{0,2,1:T(8,128)S(1)}, f32[122,4,32]{0,2,1:T(8,128)S(1)}, u32[]{:S(2)}, u32[]{:S(2)}) %collective-permute-start.1) | collective-permute-done | bytes 62496 | tf_op jit(solution)/shard_map/ppermute | solution.py:52
  25.5 1.9 %collective-permute-start.2 = (f32[122,4,32]{0,2,1:T(8,128)S(1)}, f32[122,4,32]{0,2,1:T(8,128)S(1)}, u32[]{:S(2)}, u32[]{:S(2)}) collective-permute-start(f32[122,4,32]{0,2,1:T(8,128)S(1)} %add.75), channel_id=1, source_target_pairs={{0,4},{1,5},{2,6},{3,7},{4,0},{5,1},{6,2},{7,3},{8,12},{9,13},{10,... | collective-permute-start | bytes 187400 | tf_op jit(solution)/shard_map/ppermute | solution.py:52
  27.4 5.7 %collective-permute-done.2 = f32[122,4,32]{0,2,1:T(8,128)S(1)} collective-permute-done((f32[122,4,32]{0,2,1:T(8,128)S(1)}, f32[122,4,32]{0,2,1:T(8,128)S(1)}, u32[]{:S(2)}, u32[]{:S(2)}) %collective-permute-start.2) | collective-permute-done | bytes 62496 | tf_op jit(solution)/shard_map/ppermute | solution.py:52
  33.2 1.9 %collective-permute-start.3 = (f32[122,4,32]{0,2,1:T(8,128)S(1)}, f32[122,4,32]{0,2,1:T(8,128)S(1)}, u32[]{:S(2)}, u32[]{:S(2)}) collective-permute-start(f32[122,4,32]{0,2,1:T(8,128)S(1)} %add.76), channel_id=1, source_target_pairs={{0,8},{1,9},{2,10},{3,11},{4,12},{5,13},{6,14},{7,15},{8,0},{9,1},... | collective-permute-start | bytes 187400 | tf_op jit(solution)/shard_map/ppermute | solution.py:52
  35.1 5.7 %collective-permute-done.3 = f32[122,4,32]{0,2,1:T(8,128)S(1)} collective-permute-done((f32[122,4,32]{0,2,1:T(8,128)S(1)}, f32[122,4,32]{0,2,1:T(8,128)S(1)}, u32[]{:S(2)}, u32[]{:S(2)}) %collective-permute-start.3) | collective-permute-done | bytes 62496 | tf_op jit(solution)/shard_map/ppermute | solution.py:52
  40.9 0.0 all-to-all-done
  40.9 0.6 copy.37
  41.5 4.2 %all-to-all-start.1 = ((f32[4,122,4,8]{1,3,2,0:T(8,128)}), f32[4,122,4,8]{1,3,2,0:T(8,128)S(1)}, u32[]{:S(2)}, u32[]{:S(2)}) async-start(f32[4,122,4,8]{1,3,2,0:T(8,128)} %bitcast.25), calls=%async_computation.1 | async-start | bytes 131072 | tf_op jit(solution)/shard_map/all_to_all | solution.py:81
  45.7 1.3 %fusion.8 = (f32[61,4,4,256]{3,2,0,1:T(4,128)S(1)}, f32[61,4,4,256]{3,2,0,1:T(4,128)}) fusion(f32[122,4,4,256]{3,2,0,1:T(4,128)S(1)} %bitcast.26), kind=kLoop, calls=%fused_computation.26 | loop fusion | bytes 3997696 | tf_op jit(solution)/shard_map/slice | solution.py:37
  47.0 0.3 copy.27
  47.3 0.3 slice.57
  47.6 1.5 %copy.30 = f32[61,4,4,256]{3,2,1,0:T(4,128)S(1)} copy(f32[61,4,4,256]{3,2,0,1:T(4,128)} %get-tuple-element.10) | data formatting | bytes 1998848 | tf_op jit(solution)/shard_map/slice | solution.py:38
  49.2 0.3 slice.61
  49.5 0.0 all-to-all-done.1
  49.5 0.1 fusion.9
  49.6 0.2 copy.29
  49.8 0.2 copy.31
  50.0 0.7 fusion.11
  50.7 0.7 fusion.12
  51.4 0.7 fusion
  52.1 0.7 fusion.1
  52.7 0.1 maximum_multiply_fusion
  52.8 0.3 copy.34
  53.2 64.0 %all_to_all.15 = f32[8,122,256]{2,1,0:T(8,128)S(1)} all-to-all(f32[8,122,256]{2,1,0:T(8,128)S(1)} %copy.34), channel_id=1, replica_groups=mesh['zhi'=8,'zlo'=2,'xlo'=2,'recv'=16] {'zhi'}, dimensions={0} | all-to-all | bytes 1998848 | tf_op jit(solution)/shard_map/all_to_all | solution.py:85
  117.2 0.1 slice_add_fusion
  117.2 0.1 reshape.24
  117.4 0.7 copy.35
  (7 shorter events, 0.1 us)
Async XLA Ops:
  4.8 11.0 %copy-start = (s32[32]{0:T(128)S(1)}, s32[32]{0:T(128)}, u32[]{:S(2)}) copy-start(s32[32]{0:T(128)} %param.6) | copy-start | bytes 388
  6.7 34.1 %all-to-all-start = ((f32[4,122,4,256]{3,2,1,0:T(4,128)}), f32[4,122,4,256]{3,2,1,0:T(4,128)S(1)}, u32[]{:S(2)}, u32[]{:S(2)}) async-start(f32[4,122,4,256]{3,2,1,0:T(4,128)} %broadcast_in_dim.2), calls=%async_computation | async-start | bytes 3997696 | tf_op jit(solution)/shard_map/all_to_all | solution.py:74
  16.2 3.1 %collective-permute-start = (f32[122,4,32]{0,2,1:T(8,128)S(1)}, f32[122,4,32]{0,2,1:T(8,128)S(1)}, u32[]{:S(2)}, u32[]{:S(2)}) collective-permute-start(f32[122,4,32]{0,2,1:T(8,128)S(1)} %fusion.2), channel_id=1, source_target_pairs={{0,1},{1,0},{2,3},{3,2},{4,5},{5,4},{6,7},{7,6},{8,9},{9,8},{10,11... | collective-permute-start | bytes 187400 | tf_op jit(solution)/shard_map/ppermute | solution.py:52
  19.3 6.2 %collective-permute-start.1 = (f32[122,4,32]{0,2,1:T(8,128)S(1)}, f32[122,4,32]{0,2,1:T(8,128)S(1)}, u32[]{:S(2)}, u32[]{:S(2)}) collective-permute-start(f32[122,4,32]{0,2,1:T(8,128)S(1)} %add.74), channel_id=1, source_target_pairs={{0,2},{1,3},{2,0},{3,1},{4,6},{5,7},{6,4},{7,5},{8,10},{9,11},{10,... | collective-permute-start | bytes 187400 | tf_op jit(solution)/shard_map/ppermute | solution.py:52
  25.5 7.7 %collective-permute-start.2 = (f32[122,4,32]{0,2,1:T(8,128)S(1)}, f32[122,4,32]{0,2,1:T(8,128)S(1)}, u32[]{:S(2)}, u32[]{:S(2)}) collective-permute-start(f32[122,4,32]{0,2,1:T(8,128)S(1)} %add.75), channel_id=1, source_target_pairs={{0,4},{1,5},{2,6},{3,7},{4,0},{5,1},{6,2},{7,3},{8,12},{9,13},{10,... | collective-permute-start | bytes 187400 | tf_op jit(solution)/shard_map/ppermute | solution.py:52
  33.2 7.7 %collective-permute-start.3 = (f32[122,4,32]{0,2,1:T(8,128)S(1)}, f32[122,4,32]{0,2,1:T(8,128)S(1)}, u32[]{:S(2)}, u32[]{:S(2)}) collective-permute-start(f32[122,4,32]{0,2,1:T(8,128)S(1)} %add.76), channel_id=1, source_target_pairs={{0,8},{1,9},{2,10},{3,11},{4,12},{5,13},{6,14},{7,15},{8,0},{9,1},... | collective-permute-start | bytes 187400 | tf_op jit(solution)/shard_map/ppermute | solution.py:52
  41.5 8.0 %all-to-all-start.1 = ((f32[4,122,4,8]{1,3,2,0:T(8,128)}), f32[4,122,4,8]{1,3,2,0:T(8,128)S(1)}, u32[]{:S(2)}, u32[]{:S(2)}) async-start(f32[4,122,4,8]{1,3,2,0:T(8,128)} %bitcast.25), calls=%async_computation.1 | async-start | bytes 131072 | tf_op jit(solution)/shard_map/all_to_all | solution.py:81

commit v16 on v13

--- a/solution.py
+++ b/solution.py
@@ -31,7 +31,7 @@
 
 
 def cross_terms(panel, white, factor):
-    high = lax.Precision.HIGHEST
+    high = lax.Precision.HIGH
     src_real = panel[:NB]
     src_imag = panel[NB:]
     own_real = white[:NB]

time: 117 us -> 116 us (level)
  matrix products: 7.03 us -> 5.78 us
where the time goes in v16:
time: 116 us; the launch traced here: 115 us
  blocking collectives  62.4 us (54%)
  starting transfers between devices  20.9 us (18%)
  waiting for transfers between devices  16.9 us (15%)
  local copies, waits for them, and re-layouts  7.28 us (6%)
  matrix products  5.78 us (5%)
  other arithmetic  1.89 us (2%)
    all_to_all x1, blocking collectives, on_device(): arrived = lax.all_to_all(totals, 'zhi', 0, 0, tiled=True)  62.4 us
    ppermute x4, waiting for transfers between devices, psum_recv(): value = value + lax.ppermute(value, 'recv', pairs)  16.9 us
    all_to_all x1, starting transfers between devices, on_device(): white_parts = lax.all_to_all(spread, group, 0, 0, tiled=True)  9.02 us
    ppermute x4, starting transfers between devices, psum_recv(): value = value + lax.ppermute(value, 'recv', pairs)  7.68 us
    all_to_all x1, starting transfers between devices, on_device(): panel = lax.all_to_all(panel, group, 0, 0, tiled=True)  4.19 us
    dot_general x1, matrix products, on_device(): lax.dot_general(basis, traces, (((1,), (2,)), ((), ())), preferred_elemen...  3.87 us
  transfers between devices with their start and end apart: 6, of which 4 were waited for; matrix products, arithmetic and copies ran while one was open for 4% of the time, Pallas kernels for 0%

profile of v16, /device:TPU:34, one launch (start us, length us, event | category | flops | bytes accessed | tf_op | source)
XLA Modules:
  0.0 115.3 jit_solution(10181801063952929997)
XLA Ops:
  0.0 0.7 convert_element_type.4
  0.7 3.9 %fusion.10 = f32[122,4,256]{2,0,1:T(8,128)S(1)} fusion(bf16[122,2048,1]{1,0,2:T(8,128)(2,1)} %constant.20, bf16[4,256,2048]{2,1,0:T(8,128)(2,1)} %param.4), kind=kOutput, calls=%fused_computation.28 | convolution fusion | flops 511705088 | bytes 5193728 | tf_op jit(solution)/shard_map/dot_general | solution.py:69
  4.6 0.1 fusion.7
  4.7 0.1 slice_multiply_fusion.1
  4.8 0.0 copy-start
  4.8 0.3 copy.26
  5.2 1.6 %broadcast_in_dim.2 = f32[4,122,4,256]{3,2,1,0:T(4,128)} broadcast(f32[122,4,256]{2,1,0:T(4,128)S(1)} %copy.26), dimensions={1,2,3} | broadcast | bytes 2498560 | tf_op jit(solution)/shard_map/broadcast_in_dim | solution.py:73
  6.7 9.0 %all-to-all-start = ((f32[4,122,4,256]{3,2,1,0:T(4,128)}), f32[4,122,4,256]{3,2,1,0:T(4,128)S(1)}, u32[]{:S(2)}, u32[]{:S(2)}) async-start(f32[4,122,4,256]{3,2,1,0:T(4,128)} %broadcast_in_dim.2), calls=%async_computation | async-start | bytes 3997696 | tf_op jit(solution)/shard_map/all_to_all | solution.py:74
  15.8 0.0 copy-done
  15.8 0.4 fusion.2
  16.2 1.9 %collective-permute-start = (f32[122,4,32]{0,2,1:T(8,128)S(1)}, f32[122,4,32]{0,2,1:T(8,128)S(1)}, u32[]{:S(2)}, u32[]{:S(2)}) collective-permute-start(f32[122,4,32]{0,2,1:T(8,128)S(1)} %fusion.2), channel_id=1, source_target_pairs={{0,1},{1,0},{2,3},{3,2},{4,5},{5,4},{6,7},{7,6},{8,9},{9,8},{10,11... | collective-permute-start | bytes 187400 | tf_op jit(solution)/shard_map/ppermute | solution.py:52
  18.1 1.2 %collective-permute-done = f32[122,4,32]{0,2,1:T(8,128)S(1)} collective-permute-done((f32[122,4,32]{0,2,1:T(8,128)S(1)}, f32[122,4,32]{0,2,1:T(8,128)S(1)}, u32[]{:S(2)}, u32[]{:S(2)}) %collective-permute-start) | collective-permute-done | bytes 62496 | tf_op jit(solution)/shard_map/ppermute | solution.py:52
  19.3 1.9 %collective-permute-start.1 = (f32[122,4,32]{0,2,1:T(8,128)S(1)}, f32[122,4,32]{0,2,1:T(8,128)S(1)}, u32[]{:S(2)}, u32[]{:S(2)}) collective-permute-start(f32[122,4,32]{0,2,1:T(8,128)S(1)} %add.74), channel_id=1, source_target_pairs={{0,2},{1,3},{2,0},{3,1},{4,6},{5,7},{6,4},{7,5},{8,10},{9,11},{10,... | collective-permute-start | bytes 187400 | tf_op jit(solution)/shard_map/ppermute | solution.py:52
  21.3 4.2 %collective-permute-done.1 = f32[122,4,32]{0,2,1:T(8,128)S(1)} collective-permute-done((f32[122,4,32]{0,2,1:T(8,128)S(1)}, f32[122,4,32]{0,2,1:T(8,128)S(1)}, u32[]{:S(2)}, u32[]{:S(2)}) %collective-permute-start.1) | collective-permute-done | bytes 62496 | tf_op jit(solution)/shard_map/ppermute | solution.py:52
  25.5 1.9 %collective-permute-start.2 = (f32[122,4,32]{0,2,1:T(8,128)S(1)}, f32[122,4,32]{0,2,1:T(8,128)S(1)}, u32[]{:S(2)}, u32[]{:S(2)}) collective-permute-start(f32[122,4,32]{0,2,1:T(8,128)S(1)} %add.75), channel_id=1, source_target_pairs={{0,4},{1,5},{2,6},{3,7},{4,0},{5,1},{6,2},{7,3},{8,12},{9,13},{10,... | collective-permute-start | bytes 187400 | tf_op jit(solution)/shard_map/ppermute | solution.py:52
  27.4 5.7 %collective-permute-done.2 = f32[122,4,32]{0,2,1:T(8,128)S(1)} collective-permute-done((f32[122,4,32]{0,2,1:T(8,128)S(1)}, f32[122,4,32]{0,2,1:T(8,128)S(1)}, u32[]{:S(2)}, u32[]{:S(2)}) %collective-permute-start.2) | collective-permute-done | bytes 62496 | tf_op jit(solution)/shard_map/ppermute | solution.py:52
  33.2 1.9 %collective-permute-start.3 = (f32[122,4,32]{0,2,1:T(8,128)S(1)}, f32[122,4,32]{0,2,1:T(8,128)S(1)}, u32[]{:S(2)}, u32[]{:S(2)}) collective-permute-start(f32[122,4,32]{0,2,1:T(8,128)S(1)} %add.76), channel_id=1, source_target_pairs={{0,8},{1,9},{2,10},{3,11},{4,12},{5,13},{6,14},{7,15},{8,0},{9,1},... | collective-permute-start | bytes 187400 | tf_op jit(solution)/shard_map/ppermute | solution.py:52
  35.1 5.7 %collective-permute-done.3 = f32[122,4,32]{0,2,1:T(8,128)S(1)} collective-permute-done((f32[122,4,32]{0,2,1:T(8,128)S(1)}, f32[122,4,32]{0,2,1:T(8,128)S(1)}, u32[]{:S(2)}, u32[]{:S(2)}) %collective-permute-start.3) | collective-permute-done | bytes 62496 | tf_op jit(solution)/shard_map/ppermute | solution.py:52
  40.9 0.0 all-to-all-done
  40.9 0.6 copy.36
  41.5 4.2 %all-to-all-start.1 = ((f32[4,122,4,8]{1,3,2,0:T(8,128)}), f32[4,122,4,8]{1,3,2,0:T(8,128)S(1)}, u32[]{:S(2)}, u32[]{:S(2)}) async-start(f32[4,122,4,8]{1,3,2,0:T(8,128)} %bitcast.29), calls=%async_computation.1 | async-start | bytes 131072 | tf_op jit(solution)/shard_map/all_to_all | solution.py:81
  45.7 1.3 %fusion.8 = (f32[61,4,4,256]{3,2,0,1:T(4,128)S(1)}, f32[61,4,4,256]{3,2,0,1:T(4,128)}) fusion(f32[122,4,4,256]{3,2,0,1:T(4,128)S(1)} %bitcast.30), kind=kLoop, calls=%fused_computation.26 | loop fusion | bytes 3997696 | tf_op jit(solution)/shard_map/slice | solution.py:37
  47.0 0.3 copy.27
  47.3 0.3 slice.57
  47.6 1.5 %copy.30 = f32[61,4,4,256]{3,2,1,0:T(4,128)S(1)} copy(f32[61,4,4,256]{3,2,0,1:T(4,128)} %get-tuple-element.10) | data formatting | bytes 1998848 | tf_op jit(solution)/shard_map/slice | solution.py:38
  49.2 0.3 slice.61
  49.5 0.0 all-to-all-done.1
  49.5 0.1 fusion.9
  49.6 0.2 copy.29
  49.8 0.2 copy.31
  50.0 0.4 fusion.11
  50.4 0.4 fusion.12
  50.7 0.4 fusion
  51.1 0.4 fusion.1
  51.5 0.1 maximum_multiply_fusion
  51.6 0.5 copy.34
  52.1 62.4 %all_to_all.15 = f32[8,2,61,256]{3,1,2,0:T(2,128)S(1)} all-to-all(f32[8,2,61,256]{3,1,2,0:T(2,128)S(1)} %copy.34), channel_id=1, replica_groups=mesh['zhi'=8,'zlo'=2,'xlo'=2,'recv'=16] {'zhi'}, dimensions={0} | all-to-all | bytes 1998848 | tf_op jit(solution)/shard_map/all_to_all | solution.py:85
  114.5 0.8 slice_add_fusion
  (7 shorter events, 0.1 us)
Async XLA Ops:
  4.8 11.0 %copy-start = (s32[32]{0:T(128)S(1)}, s32[32]{0:T(128)}, u32[]{:S(2)}) copy-start(s32[32]{0:T(128)} %param.6) | copy-start | bytes 388
  6.7 34.1 %all-to-all-start = ((f32[4,122,4,256]{3,2,1,0:T(4,128)}), f32[4,122,4,256]{3,2,1,0:T(4,128)S(1)}, u32[]{:S(2)}, u32[]{:S(2)}) async-start(f32[4,122,4,256]{3,2,1,0:T(4,128)} %broadcast_in_dim.2), calls=%async_computation | async-start | bytes 3997696 | tf_op jit(solution)/shard_map/all_to_all | solution.py:74
  16.2 3.1 %collective-permute-start = (f32[122,4,32]{0,2,1:T(8,128)S(1)}, f32[122,4,32]{0,2,1:T(8,128)S(1)}, u32[]{:S(2)}, u32[]{:S(2)}) collective-permute-start(f32[122,4,32]{0,2,1:T(8,128)S(1)} %fusion.2), channel_id=1, source_target_pairs={{0,1},{1,0},{2,3},{3,2},{4,5},{5,4},{6,7},{7,6},{8,9},{9,8},{10,11... | collective-permute-start | bytes 187400 | tf_op jit(solution)/shard_map/ppermute | solution.py:52
  19.3 6.2 %collective-permute-start.1 = (f32[122,4,32]{0,2,1:T(8,128)S(1)}, f32[122,4,32]{0,2,1:T(8,128)S(1)}, u32[]{:S(2)}, u32[]{:S(2)}) collective-permute-start(f32[122,4,32]{0,2,1:T(8,128)S(1)} %add.74), channel_id=1, source_target_pairs={{0,2},{1,3},{2,0},{3,1},{4,6},{5,7},{6,4},{7,5},{8,10},{9,11},{10,... | collective-permute-start | bytes 187400 | tf_op jit(solution)/shard_map/ppermute | solution.py:52
  25.5 7.7 %collective-permute-start.2 = (f32[122,4,32]{0,2,1:T(8,128)S(1)}, f32[122,4,32]{0,2,1:T(8,128)S(1)}, u32[]{:S(2)}, u32[]{:S(2)}) collective-permute-start(f32[122,4,32]{0,2,1:T(8,128)S(1)} %add.75), channel_id=1, source_target_pairs={{0,4},{1,5},{2,6},{3,7},{4,0},{5,1},{6,2},{7,3},{8,12},{9,13},{10,... | collective-permute-start | bytes 187400 | tf_op jit(solution)/shard_map/ppermute | solution.py:52
  33.2 7.7 %collective-permute-start.3 = (f32[122,4,32]{0,2,1:T(8,128)S(1)}, f32[122,4,32]{0,2,1:T(8,128)S(1)}, u32[]{:S(2)}, u32[]{:S(2)}) collective-permute-start(f32[122,4,32]{0,2,1:T(8,128)S(1)} %add.76), channel_id=1, source_target_pairs={{0,8},{1,9},{2,10},{3,11},{4,12},{5,13},{6,14},{7,15},{8,0},{9,1},... | collective-permute-start | bytes 187400 | tf_op jit(solution)/shard_map/ppermute | solution.py:52
  41.5 8.0 %all-to-all-start.1 = ((f32[4,122,4,8]{1,3,2,0:T(8,128)}), f32[4,122,4,8]{1,3,2,0:T(8,128)S(1)}, u32[]{:S(2)}, u32[]{:S(2)}) async-start(f32[4,122,4,8]{1,3,2,0:T(8,128)} %bitcast.29), calls=%async_computation.1 | async-start | bytes 131072 | tf_op jit(solution)/shard_map/all_to_all | solution.py:81

commit v17 on v16

--- a/solution.py
+++ b/solution.py
@@ -36,12 +36,12 @@
     src_imag = panel[NB:]
     own_real = white[:NB]
     own_imag = white[NB:]
-    real_sum = jnp.einsum("fts,ftc->sfc", src_real, own_real, precision=high) + jnp.einsum(
-        "fts,ftc->sfc", src_imag, own_imag, precision=high
-    )
-    imag_sum = jnp.einsum("fts,ftc->sfc", src_real, own_imag, precision=high) - jnp.einsum(
-        "fts,ftc->sfc", src_imag, own_real, precision=high
-    )
+    src_both = jnp.concatenate([src_real, src_imag], axis=1)
+    src_flip = jnp.concatenate([src_real, -src_imag], axis=1)
+    own_both = jnp.concatenate([own_real, own_imag], axis=1)
+    own_swap = jnp.concatenate([own_imag, own_real], axis=1)
+    real_sum = jnp.einsum("fts,ftc->sfc", src_both, own_both, precision=high)
+    imag_sum = jnp.einsum("fts,ftc->sfc", src_flip, own_swap, precision=high)
     return jnp.stack([real_sum, imag_sum], axis=1) * factor
 
 

time: 116 us -> 116 us (level)
  no operation moved by 1% of the time
where the time goes in v17:
time: 116 us; the launch traced here: 115 us
  blocking collectives  62.4 us (54%)
  starting transfers between devices  21 us (18%)
  waiting for transfers between devices  16.9 us (15%)
  local copies, waits for them, and re-layouts  7.45 us (6%)
  matrix products  5.53 us (5%)
  other arithmetic  1.91 us (2%)
    all_to_all x1, blocking collectives, on_device(): arrived = lax.all_to_all(totals, 'zhi', 0, 0, tiled=True)  62.4 us
    ppermute x4, waiting for transfers between devices, psum_recv(): value = value + lax.ppermute(value, 'recv', pairs)  16.9 us
    all_to_all x1, starting transfers between devices, on_device(): white_parts = lax.all_to_all(spread, group, 0, 0, tiled=True)  9.15 us
    ppermute x4, starting transfers between devices, psum_recv(): value = value + lax.ppermute(value, 'recv', pairs)  7.68 us
    all_to_all x1, starting transfers between devices, on_device(): panel = lax.all_to_all(panel, group, 0, 0, tiled=True)  4.19 us
    dot_general x1, matrix products, on_device(): lax.dot_general(basis, traces, (((1,), (2,)), ((), ())), preferred_elemen...  3.87 us
  transfers between devices with their start and end apart: 6, of which 4 were waited for; matrix products, arithmetic and copies ran while one was open for 4% of the time, Pallas kernels for 0%

profile of v17, /device:TPU:34, one launch (start us, length us, event | category | flops | bytes accessed | tf_op | source)
XLA Modules:
  0.0 115.4 jit_solution(9029593566343455206)
XLA Ops:
  0.0 0.7 convert_element_type.4
  0.7 3.9 %fusion.27 = f32[122,4,256]{2,0,1:T(8,128)S(1)} fusion(bf16[122,2048,1]{1,0,2:T(8,128)(2,1)} %constant.20, bf16[4,256,2048]{2,1,0:T(8,128)(2,1)} %param.4), kind=kOutput, calls=%fused_computation.41 | convolution fusion | flops 511705088 | bytes 5193728 | tf_op jit(solution)/shard_map/dot_general | solution.py:69
  4.6 0.1 fusion.24
  4.7 0.1 slice_multiply_fusion.1
  4.8 0.3 copy.35
  5.2 1.6 %broadcast_in_dim.2 = f32[4,122,4,256]{3,2,1,0:T(4,128)} broadcast(f32[122,4,256]{2,1,0:T(4,128)S(1)} %copy.35), dimensions={1,2,3} | broadcast | bytes 2498560 | tf_op jit(solution)/shard_map/broadcast_in_dim | solution.py:73
  6.7 0.0 copy-start
  6.7 9.2 %all-to-all-start = ((f32[4,122,4,256]{3,2,1,0:T(4,128)}), f32[4,122,4,256]{3,2,1,0:T(4,128)S(1)}, u32[]{:S(2)}, u32[]{:S(2)}) async-start(f32[4,122,4,256]{3,2,1,0:T(4,128)} %broadcast_in_dim.2), calls=%async_computation | async-start | bytes 3997696 | tf_op jit(solution)/shard_map/all_to_all | solution.py:74
  15.9 0.0 copy-done
  15.9 0.4 fusion.17
  16.3 1.9 %collective-permute-start = (f32[122,4,32]{0,2,1:T(8,128)S(1)}, f32[122,4,32]{0,2,1:T(8,128)S(1)}, u32[]{:S(2)}, u32[]{:S(2)}) collective-permute-start(f32[122,4,32]{0,2,1:T(8,128)S(1)} %fusion.17), channel_id=1, source_target_pairs={{0,1},{1,0},{2,3},{3,2},{4,5},{5,4},{6,7},{7,6},{8,9},{9,8},{10,11... | collective-permute-start | bytes 187400 | tf_op jit(solution)/shard_map/ppermute | solution.py:52
  18.2 1.2 %collective-permute-done = f32[122,4,32]{0,2,1:T(8,128)S(1)} collective-permute-done((f32[122,4,32]{0,2,1:T(8,128)S(1)}, f32[122,4,32]{0,2,1:T(8,128)S(1)}, u32[]{:S(2)}, u32[]{:S(2)}) %collective-permute-start) | collective-permute-done | bytes 62496 | tf_op jit(solution)/shard_map/ppermute | solution.py:52
  19.4 1.9 %collective-permute-start.1 = (f32[122,4,32]{0,2,1:T(8,128)S(1)}, f32[122,4,32]{0,2,1:T(8,128)S(1)}, u32[]{:S(2)}, u32[]{:S(2)}) collective-permute-start(f32[122,4,32]{0,2,1:T(8,128)S(1)} %add.68), channel_id=1, source_target_pairs={{0,2},{1,3},{2,0},{3,1},{4,6},{5,7},{6,4},{7,5},{8,10},{9,11},{10,... | collective-permute-start | bytes 187400 | tf_op jit(solution)/shard_map/ppermute | solution.py:52
  21.4 4.2 %collective-permute-done.1 = f32[122,4,32]{0,2,1:T(8,128)S(1)} collective-permute-done((f32[122,4,32]{0,2,1:T(8,128)S(1)}, f32[122,4,32]{0,2,1:T(8,128)S(1)}, u32[]{:S(2)}, u32[]{:S(2)}) %collective-permute-start.1) | collective-permute-done | bytes 62496 | tf_op jit(solution)/shard_map/ppermute | solution.py:52
  25.6 1.9 %collective-permute-start.2 = (f32[122,4,32]{0,2,1:T(8,128)S(1)}, f32[122,4,32]{0,2,1:T(8,128)S(1)}, u32[]{:S(2)}, u32[]{:S(2)}) collective-permute-start(f32[122,4,32]{0,2,1:T(8,128)S(1)} %add.69), channel_id=1, source_target_pairs={{0,4},{1,5},{2,6},{3,7},{4,0},{5,1},{6,2},{7,3},{8,12},{9,13},{10,... | collective-permute-start | bytes 187400 | tf_op jit(solution)/shard_map/ppermute | solution.py:52
  27.5 5.7 %collective-permute-done.2 = f32[122,4,32]{0,2,1:T(8,128)S(1)} collective-permute-done((f32[122,4,32]{0,2,1:T(8,128)S(1)}, f32[122,4,32]{0,2,1:T(8,128)S(1)}, u32[]{:S(2)}, u32[]{:S(2)}) %collective-permute-start.2) | collective-permute-done | bytes 62496 | tf_op jit(solution)/shard_map/ppermute | solution.py:52
  33.3 1.9 %collective-permute-start.3 = (f32[122,4,32]{0,2,1:T(8,128)S(1)}, f32[122,4,32]{0,2,1:T(8,128)S(1)}, u32[]{:S(2)}, u32[]{:S(2)}) collective-permute-start(f32[122,4,32]{0,2,1:T(8,128)S(1)} %add.70), channel_id=1, source_target_pairs={{0,8},{1,9},{2,10},{3,11},{4,12},{5,13},{6,14},{7,15},{8,0},{9,1},... | collective-permute-start | bytes 187400 | tf_op jit(solution)/shard_map/ppermute | solution.py:52
  35.2 5.7 %collective-permute-done.3 = f32[122,4,32]{0,2,1:T(8,128)S(1)} collective-permute-done((f32[122,4,32]{0,2,1:T(8,128)S(1)}, f32[122,4,32]{0,2,1:T(8,128)S(1)}, u32[]{:S(2)}, u32[]{:S(2)}) %collective-permute-start.3) | collective-permute-done | bytes 62496 | tf_op jit(solution)/shard_map/ppermute | solution.py:52
  41.0 0.0 all-to-all-done
  41.0 0.6 copy.44
  41.6 4.2 %all-to-all-start.1 = ((f32[4,122,4,8]{1,3,2,0:T(8,128)}), f32[4,122,4,8]{1,3,2,0:T(8,128)S(1)}, u32[]{:S(2)}, u32[]{:S(2)}) async-start(f32[4,122,4,8]{1,3,2,0:T(8,128)} %bitcast.23), calls=%async_computation.1 | async-start | bytes 131072 | tf_op jit(solution)/shard_map/all_to_all | solution.py:81
  45.8 1.3 %fusion.25 = (f32[61,4,4,256]{3,2,0,1:T(4,128)S(1)}, f32[61,4,4,256]{3,2,0,1:T(4,128)}) fusion(f32[122,4,4,256]{3,2,0,1:T(4,128)S(1)} %bitcast.24), kind=kLoop, calls=%fused_computation.39 | loop fusion | bytes 3997696 | tf_op jit(solution)/shard_map/slice | solution.py:38
  47.1 0.3 copy.37
  47.4 0.3 slice.59
  47.8 1.5 %copy.36 = f32[61,4,4,256]{3,2,1,0:T(4,128)S(1)} copy(f32[61,4,4,256]{3,2,0,1:T(4,128)} %get-tuple-element.10) | data formatting | bytes 1998848 | tf_op jit(solution)/shard_map/slice | solution.py:37
  49.3 0.3 slice.57
  49.6 0.0 all-to-all-done.1
  49.6 0.1 fusion.26
  49.7 0.2 copy.39
  49.9 0.2 copy.41
  50.1 0.2 copy.40
  50.3 0.6 fusion.8
  50.9 0.7 fusion.11
  51.6 0.1 maximum_multiply_fusion
  51.7 0.5 copy.42
  52.2 62.4 %all_to_all.15 = f32[8,2,61,256]{3,1,2,0:T(2,128)S(1)} all-to-all(f32[8,2,61,256]{3,1,2,0:T(2,128)S(1)} %copy.42), channel_id=1, replica_groups=mesh['zhi'=8,'zlo'=2,'xlo'=2,'recv'=16] {'zhi'}, dimensions={0} | all-to-all | bytes 1998848 | tf_op jit(solution)/shard_map/all_to_all | solution.py:85
  114.6 0.8 slice_add_fusion
  (9 shorter events, 0.1 us)
Async XLA Ops:
  6.7 9.2 %copy-start = (s32[32]{0:T(128)S(1)}, s32[32]{0:T(128)}, u32[]{:S(2)}) copy-start(s32[32]{0:T(128)} %param.6) | copy-start | bytes 388
  6.7 34.3 %all-to-all-start = ((f32[4,122,4,256]{3,2,1,0:T(4,128)}), f32[4,122,4,256]{3,2,1,0:T(4,128)S(1)}, u32[]{:S(2)}, u32[]{:S(2)}) async-start(f32[4,122,4,256]{3,2,1,0:T(4,128)} %broadcast_in_dim.2), calls=%async_computation | async-start | bytes 3997696 | tf_op jit(solution)/shard_map/all_to_all | solution.py:74
  16.3 3.1 %collective-permute-start = (f32[122,4,32]{0,2,1:T(8,128)S(1)}, f32[122,4,32]{0,2,1:T(8,128)S(1)}, u32[]{:S(2)}, u32[]{:S(2)}) collective-permute-start(f32[122,4,32]{0,2,1:T(8,128)S(1)} %fusion.17), channel_id=1, source_target_pairs={{0,1},{1,0},{2,3},{3,2},{4,5},{5,4},{6,7},{7,6},{8,9},{9,8},{10,11... | collective-permute-start | bytes 187400 | tf_op jit(solution)/shard_map/ppermute | solution.py:52
  19.4 6.2 %collective-permute-start.1 = (f32[122,4,32]{0,2,1:T(8,128)S(1)}, f32[122,4,32]{0,2,1:T(8,128)S(1)}, u32[]{:S(2)}, u32[]{:S(2)}) collective-permute-start(f32[122,4,32]{0,2,1:T(8,128)S(1)} %add.68), channel_id=1, source_target_pairs={{0,2},{1,3},{2,0},{3,1},{4,6},{5,7},{6,4},{7,5},{8,10},{9,11},{10,... | collective-permute-start | bytes 187400 | tf_op jit(solution)/shard_map/ppermute | solution.py:52
  25.6 7.7 %collective-permute-start.2 = (f32[122,4,32]{0,2,1:T(8,128)S(1)}, f32[122,4,32]{0,2,1:T(8,128)S(1)}, u32[]{:S(2)}, u32[]{:S(2)}) collective-permute-start(f32[122,4,32]{0,2,1:T(8,128)S(1)} %add.69), channel_id=1, source_target_pairs={{0,4},{1,5},{2,6},{3,7},{4,0},{5,1},{6,2},{7,3},{8,12},{9,13},{10,... | collective-permute-start | bytes 187400 | tf_op jit(solution)/shard_map/ppermute | solution.py:52
  33.3 7.7 %collective-permute-start.3 = (f32[122,4,32]{0,2,1:T(8,128)S(1)}, f32[122,4,32]{0,2,1:T(8,128)S(1)}, u32[]{:S(2)}, u32[]{:S(2)}) collective-permute-start(f32[122,4,32]{0,2,1:T(8,128)S(1)} %add.70), channel_id=1, source_target_pairs={{0,8},{1,9},{2,10},{3,11},{4,12},{5,13},{6,14},{7,15},{8,0},{9,1},... | collective-permute-start | bytes 187400 | tf_op jit(solution)/shard_map/ppermute | solution.py:52
  41.6 8.0 %all-to-all-start.1 = ((f32[4,122,4,8]{1,3,2,0:T(8,128)}), f32[4,122,4,8]{1,3,2,0:T(8,128)S(1)}, u32[]{:S(2)}, u32[]{:S(2)}) async-start(f32[4,122,4,8]{1,3,2,0:T(8,128)} %bitcast.23), calls=%async_computation.1 | async-start | bytes 131072 | tf_op jit(solution)/shard_map/all_to_all | solution.py:81

commit v18 on v17

--- a/solution.py
+++ b/solution.py
@@ -72,12 +72,12 @@
     white = whiten_block(spec, valid_float)
     spread = jnp.broadcast_to(white[None], (width,) + white.shape)
     white_parts = lax.all_to_all(spread, group, 0, 0, tiled=True)
-    partial_value = jnp.einsum("ktc,sc->kts", white, onehot, precision=lax.Precision.HIGHEST)
+    nsrc = onehot.shape[0]
+    onehot = onehot.reshape(nsrc // width, width, chan_count).transpose(1, 0, 2)
+    partial_value = jnp.einsum("ktc,rsc->rkts", white, onehot, precision=lax.Precision.HIGHEST)
     panel, white_parts = psum_recv(partial_value, lax.axis_size("recv"), white_parts)
     rows, segs, nchan = white.shape
     white_all = white_parts.transpose(1, 0, 2, 3).reshape(rows, width * segs, nchan)
-    nsrc = panel.shape[2]
-    panel = panel.reshape(rows, segs, nsrc // width, width).transpose(3, 0, 1, 2)
     panel = lax.all_to_all(panel, group, 0, 0, tiled=True)
     panel_own = panel.transpose(1, 0, 2, 3).reshape(rows, width * segs, nsrc // width)
     factor = 1.0 / math.sqrt(total_segs)

time: 116 us -> 116 us (level)
  no operation moved by 1% of the time
where the time goes in v18:
time: 116 us; the launch traced here: 115 us
  blocking collectives  62.1 us (54%)
  starting transfers between devices  21 us (18%)
  waiting for transfers between devices  16.9 us (15%)
  local copies, waits for them, and re-layouts  6.79 us (6%)
  matrix products  5.48 us (5%)
  other arithmetic  2.56 us (2%)
    all_to_all x1, blocking collectives, on_device(): arrived = lax.all_to_all(totals, 'zhi', 0, 0, tiled=True)  62.1 us
    ppermute x4, waiting for transfers between devices, psum_recv(): value = value + lax.ppermute(value, 'recv', pairs)  16.9 us
    all_to_all x1, starting transfers between devices, on_device(): white_parts = lax.all_to_all(spread, group, 0, 0, tiled=True)  9.15 us
    ppermute x4, starting transfers between devices, psum_recv(): value = value + lax.ppermute(value, 'recv', pairs)  7.68 us
    all_to_all x1, starting transfers between devices, on_device(): panel = lax.all_to_all(panel, group, 0, 0, tiled=True)  4.19 us
    dot_general x1, matrix products, on_device(): lax.dot_general(basis, traces, (((1,), (2,)), ((), ())), preferred_elemen...  3.87 us
  transfers between devices with their start and end apart: 6, of which 4 were waited for; matrix products, arithmetic and copies ran while one was open for 4% of the time, Pallas kernels for 0%

profile of v18, /device:TPU:34, one launch (start us, length us, event | category | flops | bytes accessed | tf_op | source)
XLA Modules:
  0.0 115.1 jit_solution(6501934960312544393)
XLA Ops:
  0.0 0.7 convert_element_type.4
  0.7 3.9 %fusion.24 = f32[122,4,256]{2,0,1:T(8,128)S(1)} fusion(bf16[122,2048,1]{1,0,2:T(8,128)(2,1)} %constant.20, bf16[4,256,2048]{2,1,0:T(8,128)(2,1)} %param.4), kind=kOutput, calls=%fused_computation.39 | convolution fusion | flops 511705088 | bytes 5193728 | tf_op jit(solution)/shard_map/dot_general | solution.py:69
  4.6 0.1 fusion.21
  4.7 0.1 slice_multiply_fusion.1
  4.8 0.3 copy.39
  5.2 1.6 %broadcast_in_dim.2 = f32[4,122,4,256]{3,2,1,0:T(4,128)} broadcast(f32[122,4,256]{2,1,0:T(4,128)S(1)} %copy.39), dimensions={1,2,3} | broadcast | bytes 2498560 | tf_op jit(solution)/shard_map/broadcast_in_dim | solution.py:73
  6.7 0.0 copy-start
  6.7 9.2 %all-to-all-start = ((f32[4,122,4,256]{3,2,1,0:T(4,128)}), f32[4,122,4,256]{3,2,1,0:T(4,128)S(1)}, u32[]{:S(2)}, u32[]{:S(2)}) async-start(f32[4,122,4,256]{3,2,1,0:T(4,128)} %broadcast_in_dim.2), calls=%async_computation | async-start | bytes 3997696 | tf_op jit(solution)/shard_map/all_to_all | solution.py:74
  15.9 0.0 copy-done
  15.9 0.1 eq.19
  15.9 0.1 copy.38
  16.0 0.4 convolution_bitcast_fusion
  16.4 1.9 %collective-permute-start = (f32[4,122,4,8]{1,3,2,0:T(8,128)S(1)}, f32[4,122,4,8]{1,3,2,0:T(8,128)S(1)}, u32[]{:S(2)}, u32[]{:S(2)}) collective-permute-start(f32[4,122,4,8]{1,3,2,0:T(8,128)S(1)} %convolution_bitcast_fusion), channel_id=1, source_target_pairs={{0,1},{1,0},{2,3},{3,2},{4,5},{5,4},{6,7},{7,6},{8,9},{9,8},{10,11... | collective-permute-start | bytes 187400 | tf_op jit(solution)/shard_map/ppermute | solution.py:52
  18.4 1.2 %collective-permute-done = f32[4,122,4,8]{1,3,2,0:T(8,128)S(1)} collective-permute-done((f32[4,122,4,8]{1,3,2,0:T(8,128)S(1)}, f32[4,122,4,8]{1,3,2,0:T(8,128)S(1)}, u32[]{:S(2)}, u32[]{:S(2)}) %collective-permute-start) | collective-permute-done | bytes 62496 | tf_op jit(solution)/shard_map/ppermute | solution.py:52
  19.6 1.9 %collective-permute-start.1 = (f32[4,122,4,8]{1,3,2,0:T(8,128)S(1)}, f32[4,122,4,8]{1,3,2,0:T(8,128)S(1)}, u32[]{:S(2)}, u32[]{:S(2)}) collective-permute-start(f32[4,122,4,8]{1,3,2,0:T(8,128)S(1)} %add.68), channel_id=1, source_target_pairs={{0,2},{1,3},{2,0},{3,1},{4,6},{5,7},{6,4},{7,5},{8,10},{9,11},{10,... | collective-permute-start | bytes 187400 | tf_op jit(solution)/shard_map/ppermute | solution.py:52
  21.5 4.2 %collective-permute-done.1 = f32[4,122,4,8]{1,3,2,0:T(8,128)S(1)} collective-permute-done((f32[4,122,4,8]{1,3,2,0:T(8,128)S(1)}, f32[4,122,4,8]{1,3,2,0:T(8,128)S(1)}, u32[]{:S(2)}, u32[]{:S(2)}) %collective-permute-start.1) | collective-permute-done | bytes 62496 | tf_op jit(solution)/shard_map/ppermute | solution.py:52
  25.8 1.9 %collective-permute-start.2 = (f32[4,122,4,8]{1,3,2,0:T(8,128)S(1)}, f32[4,122,4,8]{1,3,2,0:T(8,128)S(1)}, u32[]{:S(2)}, u32[]{:S(2)}) collective-permute-start(f32[4,122,4,8]{1,3,2,0:T(8,128)S(1)} %add.69), channel_id=1, source_target_pairs={{0,4},{1,5},{2,6},{3,7},{4,0},{5,1},{6,2},{7,3},{8,12},{9,13},{10,... | collective-permute-start | bytes 187400 | tf_op jit(solution)/shard_map/ppermute | solution.py:52
  27.7 5.7 %collective-permute-done.2 = f32[4,122,4,8]{1,3,2,0:T(8,128)S(1)} collective-permute-done((f32[4,122,4,8]{1,3,2,0:T(8,128)S(1)}, f32[4,122,4,8]{1,3,2,0:T(8,128)S(1)}, u32[]{:S(2)}, u32[]{:S(2)}) %collective-permute-start.2) | collective-permute-done | bytes 62496 | tf_op jit(solution)/shard_map/ppermute | solution.py:52
  33.5 1.9 %collective-permute-start.3 = (f32[4,122,4,8]{1,3,2,0:T(8,128)S(1)}, f32[4,122,4,8]{1,3,2,0:T(8,128)S(1)}, u32[]{:S(2)}, u32[]{:S(2)}) collective-permute-start(f32[4,122,4,8]{1,3,2,0:T(8,128)S(1)} %add.70), channel_id=1, source_target_pairs={{0,8},{1,9},{2,10},{3,11},{4,12},{5,13},{6,14},{7,15},{8,0},{9,1},... | collective-permute-start | bytes 187400 | tf_op jit(solution)/shard_map/ppermute | solution.py:52
  35.4 5.7 %collective-permute-done.3 = f32[4,122,4,8]{1,3,2,0:T(8,128)S(1)} collective-permute-done((f32[4,122,4,8]{1,3,2,0:T(8,128)S(1)}, f32[4,122,4,8]{1,3,2,0:T(8,128)S(1)}, u32[]{:S(2)}, u32[]{:S(2)}) %collective-permute-start.3) | collective-permute-done | bytes 62496 | tf_op jit(solution)/shard_map/ppermute | solution.py:52
  41.1 0.6 add.71
  41.8 0.0 all-to-all-done
  41.8 4.2 %all-to-all-start.1 = ((f32[4,122,4,8]{1,3,2,0:T(8,128)}), f32[4,122,4,8]{1,3,2,0:T(8,128)S(1)}, u32[]{:S(2)}, u32[]{:S(2)}) async-start(f32[4,122,4,8]{1,3,2,0:T(8,128)} %add.71), calls=%async_computation.1 | async-start | bytes 131072 | tf_op jit(solution)/shard_map/all_to_all | solution.py:81
  46.0 1.3 %fusion.22 = (f32[61,4,4,256]{3,2,0,1:T(4,128)S(1)}, f32[61,4,4,256]{3,2,0,1:T(4,128)}) fusion(f32[122,4,4,256]{3,2,0,1:T(4,128)S(1)} %bitcast.29), kind=kLoop, calls=%fused_computation.37 | loop fusion | bytes 3997696 | tf_op jit(solution)/shard_map/slice | solution.py:38
  47.2 0.3 copy.41
  47.6 0.3 slice.59
  47.9 1.5 %copy.40 = f32[61,4,4,256]{3,2,1,0:T(4,128)S(1)} copy(f32[61,4,4,256]{3,2,0,1:T(4,128)} %get-tuple-element.10) | data formatting | bytes 1998848 | tf_op jit(solution)/shard_map/slice | solution.py:37
  49.4 0.3 slice.57
  49.8 0.0 all-to-all-done.1
  49.8 0.1 fusion.23
  49.9 0.2 copy.42
  50.1 0.2 copy.43
  50.3 0.6 fusion.8
  50.9 0.6 fusion.11
  51.5 0.1 maximum_multiply_fusion
  51.6 0.5 copy.44
  52.1 62.1 %all_to_all.15 = f32[8,2,61,256]{3,1,2,0:T(2,128)S(1)} all-to-all(f32[8,2,61,256]{3,1,2,0:T(2,128)S(1)} %copy.44), channel_id=1, replica_groups=mesh['zhi'=8,'zlo'=2,'xlo'=2,'recv'=16] {'zhi'}, dimensions={0} | all-to-all | bytes 1998848 | tf_op jit(solution)/shard_map/all_to_all | solution.py:85
  114.2 0.8 slice_add_fusion
  (8 shorter events, 0.1 us)
Async XLA Ops:
  6.7 9.2 %copy-start = (s32[32]{0:T(128)S(1)}, s32[32]{0:T(128)}, u32[]{:S(2)}) copy-start(s32[32]{0:T(128)} %param.6) | copy-start | bytes 388
  6.7 35.1 %all-to-all-start = ((f32[4,122,4,256]{3,2,1,0:T(4,128)}), f32[4,122,4,256]{3,2,1,0:T(4,128)S(1)}, u32[]{:S(2)}, u32[]{:S(2)}) async-start(f32[4,122,4,256]{3,2,1,0:T(4,128)} %broadcast_in_dim.2), calls=%async_computation | async-start | bytes 3997696 | tf_op jit(solution)/shard_map/all_to_all | solution.py:74
  16.4 3.1 %collective-permute-start = (f32[4,122,4,8]{1,3,2,0:T(8,128)S(1)}, f32[4,122,4,8]{1,3,2,0:T(8,128)S(1)}, u32[]{:S(2)}, u32[]{:S(2)}) collective-permute-start(f32[4,122,4,8]{1,3,2,0:T(8,128)S(1)} %convolution_bitcast_fusion), channel_id=1, source_target_pairs={{0,1},{1,0},{2,3},{3,2},{4,5},{5,4},{6,7},{7,6},{8,9},{9,8},{10,11... | collective-permute-start | bytes 187400 | tf_op jit(solution)/shard_map/ppermute | solution.py:52
  19.6 6.2 %collective-permute-start.1 = (f32[4,122,4,8]{1,3,2,0:T(8,128)S(1)}, f32[4,122,4,8]{1,3,2,0:T(8,128)S(1)}, u32[]{:S(2)}, u32[]{:S(2)}) collective-permute-start(f32[4,122,4,8]{1,3,2,0:T(8,128)S(1)} %add.68), channel_id=1, source_target_pairs={{0,2},{1,3},{2,0},{3,1},{4,6},{5,7},{6,4},{7,5},{8,10},{9,11},{10,... | collective-permute-start | bytes 187400 | tf_op jit(solution)/shard_map/ppermute | solution.py:52
  25.8 7.7 %collective-permute-start.2 = (f32[4,122,4,8]{1,3,2,0:T(8,128)S(1)}, f32[4,122,4,8]{1,3,2,0:T(8,128)S(1)}, u32[]{:S(2)}, u32[]{:S(2)}) collective-permute-start(f32[4,122,4,8]{1,3,2,0:T(8,128)S(1)} %add.69), channel_id=1, source_target_pairs={{0,4},{1,5},{2,6},{3,7},{4,0},{5,1},{6,2},{7,3},{8,12},{9,13},{10,... | collective-permute-start | bytes 187400 | tf_op jit(solution)/shard_map/ppermute | solution.py:52
  33.5 7.7 %collective-permute-start.3 = (f32[4,122,4,8]{1,3,2,0:T(8,128)S(1)}, f32[4,122,4,8]{1,3,2,0:T(8,128)S(1)}, u32[]{:S(2)}, u32[]{:S(2)}) collective-permute-start(f32[4,122,4,8]{1,3,2,0:T(8,128)S(1)} %add.70), channel_id=1, source_target_pairs={{0,8},{1,9},{2,10},{3,11},{4,12},{5,13},{6,14},{7,15},{8,0},{9,1},... | collective-permute-start | bytes 187400 | tf_op jit(solution)/shard_map/ppermute | solution.py:52
  41.8 8.0 %all-to-all-start.1 = ((f32[4,122,4,8]{1,3,2,0:T(8,128)}), f32[4,122,4,8]{1,3,2,0:T(8,128)S(1)}, u32[]{:S(2)}, u32[]{:S(2)}) async-start(f32[4,122,4,8]{1,3,2,0:T(8,128)} %add.71), calls=%async_computation.1 | async-start | bytes 131072 | tf_op jit(solution)/shard_map/all_to_all | solution.py:81

commit v19 on v18

--- a/solution.py
+++ b/solution.py
@@ -74,7 +74,7 @@
     white_parts = lax.all_to_all(spread, group, 0, 0, tiled=True)
     nsrc = onehot.shape[0]
     onehot = onehot.reshape(nsrc // width, width, chan_count).transpose(1, 0, 2)
-    partial_value = jnp.einsum("ktc,rsc->rkts", white, onehot, precision=lax.Precision.HIGHEST)
+    partial_value = jnp.einsum("ktc,rsc->rkts", white, onehot, precision=lax.Precision.HIGH)
     panel, white_parts = psum_recv(partial_value, lax.axis_size("recv"), white_parts)
     rows, segs, nchan = white.shape
     white_all = white_parts.transpose(1, 0, 2, 3).reshape(rows, width * segs, nchan)

time: 116 us -> 116 us (level)
  no operation moved by 1% of the time
where the time goes in v19:
time: 116 us; the launch traced here: 115 us
  blocking collectives  62.3 us (54%)
  starting transfers between devices  21 us (18%)
  waiting for transfers between devices  16.9 us (15%)
  local copies, waits for them, and re-layouts  6.79 us (6%)
  matrix products  5.35 us (5%)
  other arithmetic  2.56 us (2%)
    all_to_all x1, blocking collectives, on_device(): arrived = lax.all_to_all(totals, 'zhi', 0, 0, tiled=True)  62.3 us
    ppermute x4, waiting for transfers between devices, psum_recv(): value = value + lax.ppermute(value, 'recv', pairs)  16.9 us
    all_to_all x1, starting transfers between devices, on_device(): white_parts = lax.all_to_all(spread, group, 0, 0, tiled=True)  9.15 us
    ppermute x4, starting transfers between devices, psum_recv(): value = value + lax.ppermute(value, 'recv', pairs)  7.68 us
    all_to_all x1, starting transfers between devices, on_device(): panel = lax.all_to_all(panel, group, 0, 0, tiled=True)  4.19 us
    dot_general x1, matrix products, on_device(): lax.dot_general(basis, traces, (((1,), (2,)), ((), ())), preferred_elemen...  3.87 us
  transfers between devices with their start and end apart: 6, of which 4 were waited for; matrix products, arithmetic and copies ran while one was open for 4% of the time, Pallas kernels for 0%

profile of v19, /device:TPU:34, one launch (start us, length us, event | category | flops | bytes accessed | tf_op | source)
XLA Modules:
  0.0 115.2 jit_solution(3763745376601668867)
XLA Ops:
  0.0 0.7 convert_element_type.4
  0.7 3.9 %fusion.24 = f32[122,4,256]{2,0,1:T(8,128)S(1)} fusion(bf16[122,2048,1]{1,0,2:T(8,128)(2,1)} %constant.20, bf16[4,256,2048]{2,1,0:T(8,128)(2,1)} %param.4), kind=kOutput, calls=%fused_computation.39 | convolution fusion | flops 511705088 | bytes 5193728 | tf_op jit(solution)/shard_map/dot_general | solution.py:69
  4.6 0.1 fusion.21
  4.7 0.1 slice_multiply_fusion.1
  4.8 0.3 copy.39
  5.2 1.6 %broadcast_in_dim.2 = f32[4,122,4,256]{3,2,1,0:T(4,128)} broadcast(f32[122,4,256]{2,1,0:T(4,128)S(1)} %copy.39), dimensions={1,2,3} | broadcast | bytes 2498560 | tf_op jit(solution)/shard_map/broadcast_in_dim | solution.py:73
  6.7 0.0 copy-start
  6.7 9.2 %all-to-all-start = ((f32[4,122,4,256]{3,2,1,0:T(4,128)}), f32[4,122,4,256]{3,2,1,0:T(4,128)S(1)}, u32[]{:S(2)}, u32[]{:S(2)}) async-start(f32[4,122,4,256]{3,2,1,0:T(4,128)} %broadcast_in_dim.2), calls=%async_computation | async-start | bytes 3997696 | tf_op jit(solution)/shard_map/all_to_all | solution.py:74
  15.9 0.0 copy-done
  15.9 0.1 eq.19
  15.9 0.1 copy.38
  16.0 0.3 convolution_bitcast_fusion
  16.3 1.9 %collective-permute-start = (f32[4,122,4,8]{1,3,2,0:T(8,128)S(1)}, f32[4,122,4,8]{1,3,2,0:T(8,128)S(1)}, u32[]{:S(2)}, u32[]{:S(2)}) collective-permute-start(f32[4,122,4,8]{1,3,2,0:T(8,128)S(1)} %convolution_bitcast_fusion), channel_id=1, source_target_pairs={{0,1},{1,0},{2,3},{3,2},{4,5},{5,4},{6,7},{7,6},{8,9},{9,8},{10,11... | collective-permute-start | bytes 187400 | tf_op jit(solution)/shard_map/ppermute | solution.py:52
  18.2 1.2 %collective-permute-done = f32[4,122,4,8]{1,3,2,0:T(8,128)S(1)} collective-permute-done((f32[4,122,4,8]{1,3,2,0:T(8,128)S(1)}, f32[4,122,4,8]{1,3,2,0:T(8,128)S(1)}, u32[]{:S(2)}, u32[]{:S(2)}) %collective-permute-start) | collective-permute-done | bytes 62496 | tf_op jit(solution)/shard_map/ppermute | solution.py:52
  19.5 1.9 %collective-permute-start.1 = (f32[4,122,4,8]{1,3,2,0:T(8,128)S(1)}, f32[4,122,4,8]{1,3,2,0:T(8,128)S(1)}, u32[]{:S(2)}, u32[]{:S(2)}) collective-permute-start(f32[4,122,4,8]{1,3,2,0:T(8,128)S(1)} %add.68), channel_id=1, source_target_pairs={{0,2},{1,3},{2,0},{3,1},{4,6},{5,7},{6,4},{7,5},{8,10},{9,11},{10,... | collective-permute-start | bytes 187400 | tf_op jit(solution)/shard_map/ppermute | solution.py:52
  21.4 4.2 %collective-permute-done.1 = f32[4,122,4,8]{1,3,2,0:T(8,128)S(1)} collective-permute-done((f32[4,122,4,8]{1,3,2,0:T(8,128)S(1)}, f32[4,122,4,8]{1,3,2,0:T(8,128)S(1)}, u32[]{:S(2)}, u32[]{:S(2)}) %collective-permute-start.1) | collective-permute-done | bytes 62496 | tf_op jit(solution)/shard_map/ppermute | solution.py:52
  25.6 1.9 %collective-permute-start.2 = (f32[4,122,4,8]{1,3,2,0:T(8,128)S(1)}, f32[4,122,4,8]{1,3,2,0:T(8,128)S(1)}, u32[]{:S(2)}, u32[]{:S(2)}) collective-permute-start(f32[4,122,4,8]{1,3,2,0:T(8,128)S(1)} %add.69), channel_id=1, source_target_pairs={{0,4},{1,5},{2,6},{3,7},{4,0},{5,1},{6,2},{7,3},{8,12},{9,13},{10,... | collective-permute-start | bytes 187400 | tf_op jit(solution)/shard_map/ppermute | solution.py:52
  27.6 5.7 %collective-permute-done.2 = f32[4,122,4,8]{1,3,2,0:T(8,128)S(1)} collective-permute-done((f32[4,122,4,8]{1,3,2,0:T(8,128)S(1)}, f32[4,122,4,8]{1,3,2,0:T(8,128)S(1)}, u32[]{:S(2)}, u32[]{:S(2)}) %collective-permute-start.2) | collective-permute-done | bytes 62496 | tf_op jit(solution)/shard_map/ppermute | solution.py:52
  33.3 1.9 %collective-permute-start.3 = (f32[4,122,4,8]{1,3,2,0:T(8,128)S(1)}, f32[4,122,4,8]{1,3,2,0:T(8,128)S(1)}, u32[]{:S(2)}, u32[]{:S(2)}) collective-permute-start(f32[4,122,4,8]{1,3,2,0:T(8,128)S(1)} %add.70), channel_id=1, source_target_pairs={{0,8},{1,9},{2,10},{3,11},{4,12},{5,13},{6,14},{7,15},{8,0},{9,1},... | collective-permute-start | bytes 187400 | tf_op jit(solution)/shard_map/ppermute | solution.py:52
  35.3 5.7 %collective-permute-done.3 = f32[4,122,4,8]{1,3,2,0:T(8,128)S(1)} collective-permute-done((f32[4,122,4,8]{1,3,2,0:T(8,128)S(1)}, f32[4,122,4,8]{1,3,2,0:T(8,128)S(1)}, u32[]{:S(2)}, u32[]{:S(2)}) %collective-permute-start.3) | collective-permute-done | bytes 62496 | tf_op jit(solution)/shard_map/ppermute | solution.py:52
  41.0 0.6 add.71
  41.6 0.0 all-to-all-done
  41.6 4.2 %all-to-all-start.1 = ((f32[4,122,4,8]{1,3,2,0:T(8,128)}), f32[4,122,4,8]{1,3,2,0:T(8,128)S(1)}, u32[]{:S(2)}, u32[]{:S(2)}) async-start(f32[4,122,4,8]{1,3,2,0:T(8,128)} %add.71), calls=%async_computation.1 | async-start | bytes 131072 | tf_op jit(solution)/shard_map/all_to_all | solution.py:81
  45.8 1.3 %fusion.22 = (f32[61,4,4,256]{3,2,0,1:T(4,128)S(1)}, f32[61,4,4,256]{3,2,0,1:T(4,128)}) fusion(f32[122,4,4,256]{3,2,0,1:T(4,128)S(1)} %bitcast.29), kind=kLoop, calls=%fused_computation.37 | loop fusion | bytes 3997696 | tf_op jit(solution)/shard_map/slice | solution.py:38
  47.1 0.3 copy.41
  47.4 0.3 slice.59
  47.8 1.5 %copy.40 = f32[61,4,4,256]{3,2,1,0:T(4,128)S(1)} copy(f32[61,4,4,256]{3,2,0,1:T(4,128)} %get-tuple-element.10) | data formatting | bytes 1998848 | tf_op jit(solution)/shard_map/slice | solution.py:37
  49.3 0.3 slice.57
  49.6 0.0 all-to-all-done.1
  49.7 0.1 fusion.23
  49.8 0.2 copy.42
  50.0 0.2 copy.43
  50.2 0.6 fusion.8
  50.8 0.6 fusion.11
  51.4 0.1 maximum_multiply_fusion
  51.5 0.5 copy.44
  52.0 62.3 %all_to_all.15 = f32[8,2,61,256]{3,1,2,0:T(2,128)S(1)} all-to-all(f32[8,2,61,256]{3,1,2,0:T(2,128)S(1)} %copy.44), channel_id=1, replica_groups=mesh['zhi'=8,'zlo'=2,'xlo'=2,'recv'=16] {'zhi'}, dimensions={0} | all-to-all | bytes 1998848 | tf_op jit(solution)/shard_map/all_to_all | solution.py:85
  114.3 0.8 slice_add_fusion
  (8 shorter events, 0.1 us)
Async XLA Ops:
  6.7 9.2 %copy-start = (s32[32]{0:T(128)S(1)}, s32[32]{0:T(128)}, u32[]{:S(2)}) copy-start(s32[32]{0:T(128)} %param.6) | copy-start | bytes 388
  6.7 34.9 %all-to-all-start = ((f32[4,122,4,256]{3,2,1,0:T(4,128)}), f32[4,122,4,256]{3,2,1,0:T(4,128)S(1)}, u32[]{:S(2)}, u32[]{:S(2)}) async-start(f32[4,122,4,256]{3,2,1,0:T(4,128)} %broadcast_in_dim.2), calls=%async_computation | async-start | bytes 3997696 | tf_op jit(solution)/shard_map/all_to_all | solution.py:74
  16.3 3.1 %collective-permute-start = (f32[4,122,4,8]{1,3,2,0:T(8,128)S(1)}, f32[4,122,4,8]{1,3,2,0:T(8,128)S(1)}, u32[]{:S(2)}, u32[]{:S(2)}) collective-permute-start(f32[4,122,4,8]{1,3,2,0:T(8,128)S(1)} %convolution_bitcast_fusion), channel_id=1, source_target_pairs={{0,1},{1,0},{2,3},{3,2},{4,5},{5,4},{6,7},{7,6},{8,9},{9,8},{10,11... | collective-permute-start | bytes 187400 | tf_op jit(solution)/shard_map/ppermute | solution.py:52
  19.5 6.2 %collective-permute-start.1 = (f32[4,122,4,8]{1,3,2,0:T(8,128)S(1)}, f32[4,122,4,8]{1,3,2,0:T(8,128)S(1)}, u32[]{:S(2)}, u32[]{:S(2)}) collective-permute-start(f32[4,122,4,8]{1,3,2,0:T(8,128)S(1)} %add.68), channel_id=1, source_target_pairs={{0,2},{1,3},{2,0},{3,1},{4,6},{5,7},{6,4},{7,5},{8,10},{9,11},{10,... | collective-permute-start | bytes 187400 | tf_op jit(solution)/shard_map/ppermute | solution.py:52
  25.6 7.7 %collective-permute-start.2 = (f32[4,122,4,8]{1,3,2,0:T(8,128)S(1)}, f32[4,122,4,8]{1,3,2,0:T(8,128)S(1)}, u32[]{:S(2)}, u32[]{:S(2)}) collective-permute-start(f32[4,122,4,8]{1,3,2,0:T(8,128)S(1)} %add.69), channel_id=1, source_target_pairs={{0,4},{1,5},{2,6},{3,7},{4,0},{5,1},{6,2},{7,3},{8,12},{9,13},{10,... | collective-permute-start | bytes 187400 | tf_op jit(solution)/shard_map/ppermute | solution.py:52
  33.3 7.7 %collective-permute-start.3 = (f32[4,122,4,8]{1,3,2,0:T(8,128)S(1)}, f32[4,122,4,8]{1,3,2,0:T(8,128)S(1)}, u32[]{:S(2)}, u32[]{:S(2)}) collective-permute-start(f32[4,122,4,8]{1,3,2,0:T(8,128)S(1)} %add.70), channel_id=1, source_target_pairs={{0,8},{1,9},{2,10},{3,11},{4,12},{5,13},{6,14},{7,15},{8,0},{9,1},... | collective-permute-start | bytes 187400 | tf_op jit(solution)/shard_map/ppermute | solution.py:52
  41.6 8.0 %all-to-all-start.1 = ((f32[4,122,4,8]{1,3,2,0:T(8,128)}), f32[4,122,4,8]{1,3,2,0:T(8,128)S(1)}, u32[]{:S(2)}, u32[]{:S(2)}) async-start(f32[4,122,4,8]{1,3,2,0:T(8,128)} %add.71), calls=%async_computation.1 | async-start | bytes 131072 | tf_op jit(solution)/shard_map/all_to_all | solution.py:81
